TPU v7x, 32 devices: a whole 2x2x4 slice. The times are simulated.
32 devices in a mesh: groups: 2 (over y), seq: 4 (over z), variant: 2 (over x), mp: 2 (over core).
Axes of the slice: x: 2, y: 2, z: 4, core: 2. Of those that a mesh axis runs over, the one named last changes fastest.
Arguments:
- queries: bfloat16 [4096, 2048], P(('groups', 'seq'), 'mp'), parts along dimension 0, may hold values from -84 to 84
- keys: bfloat16 [4096, 1024], P(('groups', 'seq'), 'mp'), parts along dimension 0, may hold values from -6 to 6
- values: bfloat16 [4096, 1024], P(('groups', 'seq'), 'mp'), parts along dimension 0, may hold values from -6 to 6
- clean_keys: bfloat16 [4096, 1024], P(('groups', 'seq', 'variant'), 'mp'), parts along dimension 0, may hold values from -6 to 6
- clean_values: bfloat16 [4096, 1024], P(('groups', 'seq', 'variant'), 'mp'), parts along dimension 0, may hold values from -6 to 6
- owner_shard: int32 [4], P(('groups', 'variant')), parts along dimension 0, may hold values from 0 to 3
- span_offset: int32 [4, 2], P(('groups', 'variant')), parts along dimension 0, may hold values from 0 to 384, as said below
- span_length: int32 [4, 2], P(('groups', 'variant')), parts along dimension 0, may hold values from 128 to 256, as said below
Outputs:
- attended: bfloat16 [2, 4096, 2048], P('variant', ('groups', 'seq'), 'mp'), parts along dimension 1
There are 2 independent parts, one for each index of `groups`. A program takes and returns all parts, laid end to end along the dimension named above; each array names one. Nothing has to cross between parts.
Inputs may be any that keep to these rules, and one draw needn't show every extreme that they name: `span_offset`: multiples of 128; span_offset + span_length <= 512 for every span. `span_length`: multiples of 128.
All inputs are finite; a program needn't handle non-finite values.
Results may differ from a plain program's by a relative error of at most 0.011.
Values may be sent and summed in bfloat16 or wider, within the bound.
No kernel may reach another device: no remote copies, remote signals or barrier semaphores. Data moves between devices by JAX's collectives and lax.ppermute only.
A program may use at most 64 MiB of HBM per device.

v0:
```python
import jax
import jax.numpy as jnp
from jax import lax
from jax.sharding import PartitionSpec as P

HEAD_DIM = 128
WINDOW = 1024
SPAN_MAX = 256


query_scale = 168.0 ** (-0.5)
masked_score = -1e30


def shifted(shard, axis, by):
    devices = lax.axis_size(axis)
    pairs = [(i, i + by) for i in range(devices) if 0 <= i + by < devices]
    return lax.ppermute(shard, axis, pairs)


def attend(query_rows, key_window, value_window, first_row):
    row_count = query_rows.shape[0]
    local_heads = key_window.shape[1] // HEAD_DIM
    query_pos = first_row + lax.broadcasted_iota(jnp.int32, (row_count,), 0)
    key_pos = first_row - 2 * row_count + lax.broadcasted_iota(jnp.int32, (3 * row_count,), 0)
    allowed = (
        (key_pos[None, :] <= query_pos[:, None])
        & (query_pos[:, None] - key_pos[None, :] < WINDOW)
        & (key_pos[None, :] >= 0)
    )
    outputs = []
    for head_index in range(local_heads):
        grouped = query_rows[
            :, head_index * 2 * HEAD_DIM : (head_index + 1) * 2 * HEAD_DIM
        ].reshape(row_count, 2, HEAD_DIM)
        key_head = key_window[:, head_index * HEAD_DIM : (head_index + 1) * HEAD_DIM]
        value_head = value_window[:, head_index * HEAD_DIM : (head_index + 1) * HEAD_DIM]
        scores = (
            jnp.einsum("qgd,kd->gqk", grouped, key_head, preferred_element_type=jnp.float32)
            * query_scale
        )
        scores = jnp.where(allowed, scores, masked_score)
        row_max = jnp.max(scores, axis=-1, keepdims=True)
        exponent = jnp.exp(scores - row_max)
        weights = (exponent / jnp.sum(exponent, axis=-1, keepdims=True)).astype(jnp.bfloat16)
        attended = jnp.einsum(
            "gqk,kd->qgd", weights, value_head, preferred_element_type=jnp.float32
        )
        outputs.append(attended.reshape(row_count, 2 * HEAD_DIM).astype(jnp.bfloat16))
    return jnp.concatenate(outputs, axis=1)


def splice_slot(base_rows, span_buffer, offsets, lengths, active):
    row_count = base_rows.shape[1]
    col_count = base_rows.shape[2]
    span_count = span_buffer.shape[1]
    span_rows = span_buffer.shape[2]
    position = lax.broadcasted_iota(jnp.int32, (row_count,), 0)
    for span_index in range(span_count):
        blank = jnp.zeros((2, row_count + span_rows, col_count), jnp.bfloat16)
        placed = lax.dynamic_update_slice_in_dim(
            blank, span_buffer[:, span_index], offsets[span_index], 1
        )[:, :row_count]
        span_mask = (
            active
            & (position >= offsets[span_index])
            & (position < offsets[span_index] + lengths[span_index])
        )
        base_rows = jnp.where(span_mask[None, :, None], placed, base_rows)
    return base_rows


def shards(queries, keys, values, clean_keys, clean_values, owner_shard, span_offset, span_length):
    row_count = keys.shape[0]
    col_count = keys.shape[1]
    shard_index = lax.axis_index("seq")
    first_row = shard_index * row_count
    gathered_keys, gathered_values = (
        lax.all_gather(clean_keys, "variant", axis=0, tiled=True),
        lax.all_gather(clean_values, "variant", axis=0, tiled=True),
    )
    clean_pair = jnp.stack([gathered_keys, gathered_values])
    clean_padded = jnp.concatenate(
        [clean_pair, jnp.zeros((2, SPAN_MAX, col_count), jnp.bfloat16)], axis=1
    )

    def cut_span(offset):
        return lax.dynamic_slice_in_dim(clean_padded, offset, SPAN_MAX, 1)

    own_spans = jax.vmap(jax.vmap(cut_span, out_axes=1), out_axes=1)(span_offset)
    span_flat = own_spans.reshape(2, -1, col_count)
    corrupt_pair = jnp.stack([keys, values])
    payload = jnp.concatenate([corrupt_pair, span_flat], axis=1)
    near_payload = shifted(payload, "seq", 1)
    far_payload = shifted(payload, "seq", 2)
    near_corrupt = near_payload[:, :row_count]
    far_corrupt = far_payload[:, :row_count]
    near_span = near_payload[:, row_count:]
    far_span = far_payload[:, row_count:]
    window_pair = jnp.concatenate([far_corrupt, near_corrupt, corrupt_pair], axis=1)
    near_spans_all = near_span.reshape(own_spans.shape)
    far_spans_all = far_span.reshape(own_spans.shape)
    owner_index = owner_shard[0]
    offsets = span_offset[0]
    lengths = span_length[0]
    slot_spans = [far_spans_all[:, 0], near_spans_all[:, 0], own_spans[:, 0]]
    slots = [
        splice_slot(
            window_pair[:, slot_index * row_count : (slot_index + 1) * row_count],
            slot_spans[slot_index],
            offsets,
            lengths,
            owner_index == shard_index - 2 + slot_index,
        )
        for slot_index in range(3)
    ]
    patched_pair = jnp.concatenate(slots, axis=1)
    result = attend(queries, patched_pair[0], patched_pair[1], first_row)
    results = [result]
    return jnp.stack(results)


def solution(mesh):
    placed = (
        P(("groups", "seq"), "mp"),
        P(("groups", "seq"), "mp"),
        P(("groups", "seq"), "mp"),
        P(("groups", "seq", "variant"), "mp"),
        P(("groups", "seq", "variant"), "mp"),
        P(("groups", "variant")),
        P(("groups", "variant"), None),
        P(("groups", "variant"), None),
    )
    return jax.shard_map(
        shards,
        mesh=mesh,
        in_specs=placed,
        out_specs=P("variant", ("groups", "seq"), "mp"),
        check_vma=False,
    )
```

profile of v0, /device:TPU:21, one launch (start us, length us, event | category | flops | bytes accessed | tf_op | source)
XLA Modules:
  0.0 233.5 jit_solution(7629535623309317657)
XLA Ops:
  0.0 8.0 %all_gather.6 = bf16[512,512]{1,0:T(8,128)(2,1)S(1)} all-gather(bf16[256,512]{1,0:T(8,128)(2,1)} %param.11), channel_id=1, replica_groups=mesh['groups'=2,'seq'=4,'variant'=2,'mp'=2] {'variant'}, dimensions={0}, use_global_device_ids=true | all-gather | bytes 786432 | tf_op jit(solution)/shard_map/all_gather | solution.py:79
  8.1 9.0 %all_gather.7 = bf16[512,512]{1,0:T(8,128)(2,1)} all-gather(bf16[256,512]{1,0:T(8,128)(2,1)} %param.12), channel_id=1, replica_groups=mesh['groups'=2,'seq'=4,'variant'=2,'mp'=2] {'variant'}, dimensions={0}, use_global_device_ids=true | all-gather | bytes 786432 | tf_op jit(solution)/shard_map/all_gather | solution.py:80
  19.0 3.0 %while.1 = (s32[]{:T(128)}, bf16[2,768,512]{2,1,0:T(8,128)(2,1)S(1)}, s32[2,3]{1,0:T(2,128)S(1)}, bf16[2,2,256,512]{3,2,1,0:T(8,128)(2,1)S(1)}, s32[]{:T(128)}) while((s32[]{:T(128)}, bf16[2,768,512]{2,1,0:T(8,128)(2,1)S(1)}, s32[2,3]{1,0:T(2,128)S(1)}, bf16[2,2,256,512]{3,2,1,0:T(8,128)(2,1)S(1)}, s32[]{:T(128)}) %tuple.31), condition=%wide.while_cond, body=%wide.while_body.sunk | while | flops 2 | bytes 1048681 | solution.py:88
  22.1 2.6 %pad_maximum_fusion.1 = bf16[2,1024,512]{2,1,0:T(8,128)(2,1)} fusion(bf16[2,512,512]{2,1,0:T(8,128)(2,1)S(1)} %bitcast.192, bf16[1,512,512]{2,1,0:T(8,128)(2,1)S(1)} %bitcast.196, bf16[1,512,512]{2,1,0:T(8,128)(2,1)} %bitcast.197), kind=kLoop, calls=%fused_computation.45 | loop fusion | flops 6291456 | bytes 4194304 | tf_op jit(solution)/shard_map/concatenate | solution.py:93
  24.7 1.3 collective-permute-start
  26.0 3.2 %collective-permute-start.1 = (bf16[2,1024,512]{2,1,0:T(8,128)(2,1)}, bf16[2,1024,512]{2,1,0:T(8,128)(2,1)}, u32[]{:S(2)}, u32[]{:S(2)}) collective-permute-start(bf16[2,1024,512]{2,1,0:T(8,128)(2,1)} %pad_maximum_fusion.1), channel_id=1, source_target_pairs={{0,4},{4,8},{8,12},{1,5},{5,9},{9,13},{2,6},{6,10},{10,14},{3,7},{... | collective-permute-start | bytes 6291464 | tf_op jit(solution)/shard_map/ppermute | solution.py:18
  41.0 3.6 %dynamic_update_slice.22 = bf16[2,768,512]{2,1,0:T(8,128)(2,1)S(1)} dynamic-update-slice(bf16[2,768,512]{2,1,0:T(8,128)(2,1)S(1)} %broadcast.110.clone.1, bf16[2,256,512]{2,1,0:T(8,128)(2,1)S(1)} %get-tuple-element.31, s32[]{:T(128)} %constant.6.clone.1, s32[]{:T(128)S(6)} %select_n.46, s32[]{:T(128)} %constant.6.clone.1) | dynamic-update-slice | bytes 1048580 | tf_op jit(solution)/shard_map/dynamic_update_slice | solution.py:61
  44.7 4.7 %dynamic_update_slice.23 = bf16[2,768,512]{2,1,0:T(8,128)(2,1)S(1)} dynamic-update-slice(bf16[2,768,512]{2,1,0:T(8,128)(2,1)S(1)} %broadcast.110.clone, bf16[2,256,512]{2,1,0:T(8,128)(2,1)} %get-tuple-element.32, s32[]{:T(128)} %constant.6.clone.1, s32[]{:T(128)S(6)} %select_n.47, s32[]{:T(128)} %constant.6.clone.1) | dynamic-update-slice | bytes 1048580 | tf_op jit(solution)/shard_map/dynamic_update_slice | solution.py:61
  50.6 1.2 fusion.50
  51.9 2.4 %fusion.41 = bf16[2,512,512]{2,1,0:T(8,128)(2,1)} fusion(bf16[2,768,512]{2,1,0:T(8,128)(2,1)S(1)} %dynamic_update_slice.23, bf16[2,768,512]{2,1,0:T(8,128)(2,1)S(1)} %dynamic_update_slice.22, bf16[1,512,512]{2,1,0:T(8,128)(2,1)} %bitcast.195, bf16[1,512,512]{2,1,0:T(8,128)(2,1)} %bitcast.198, pred[512]{0:T(512)(128)(4,1)S(1)} %get-tuple-element.37, ...), kind=kLoop, calls=%fused_computation.58 | loop fusion | flops 1572864 | bytes 4195328 | tf_op jit(solution)/shard_map/jit(_where)/select_n | solution.py:69
  54.3 1.9 fusion.19
  56.2 16.7 %collective-permute-done = bf16[2,1024,512]{2,1,0:T(8,128)(2,1)} collective-permute-done((bf16[2,1024,512]{2,1,0:T(8,128)(2,1)}, bf16[2,1024,512]{2,1,0:T(8,128)(2,1)}, u32[]{:S(2)}, u32[]{:S(2)}) %collective-permute-start) | collective-permute-done | bytes 2097184 | tf_op jit(solution)/shard_map/ppermute | solution.py:18
  73.0 1.3 slice.175
  75.2 90.1 %collective-permute-done.1 = bf16[2,1024,512]{2,1,0:T(8,128)(2,1)} collective-permute-done((bf16[2,1024,512]{2,1,0:T(8,128)(2,1)}, bf16[2,1024,512]{2,1,0:T(8,128)(2,1)}, u32[]{:S(2)}, u32[]{:S(2)}) %collective-permute-start.1) | collective-permute-done | bytes 2097184 | tf_op jit(solution)/shard_map/ppermute | solution.py:18
  165.3 1.3 slice.181
  167.8 3.6 %dynamic_update_slice.18 = bf16[2,768,512]{2,1,0:T(8,128)(2,1)S(1)} dynamic-update-slice(bf16[2,768,512]{2,1,0:T(8,128)(2,1)S(1)} %broadcast.110.clone.5, bf16[2,256,512]{2,1,0:T(8,128)(2,1)S(1)} %get-tuple-element.27, s32[]{:T(128)} %constant.6.clone.1, s32[]{:T(128)S(6)} %select_n.46, s32[]{:T(128)} %constant.6.clone.1) | dynamic-update-slice | bytes 1048580 | tf_op jit(solution)/shard_map/dynamic_update_slice | solution.py:61
  171.5 4.9 %dynamic_update_slice.19 = bf16[2,768,512]{2,1,0:T(8,128)(2,1)S(1)} dynamic-update-slice(bf16[2,768,512]{2,1,0:T(8,128)(2,1)S(1)} %broadcast.110.clone.4, bf16[2,256,512]{2,1,0:T(8,128)(2,1)} %get-tuple-element.28, s32[]{:T(128)} %constant.6.clone.1, s32[]{:T(128)S(6)} %select_n.47, s32[]{:T(128)} %constant.6.clone.1) | dynamic-update-slice | bytes 1048580 | tf_op jit(solution)/shard_map/dynamic_update_slice | solution.py:61
  176.5 4.9 %dynamic_update_slice.20 = bf16[2,768,512]{2,1,0:T(8,128)(2,1)S(1)} dynamic-update-slice(bf16[2,768,512]{2,1,0:T(8,128)(2,1)S(1)} %broadcast.110.clone.3, bf16[2,256,512]{2,1,0:T(8,128)(2,1)} %get-tuple-element.29, s32[]{:T(128)} %constant.6.clone.1, s32[]{:T(128)S(6)} %select_n.46, s32[]{:T(128)} %constant.6.clone.1) | dynamic-update-slice | bytes 1048580 | tf_op jit(solution)/shard_map/dynamic_update_slice | solution.py:61
  181.5 4.7 %dynamic_update_slice.21 = bf16[2,768,512]{2,1,0:T(8,128)(2,1)S(1)} dynamic-update-slice(bf16[2,768,512]{2,1,0:T(8,128)(2,1)S(1)} %broadcast.110.clone.2, bf16[2,256,512]{2,1,0:T(8,128)(2,1)} %get-tuple-element.30, s32[]{:T(128)} %constant.6.clone.1, s32[]{:T(128)S(6)} %select_n.47, s32[]{:T(128)} %constant.6.clone.1) | dynamic-update-slice | bytes 1048580 | tf_op jit(solution)/shard_map/dynamic_update_slice | solution.py:61
  186.2 2.1 fusion.43
  188.3 1.5 fusion.42
  190.6 3.6 %fusion.95 = f32[2,512]{1,0:T(2,128)S(1)} fusion(pred[512,1536]{0,1:T(8,128)(4,1)} %fusion.19, bf16[512,2,128]{0,2,1:T(8,128)(2,1)S(1)} %bitcast.205, bf16[1536,512]{1,0:T(8,128)(2,1)S(1)} %get-tuple-element.22), kind=kOutput, calls=%fused_computation.130 | convolution fusion | flops 408946176 | bytes 1445888 | tf_op jit(solution)/shard_map/sub | solution.py:44
  194.1 5.0 %fusion.32 = bf16[128,2,512]{2,0,1:T(8,128)(2,1)} fusion(f32[2,512]{1,0:T(2,128)S(1)} %fusion.95, bf16[1536,512]{1,0:T(8,128)(2,1)S(1)} %get-tuple-element.21, pred[512,1536]{0,1:T(8,128)(4,1)} %fusion.19, bf16[512,2,128]{0,2,1:T(8,128)(2,1)S(1)} %bitcast.206, bf16[1536,512]{1,0:T(8,128)(2,1)S(1)} %get-tuple-element.22), kind=kOutput, calls=%fused_computation.52 | convolution fusion | flops 813304320 | bytes 2101248 | tf_op jit(solution)/shard_map/gqk,kd->qgd/dot_general | solution.py:46
  200.2 3.7 %fusion.94 = f32[2,512]{1,0:T(2,128)S(1)} fusion(pred[512,1536]{0,1:T(8,128)(4,1)} %fusion.19, bf16[512,2,128]{0,2,1:T(8,128)(2,1)} %bitcast.203, bf16[1536,512]{1,0:T(8,128)(2,1)S(1)} %get-tuple-element.22), kind=kOutput, calls=%fused_computation.129 | convolution fusion | flops 408946176 | bytes 1445888 | tf_op jit(solution)/shard_map/sub | solution.py:44
  203.9 5.1 %fusion.31 = bf16[128,2,512]{2,0,1:T(8,128)(2,1)} fusion(f32[2,512]{1,0:T(2,128)S(1)} %fusion.94, bf16[1536,512]{1,0:T(8,128)(2,1)S(1)} %get-tuple-element.21, pred[512,1536]{0,1:T(8,128)(4,1)} %fusion.19, bf16[512,2,128]{0,2,1:T(8,128)(2,1)} %bitcast.204, bf16[1536,512]{1,0:T(8,128)(2,1)S(1)} %get-tuple-element.22), kind=kOutput, calls=%fused_computation.51 | convolution fusion | flops 813304320 | bytes 2101248 | tf_op jit(solution)/shard_map/gqk,kd->qgd/dot_general | solution.py:46
  209.0 1.8 copy.45
  210.8 3.9 %fusion.93 = f32[2,512]{1,0:T(2,128)S(1)} fusion(pred[512,1536]{0,1:T(8,128)(4,1)} %fusion.19, bf16[512,2,128]{0,2,1:T(8,128)(2,1)} %bitcast.201, bf16[1536,512]{1,0:T(8,128)(2,1)S(1)} %get-tuple-element.22), kind=kOutput, calls=%fused_computation.128 | convolution fusion | flops 408946176 | bytes 1445888 | tf_op jit(solution)/shard_map/sub | solution.py:44
  214.7 5.1 %fusion.30 = bf16[128,2,512]{2,0,1:T(8,128)(2,1)} fusion(f32[2,512]{1,0:T(2,128)S(1)} %fusion.93, bf16[1536,512]{1,0:T(8,128)(2,1)S(1)} %get-tuple-element.21, pred[512,1536]{0,1:T(8,128)(4,1)} %fusion.19, bf16[512,2,128]{0,2,1:T(8,128)(2,1)} %bitcast.202, bf16[1536,512]{1,0:T(8,128)(2,1)S(1)} %get-tuple-element.22), kind=kOutput, calls=%fused_computation.50 | convolution fusion | flops 813304320 | bytes 2101248 | tf_op jit(solution)/shard_map/gqk,kd->qgd/dot_general | solution.py:46
  219.7 1.8 copy.46
  221.5 3.7 %fusion.92 = f32[2,512]{1,0:T(2,128)S(1)} fusion(pred[512,1536]{0,1:T(8,128)(4,1)} %fusion.19, bf16[512,2,128]{0,2,1:T(8,128)(2,1)} %bitcast.199, bf16[1536,512]{1,0:T(8,128)(2,1)S(1)} %get-tuple-element.22), kind=kOutput, calls=%fused_computation.127 | convolution fusion | flops 408946176 | bytes 1445888 | tf_op jit(solution)/shard_map/sub | solution.py:44
  225.2 5.1 %fusion.29 = bf16[128,2,512]{2,0,1:T(8,128)(2,1)} fusion(f32[2,512]{1,0:T(2,128)S(1)} %fusion.92, bf16[1536,512]{1,0:T(8,128)(2,1)S(1)} %get-tuple-element.21, pred[512,1536]{0,1:T(8,128)(4,1)} %fusion.19, bf16[512,2,128]{0,2,1:T(8,128)(2,1)} %bitcast.200, bf16[1536,512]{1,0:T(8,128)(2,1)S(1)} %get-tuple-element.22), kind=kOutput, calls=%fused_computation.49 | convolution fusion | flops 813304320 | bytes 2101248 | tf_op jit(solution)/shard_map/gqk,kd->qgd/dot_general | solution.py:46
  231.4 2.1 maximum_bitcast_fusion
  (52 shorter events, 16.5 us)
Async XLA Ops:
  18.9 3.2 %copy-start.3 = (bf16[512,512]{1,0:T(8,128)(2,1)S(1)}, bf16[512,512]{1,0:T(8,128)(2,1)}, u32[]{:S(2)}) copy-start(bf16[512,512]{1,0:T(8,128)(2,1)} %param.10) | copy-start | bytes 1572868
  22.0 7.2 %copy-start.5 = (s32[1,2]{1,0:T(1,128)S(1)}, s32[1,2]{1,0:T(1,128)}, u32[]{:S(2)}) copy-start(s32[1,2]{1,0:T(1,128)} %param.14) | copy-start | bytes 28
  22.0 10.2 %copy-start.4 = (bf16[512,1024]{1,0:T(8,128)(2,1)S(1)}, bf16[512,1024]{1,0:T(8,128)(2,1)}, u32[]{:S(2)}) copy-start(bf16[512,1024]{1,0:T(8,128)(2,1)} %param.8) | copy-start | bytes 3145732
  22.1 10.2 %copy-start.6 = (s32[1,2]{1,0:T(1,128)S(1)}, s32[1,2]{1,0:T(1,128)}, u32[]{:S(2)}) copy-start(s32[1,2]{1,0:T(1,128)} %param.15) | copy-start | bytes 28
  24.7 48.3 %collective-permute-start = (bf16[2,1024,512]{2,1,0:T(8,128)(2,1)}, bf16[2,1024,512]{2,1,0:T(8,128)(2,1)}, u32[]{:S(2)}, u32[]{:S(2)}) collective-permute-start(bf16[2,1024,512]{2,1,0:T(8,128)(2,1)} %pad_maximum_fusion.1), channel_id=1, source_target_pairs={{0,8},{4,12},{1,9},{5,13},{2,10},{6,14},{3,11},{7,15},{16,24},{20,... | collective-permute-start | bytes 6291464 | tf_op jit(solution)/shard_map/ppermute | solution.py:18
  26.0 139.3 %collective-permute-start.1 = (bf16[2,1024,512]{2,1,0:T(8,128)(2,1)}, bf16[2,1024,512]{2,1,0:T(8,128)(2,1)}, u32[]{:S(2)}, u32[]{:S(2)}) collective-permute-start(bf16[2,1024,512]{2,1,0:T(8,128)(2,1)} %pad_maximum_fusion.1), channel_id=1, source_target_pairs={{0,4},{4,8},{8,12},{1,5},{5,9},{9,13},{2,6},{6,10},{10,14},{3,7},{... | collective-permute-start | bytes 6291464 | tf_op jit(solution)/shard_map/ppermute | solution.py:18
  171.4 5.0 %copy-start = (bf16[2,768,512]{2,1,0:T(8,128)(2,1)}, bf16[2,768,512]{2,1,0:T(8,128)(2,1)S(1)}, u32[]{:S(2)}) copy-start(bf16[2,768,512]{2,1,0:T(8,128)(2,1)S(1)} %dynamic_update_slice.18) | copy-start | bytes 4718596
  176.4 5.0 %copy-start.1 = (bf16[2,768,512]{2,1,0:T(8,128)(2,1)}, bf16[2,768,512]{2,1,0:T(8,128)(2,1)S(1)}, u32[]{:S(2)}) copy-start(bf16[2,768,512]{2,1,0:T(8,128)(2,1)S(1)} %dynamic_update_slice.19) | copy-start | bytes 4718596
  188.3 1.6 copy-start.2
where the time goes:
time: 235 us; the launch traced here: 233 us
  waiting for transfers between devices  107 us (46%)
  local copies, waits for them, and re-layouts  45.5 us (19%)
  matrix products  35 us (15%)
  other arithmetic  17.4 us (7%)
  blocking collectives  17 us (7%)
  between operations  7.14 us (3%)
  starting transfers between devices  4.49 us (2%)
    ppermute x2, waiting for transfers between devices, shifted(): return lax.ppermute(shard, axis, pairs)  107 us
    dynamic_update_slice x6, local copies, waits for them, and re-layouts, splice_slot(): lax.dynamic_update_slice_in_dim(blank, span_buffer[:, span_index], offset...  26.3 us
    dot_general x4, matrix products, attend(): jnp.einsum('gqk,kd->qgd', weights, value_head, preferred_element_type=jnp...  20.2 us
    sub x4, matrix products, attend(): exponent = jnp.exp(scores - row_max)  14.8 us
    all_gather x1, blocking collectives, shards(): lax.all_gather(clean_values, 'variant', axis=0, tiled=True)  8.97 us
    all_gather x1, blocking collectives, shards(): lax.all_gather(clean_keys, 'variant', axis=0, tiled=True)  8.05 us
    select_n x3, other arithmetic, splice_slot(): base_rows = jnp.where(span_mask[None, :, None], placed, base_rows)  6.07 us
    convert_element_type x4, local copies, waits for them, and re-layouts, attend(): attended.reshape(row_count, 2 * HEAD_DIM).astype(jnp.bfloat16)  5.76 us
  transfers between devices with their start and end apart: 2, of which 2 were waited for; matrix products, arithmetic and copies ran while one was open for 10% of the time, Pallas kernels for 0%

commit v1 on v0

v1 whole, which is shorter than its diff:
```python
import functools

import jax
import jax.numpy as jnp
from jax import lax
from jax.experimental import pallas as pl
from jax.experimental.pallas import tpu as pltpu
from jax.sharding import PartitionSpec as P

HEAD_DIM = 128
WINDOW = 1024
QUERY_BLOCK = 128

query_scale = 168.0 ** (-0.5)
masked_score = -1e30


def shifted(shard, axis, by):
    devices = lax.axis_size(axis)
    pairs = [(i, i + by) for i in range(devices) if 0 <= i + by < devices]
    return lax.ppermute(shard, axis, pairs)


def attend_kernel(first_ref, q_ref, kf_ref, kn_ref, ko_ref, vf_ref, vn_ref, vo_ref, o_ref):
    block = pl.program_id(0)
    rows = ko_ref.shape[0]
    query_count = q_ref.shape[0]
    local_heads = ko_ref.shape[1] // HEAD_DIM
    first_row = first_ref[0]
    query_local = block * query_count + lax.broadcasted_iota(jnp.int32, (query_count, rows), 0)
    key_local = lax.broadcasted_iota(jnp.int32, (query_count, rows), 1)
    query_pos = first_row + query_local
    masks = []
    for chunk in range(3):
        key_pos = first_row - (2 - chunk) * rows + key_local
        masks.append(
            (key_pos <= query_pos) & (query_pos - key_pos < WINDOW) & (key_pos >= 0)
        )
    key_refs = (kf_ref, kn_ref, ko_ref)
    value_refs = (vf_ref, vn_ref, vo_ref)
    for head_index in range(local_heads):
        cols = slice(head_index * HEAD_DIM, (head_index + 1) * HEAD_DIM)
        keys = [ref[:, cols] for ref in key_refs]
        values = [ref[:, cols] for ref in value_refs]
        for group in range(2):
            qcols = slice((2 * head_index + group) * HEAD_DIM, (2 * head_index + group + 1) * HEAD_DIM)
            query = q_ref[:, qcols]
            scores = []
            for chunk in range(3):
                s = lax.dot_general(
                    query, keys[chunk], (((1,), (1,)), ((), ())),
                    preferred_element_type=jnp.float32,
                ) * query_scale
                scores.append(jnp.where(masks[chunk], s, masked_score))
            row_max = jnp.maximum(
                jnp.maximum(jnp.max(scores[0], axis=1, keepdims=True),
                            jnp.max(scores[1], axis=1, keepdims=True)),
                jnp.max(scores[2], axis=1, keepdims=True),
            )
            exps = [jnp.exp(s - row_max) for s in scores]
            total = (
                jnp.sum(exps[0], axis=1, keepdims=True)
                + jnp.sum(exps[1], axis=1, keepdims=True)
                + jnp.sum(exps[2], axis=1, keepdims=True)
            )
            acc = None
            for chunk in range(3):
                w = (exps[chunk] / total).astype(jnp.bfloat16)
                part = jnp.dot(w, values[chunk], preferred_element_type=jnp.float32)
                acc = part if acc is None else acc + part
            o_ref[:, qcols] = acc.astype(o_ref.dtype)


def attend(queries, key_chunks, value_chunks, first_row):
    rows, key_cols = key_chunks[2].shape
    query_rows, query_cols = queries.shape
    blocks = query_rows // QUERY_BLOCK
    kv_spec = pl.BlockSpec((rows, key_cols), lambda i, f: (0, 0))
    grid_spec = pltpu.PrefetchScalarGridSpec(
        num_scalar_prefetch=1,
        grid=(blocks,),
        in_specs=[pl.BlockSpec((QUERY_BLOCK, query_cols), lambda i, f: (i, 0))] + [kv_spec] * 6,
        out_specs=pl.BlockSpec((QUERY_BLOCK, query_cols), lambda i, f: (i, 0)),
    )
    return pl.pallas_call(
        attend_kernel,
        grid_spec=grid_spec,
        out_shape=jax.ShapeDtypeStruct((query_rows, query_cols), jnp.bfloat16),
        compiler_params=pltpu.CompilerParams(dimension_semantics=("arbitrary",)),
    )(first_row.reshape(1), queries, *key_chunks, *value_chunks)


def gather_clean(clean_pair):
    variants = lax.axis_size("variant")
    if variants != 2:
        return lax.all_gather(clean_pair, "variant", axis=1, tiled=True)
    variant_index = lax.axis_index("variant")
    other = lax.ppermute(clean_pair, "variant", [(0, 1), (1, 0)])
    first = jnp.where(variant_index == 0, clean_pair, other)
    second = jnp.where(variant_index == 0, other, clean_pair)
    return jnp.concatenate([first, second], axis=1)


def shards(queries, keys, values, clean_keys, clean_values, owner_shard, span_offset, span_length):
    row_count = keys.shape[0]
    shard_index = lax.axis_index("seq")
    first_row = (shard_index * row_count).astype(jnp.int32)
    clean_full = gather_clean(jnp.stack([clean_keys, clean_values]))
    corrupt_pair = jnp.stack([keys, values])
    position = lax.broadcasted_iota(jnp.int32, (row_count,), 0)
    owner_here = owner_shard[0] == shard_index
    inside = jnp.zeros((row_count,), bool)
    for span_index in range(span_offset.shape[1]):
        start = span_offset[0, span_index]
        inside = inside | (
            (position >= start) & (position < start + span_length[0, span_index])
        )
    inside = inside & owner_here
    patched = jnp.where(inside[None, :, None], clean_full, corrupt_pair)
    near = shifted(patched, "seq", 1)
    far = shifted(near, "seq", 1)
    result = attend(
        queries,
        (far[0], near[0], patched[0]),
        (far[1], near[1], patched[1]),
        first_row,
    )
    return result[None]


def solution(mesh):
    placed = (
        P(("groups", "seq"), "mp"),
        P(("groups", "seq"), "mp"),
        P(("groups", "seq"), "mp"),
        P(("groups", "seq", "variant"), "mp"),
        P(("groups", "seq", "variant"), "mp"),
        P(("groups", "variant")),
        P(("groups", "variant"), None),
        P(("groups", "variant"), None),
    )
    return jax.shard_map(
        shards,
        mesh=mesh,
        in_specs=placed,
        out_specs=P("variant", ("groups", "seq"), "mp"),
        check_vma=False,
    )
```

time: 235 us -> 90.3 us (0.38)
  the two profiles are of different devices: /device:TPU:21 before, /device:TPU:0 now
where the time goes in v1:
time: 90.3 us; the launch traced here: 90.1 us
  waiting for transfers between devices  46.3 us (51%)
  Pallas kernels  22.1 us (24%)
  starting transfers between devices  11.3 us (13%)
  local copies, waits for them, and re-layouts  4.35 us (5%)
  between operations  3.21 us (4%)
  other arithmetic  2.81 us (3%)
    ppermute x2, waiting for transfers between devices, shifted(): return lax.ppermute(shard, axis, pairs)  40 us
    pallas_call x1, Pallas kernels, attend(): pl.pallas_call(attend_kernel, grid_spec=grid_spec, out_shape=jax.ShapeDty...  22.1 us
    ppermute x2, starting transfers between devices, shifted(): return lax.ppermute(shard, axis, pairs)  8.24 us
    ppermute x1, waiting for transfers between devices, gather_clean(): other = lax.ppermute(clean_pair, 'variant', [(0, 1), (1, 0)])  6.31 us
    ppermute x1, starting transfers between devices, gather_clean(): other = lax.ppermute(clean_pair, 'variant', [(0, 1), (1, 0)])  3.04 us
  transfers between devices with their start and end apart: 3, of which 3 were waited for; matrix products, arithmetic and copies ran while one was open for 5% of the time, Pallas kernels for 0%

profile of v1, /device:TPU:0, one launch (start us, length us, event | category | flops | bytes accessed | tf_op | source)
XLA Modules:
  0.0 90.1 jit_solution(11273009700001047827)
XLA Ops:
  0.0 0.0 copy-start.1
  0.0 0.0 copy-start
  0.0 0.0 copy-start.4
  0.0 0.0 copy-start.5
  0.0 1.1 %pad_maximum_fusion = bf16[2,256,512]{2,1,0:T(8,128)(2,1)S(1)} fusion(bf16[1,256,512]{2,1,0:T(8,128)(2,1)} %bitcast.24, bf16[1,256,512]{2,1,0:T(8,128)(2,1)} %bitcast.26), kind=kLoop, calls=%fused_computation.7 | loop fusion | flops 262144 | bytes 1048576 | tf_op jit(solution)/shard_map/stack | solution.py:108
  1.1 3.0 %collective-permute-start = (bf16[2,256,512]{2,1,0:T(8,128)(2,1)S(1)}, bf16[2,256,512]{2,1,0:T(8,128)(2,1)S(1)}, u32[]{:S(2)}, u32[]{:S(2)}) collective-permute-start(bf16[2,256,512]{2,1,0:T(8,128)(2,1)S(1)} %pad_maximum_fusion), channel_id=1, source_target_pairs={{0,2},{2,0},{1,3},{3,1},{4,6},{6,4},{5,7},{7,5},{8,10},{10,8},{9,1... | collective-permute-start | bytes 1572872 | tf_op jit(solution)/shard_map/ppermute | solution.py:98
  4.8 0.0 copy-done.4
  4.9 0.6 fusion.5
  5.5 0.0 copy-done.5
  5.5 0.6 fusion.4
  8.5 1.3 %fusion.2 = pred[512]{0:T(512)(128)(4,1)S(1)} fusion(s32[]{:T(128)S(6)} %add.7, s32[]{:T(128)} %bitcast.3, s32[]{:T(128)S(6)} %add.6, s32[]{:T(128)} %bitcast.1, pred[]{:T(512)S(6)} %eq.7), kind=kLoop, calls=%fused_computation.16 | loop fusion | flops 4096 | bytes 529 | tf_op jit(solution)/shard_map/and | solution.py:118
  9.8 0.0 copy-start.2
  9.8 0.0 copy-start.3
  9.8 6.3 %collective-permute-done = bf16[2,256,512]{2,1,0:T(8,128)(2,1)S(1)} collective-permute-done((bf16[2,256,512]{2,1,0:T(8,128)(2,1)S(1)}, bf16[2,256,512]{2,1,0:T(8,128)(2,1)S(1)}, u32[]{:S(2)}, u32[]{:S(2)}) %collective-permute-start) | collective-permute-done | bytes 524320 | tf_op jit(solution)/shard_map/ppermute | solution.py:98
  16.1 0.0 copy-done.1
  16.1 0.0 copy-done
  16.1 0.1 broadcast_select_fusion.1
  16.2 0.0 copy-done.2
  16.2 0.0 copy-done.3
  16.2 0.3 maximum_select_fusion
  16.5 3.8 %collective-permute-start.1 = (bf16[2,512,512]{2,1,0:T(8,128)(2,1)S(1)}, bf16[2,512,512]{2,1,0:T(8,128)(2,1)S(1)}, u32[]{:S(2)}, u32[]{:S(2)}) collective-permute-start(bf16[2,512,512]{2,1,0:T(8,128)(2,1)S(1)} %maximum_select_fusion), channel_id=1, source_target_pairs={{0,4},{4,8},{8,12},{1,5},{5,9},{9,13},{2,6},{6,10},{10,14},{3,7},{... | collective-permute-start | bytes 3145736 | tf_op jit(solution)/shard_map/ppermute | solution.py:21
  20.3 21.5 %collective-permute-done.1 = bf16[2,512,512]{2,1,0:T(8,128)(2,1)S(1)} collective-permute-done((bf16[2,512,512]{2,1,0:T(8,128)(2,1)S(1)}, bf16[2,512,512]{2,1,0:T(8,128)(2,1)S(1)}, u32[]{:S(2)}, u32[]{:S(2)}) %collective-permute-start.1) | collective-permute-done | bytes 1048608 | tf_op jit(solution)/shard_map/ppermute | solution.py:21
  41.8 4.4 %collective-permute-start.2 = (bf16[2,512,512]{2,1,0:T(8,128)(2,1)S(1)}, bf16[2,512,512]{2,1,0:T(8,128)(2,1)S(1)}, u32[]{:S(2)}, u32[]{:S(2)}) collective-permute-start(bf16[2,512,512]{2,1,0:T(8,128)(2,1)S(1)} %collective-permute-done.1), channel_id=1, source_target_pairs={{0,4},{4,8},{8,12},{1,5},{5,9},{9,13},{2,6},{6,10},{10,14},{3,7},{... | collective-permute-start | bytes 3145736 | tf_op jit(solution)/shard_map/ppermute | solution.py:21
  46.3 1.0 %slice_bitcast_fusion = (bf16[512,512]{1,0:T(8,128)(2,1)}, bf16[512,512]{1,0:T(8,128)(2,1)}) fusion(bf16[2,512,512]{2,1,0:T(8,128)(2,1)S(1)} %maximum_select_fusion), kind=kLoop, calls=%fused_computation.1 | loop fusion | bytes 2097152 | tf_op jit(solution)/shard_map/squeeze | solution.py:125
  47.3 1.1 %slice_bitcast_fusion.1 = (bf16[512,512]{1,0:T(8,128)(2,1)}, bf16[512,512]{1,0:T(8,128)(2,1)}) fusion(bf16[2,512,512]{2,1,0:T(8,128)(2,1)S(1)} %collective-permute-done.1), kind=kLoop, calls=%fused_computation.2 | loop fusion | bytes 2097152 | tf_op jit(solution)/shard_map/squeeze | solution.py:125
  48.4 18.5 %collective-permute-done.2 = bf16[2,512,512]{2,1,0:T(8,128)(2,1)S(1)} collective-permute-done((bf16[2,512,512]{2,1,0:T(8,128)(2,1)S(1)}, bf16[2,512,512]{2,1,0:T(8,128)(2,1)S(1)}, u32[]{:S(2)}, u32[]{:S(2)}) %collective-permute-start.2) | collective-permute-done | bytes 1048608 | tf_op jit(solution)/shard_map/ppermute | solution.py:21
  66.9 1.1 %slice_bitcast_fusion.2 = (bf16[512,512]{1,0:T(8,128)(2,1)}, bf16[512,512]{1,0:T(8,128)(2,1)}) fusion(bf16[2,512,512]{2,1,0:T(8,128)(2,1)S(1)} %collective-permute-done.2), kind=kLoop, calls=%fused_computation.3 | loop fusion | bytes 2097152 | tf_op jit(solution)/shard_map/squeeze | solution.py:125
  67.9 22.1 %shard_map.82 = bf16[512,1024]{1,0:T(8,128)(2,1)} custom-call(s32[1]{0:T(128)} %bitcast.first_ref, bf16[512,1024]{1,0:T(8,128)(2,1)} %q_ref.1, bf16[512,512]{1,0:T(8,128)(2,1)} %get-tuple-element.10.kf_ref, bf16[512,512]{1,0:T(8,128)(2,1)} %get-tuple-element.8.kn_ref, bf16[512,512]{1,0:T(8,128)(2,1)} %get-tuple-element.6.ko_ref, ...), custom_call_target="tpu_custom_call" | custom-call | tf_op jit(solution)/shard_map/pallas_call | solution.py:85
Async XLA Ops:
  0.0 16.1 %copy-start.1 = (bf16[256,512]{1,0:T(8,128)(2,1)S(1)}, bf16[256,512]{1,0:T(8,128)(2,1)}, u32[]{:S(2)}) copy-start(bf16[256,512]{1,0:T(8,128)(2,1)} %param.11) | copy-start | bytes 786436
  0.0 16.1 %copy-start = (bf16[256,512]{1,0:T(8,128)(2,1)S(1)}, bf16[256,512]{1,0:T(8,128)(2,1)}, u32[]{:S(2)}) copy-start(bf16[256,512]{1,0:T(8,128)(2,1)} %param.12) | copy-start | bytes 786436
  0.0 4.8 %copy-start.4 = (s32[1,2]{1,0:T(1,128)S(1)}, s32[1,2]{1,0:T(1,128)}, u32[]{:S(2)}) copy-start(s32[1,2]{1,0:T(1,128)} %param.14) | copy-start | bytes 28
  0.0 5.5 %copy-start.5 = (s32[1,2]{1,0:T(1,128)S(1)}, s32[1,2]{1,0:T(1,128)}, u32[]{:S(2)}) copy-start(s32[1,2]{1,0:T(1,128)} %param.15) | copy-start | bytes 28
  1.1 15.0 %collective-permute-start = (bf16[2,256,512]{2,1,0:T(8,128)(2,1)S(1)}, bf16[2,256,512]{2,1,0:T(8,128)(2,1)S(1)}, u32[]{:S(2)}, u32[]{:S(2)}) collective-permute-start(bf16[2,256,512]{2,1,0:T(8,128)(2,1)S(1)} %pad_maximum_fusion), channel_id=1, source_target_pairs={{0,2},{2,0},{1,3},{3,1},{4,6},{6,4},{5,7},{7,5},{8,10},{10,8},{9,1... | collective-permute-start | bytes 1572872 | tf_op jit(solution)/shard_map/ppermute | solution.py:98
  9.8 6.4 %copy-start.2 = (bf16[512,512]{1,0:T(8,128)(2,1)S(1)}, bf16[512,512]{1,0:T(8,128)(2,1)}, u32[]{:S(2)}) copy-start(bf16[512,512]{1,0:T(8,128)(2,1)} %param.10) | copy-start | bytes 1572868
  9.8 6.4 %copy-start.3 = (bf16[512,512]{1,0:T(8,128)(2,1)S(1)}, bf16[512,512]{1,0:T(8,128)(2,1)}, u32[]{:S(2)}) copy-start(bf16[512,512]{1,0:T(8,128)(2,1)} %param.9) | copy-start | bytes 1572868
  16.5 25.3 %collective-permute-start.1 = (bf16[2,512,512]{2,1,0:T(8,128)(2,1)S(1)}, bf16[2,512,512]{2,1,0:T(8,128)(2,1)S(1)}, u32[]{:S(2)}, u32[]{:S(2)}) collective-permute-start(bf16[2,512,512]{2,1,0:T(8,128)(2,1)S(1)} %maximum_select_fusion), channel_id=1, source_target_pairs={{0,4},{4,8},{8,12},{1,5},{5,9},{9,13},{2,6},{6,10},{10,14},{3,7},{... | collective-permute-start | bytes 3145736 | tf_op jit(solution)/shard_map/ppermute | solution.py:21
  41.8 25.1 %collective-permute-start.2 = (bf16[2,512,512]{2,1,0:T(8,128)(2,1)S(1)}, bf16[2,512,512]{2,1,0:T(8,128)(2,1)S(1)}, u32[]{:S(2)}, u32[]{:S(2)}) collective-permute-start(bf16[2,512,512]{2,1,0:T(8,128)(2,1)S(1)} %collective-permute-done.1), channel_id=1, source_target_pairs={{0,4},{4,8},{8,12},{1,5},{5,9},{9,13},{2,6},{6,10},{10,14},{3,7},{... | collective-permute-start | bytes 3145736 | tf_op jit(solution)/shard_map/ppermute | solution.py:21

commit v2 on v1

v2 whole, which is shorter than its diff:
```python
import jax
import jax.numpy as jnp
from jax import lax
from jax.experimental import pallas as pl
from jax.experimental.pallas import tpu as pltpu
from jax.sharding import PartitionSpec as P

HEAD_DIM = 128
WINDOW = 1024
QUERY_BLOCK = 128

query_scale = 168.0 ** (-0.5)
masked_score = -1e30


def shifted(shard, axis, by):
    devices = lax.axis_size(axis)
    pairs = [(i, i + by) for i in range(devices) if 0 <= i + by < devices]
    return lax.ppermute(shard, axis, pairs)


def chunk_kernel(chunk, first, last, rows, query_block, group):
    blocks = rows // query_block

    def kernel(first_ref, q_ref, k_ref, v_ref, *rest):
        if first:
            m_out, l_out, acc_out = rest
        elif last:
            m_in, l_in, acc_in, o_ref = rest
        else:
            m_in, l_in, acc_in, m_out, l_out, acc_out = rest
        head = pl.program_id(0)
        first_row = first_ref[0]
        stat_cols = (m_out if first else m_in).shape[1]
        for block in range(blocks):
            r0 = block * query_block
            if chunk == 2:
                k0, k1 = 0, r0 + query_block
            elif chunk == 1:
                k0, k1 = 0, rows
            else:
                k0, k1 = r0, rows
            keys = k_ref[k0:k1, :]
            values = v_ref[k0:k1, :]
            shape = (query_block, k1 - k0)
            query_pos = first_row + r0 + lax.broadcasted_iota(jnp.int32, shape, 0)
            key_pos = first_row - (2 - chunk) * rows + k0 + lax.broadcasted_iota(jnp.int32, shape, 1)
            allowed = (key_pos <= query_pos) & (query_pos - key_pos < WINDOW) & (key_pos >= 0)
            qrows = slice(r0, r0 + query_block)
            lane = lax.broadcasted_iota(jnp.int32, (query_block, stat_cols), 1)
            if not first:
                m_block = m_in[qrows, :]
                l_block = l_in[qrows, :]
            if not last:
                m_keep = m_out[qrows, :]
                l_keep = l_out[qrows, :]
            for g in range(group):
                pick = lane == group * head + g
                cols = slice(g * HEAD_DIM, (g + 1) * HEAD_DIM)
                query = q_ref[qrows, cols]
                s = lax.dot_general(
                    query, keys, (((1,), (1,)), ((), ())),
                    preferred_element_type=jnp.float32,
                ) * query_scale
                s = jnp.where(allowed, s, masked_score)
                block_max = jnp.max(s, axis=1, keepdims=True)
                if first:
                    m_new = block_max
                else:
                    m_prev = jnp.sum(jnp.where(pick, m_block, 0.0), axis=1, keepdims=True)
                    l_prev = jnp.sum(jnp.where(pick, l_block, 0.0), axis=1, keepdims=True)
                    m_new = jnp.maximum(m_prev, block_max)
                    alpha = jnp.exp(m_prev - m_new)
                p = jnp.exp(s - m_new)
                l_part = jnp.sum(p, axis=1, keepdims=True)
                pv = jnp.dot(p.astype(jnp.bfloat16), values, preferred_element_type=jnp.float32)
                if first:
                    l_new = l_part
                    acc_new = pv
                else:
                    l_new = alpha * l_prev + l_part
                    acc_new = alpha * acc_in[qrows, cols] + pv
                if last:
                    o_ref[qrows, cols] = (acc_new / l_new).astype(o_ref.dtype)
                else:
                    acc_out[qrows, cols] = acc_new
                    m_keep = jnp.where(pick, m_new, m_keep)
                    l_keep = jnp.where(pick, l_new, l_keep)
            if not last:
                m_out[qrows, :] = m_keep
                l_out[qrows, :] = l_keep

    return kernel


def attend_chunk(chunk, queries, key_rows, value_rows, first_row, state):
    rows, key_cols = key_rows.shape
    query_cols = queries.shape[1]
    kv_heads = key_cols // HEAD_DIM
    group = query_cols // key_cols
    heads = kv_heads * group
    first = state is None
    last = chunk == 0
    kernel = chunk_kernel(chunk, first, last, rows, QUERY_BLOCK, group)
    q_spec = pl.BlockSpec((rows, group * HEAD_DIM), lambda h, f: (0, h))
    kv_spec = pl.BlockSpec((rows, HEAD_DIM), lambda h, f: (0, h))
    stat_spec = pl.BlockSpec((rows, heads), lambda h, f: (0, 0))
    state_specs = [stat_spec, stat_spec, q_spec]
    in_specs = [q_spec, kv_spec, kv_spec] + ([] if first else state_specs)
    stat_shape = jax.ShapeDtypeStruct((rows, heads), jnp.float32)
    if last:
        out_specs = q_spec
        out_shape = jax.ShapeDtypeStruct((rows, query_cols), jnp.bfloat16)
    else:
        out_specs = state_specs
        out_shape = [stat_shape, stat_shape, jax.ShapeDtypeStruct((rows, query_cols), jnp.float32)]
    keys_per_row = rows + QUERY_BLOCK // 2 if chunk != 1 else rows
    cost = pl.CostEstimate(
        flops=4 * heads * rows * keys_per_row * HEAD_DIM,
        transcendentals=heads * rows * keys_per_row,
        bytes_accessed=rows * query_cols * (2 + 4 + (0 if first else 4)) + 4 * rows * key_cols,
    )
    grid_spec = pltpu.PrefetchScalarGridSpec(
        num_scalar_prefetch=1,
        grid=(kv_heads,),
        in_specs=in_specs,
        out_specs=out_specs,
    )
    return pl.pallas_call(
        kernel,
        grid_spec=grid_spec,
        out_shape=out_shape,
        cost_estimate=cost,
        compiler_params=pltpu.CompilerParams(dimension_semantics=("arbitrary",)),
    )(first_row.reshape(1), queries, key_rows, value_rows, *([] if first else state))


def gather_clean(clean_pair):
    variants = lax.axis_size("variant")
    if variants != 2:
        return lax.all_gather(clean_pair, "variant", axis=1, tiled=True)
    variant_index = lax.axis_index("variant")
    other = lax.ppermute(clean_pair, "variant", [(0, 1), (1, 0)])
    first = jnp.where(variant_index == 0, clean_pair, other)
    second = jnp.where(variant_index == 0, other, clean_pair)
    return jnp.concatenate([first, second], axis=1)


def shards(queries, keys, values, clean_keys, clean_values, owner_shard, span_offset, span_length):
    row_count = keys.shape[0]
    shard_index = lax.axis_index("seq")
    first_row = (shard_index * row_count).astype(jnp.int32)
    clean_full = gather_clean(jnp.stack([clean_keys, clean_values]))
    corrupt_pair = jnp.stack([keys, values])
    position = lax.broadcasted_iota(jnp.int32, (row_count,), 0)
    owner_here = owner_shard[0] == shard_index
    inside = jnp.zeros((row_count,), bool)
    for span_index in range(span_offset.shape[1]):
        start = span_offset[0, span_index]
        inside = inside | (
            (position >= start) & (position < start + span_length[0, span_index])
        )
    inside = inside & owner_here
    patched = jnp.where(inside[None, :, None], clean_full, corrupt_pair)
    near = shifted(patched, "seq", 1)
    far = shifted(near, "seq", 1)
    assert WINDOW == 2 * row_count
    state = attend_chunk(2, queries, patched[0], patched[1], first_row, None)
    state = attend_chunk(1, queries, near[0], near[1], first_row, state)
    result = attend_chunk(0, queries, far[0], far[1], first_row, state)
    return result[None]


def solution(mesh):
    placed = (
        P(("groups", "seq"), "mp"),
        P(("groups", "seq"), "mp"),
        P(("groups", "seq"), "mp"),
        P(("groups", "seq", "variant"), "mp"),
        P(("groups", "seq", "variant"), "mp"),
        P(("groups", "variant")),
        P(("groups", "variant"), None),
        P(("groups", "variant"), None),
    )
    return jax.shard_map(
        shards,
        mesh=mesh,
        in_specs=placed,
        out_specs=P("variant", ("groups", "seq"), "mp"),
        check_vma=False,
    )
```

time: 90.3 us -> 83.3 us (0.922)
  waiting for transfers between devices: 46.3 us -> 26.3 us
  Pallas kernels: 22.1 us -> 32.5 us
  local copies, waits for them, and re-layouts: 4.35 us -> 5.82 us
  other arithmetic: 2.81 us -> 3.87 us
    ppermute x2, waiting for transfers between devices: 40 us -> 21.5 us  [shifted(): return lax.ppermute(shard, axis, pairs)]
    pallas_call x1 -> x3, Pallas kernels: 22.1 us -> 32.5 us  [attend_chunk(): pl.pallas_call(kernel, grid_spec=grid_spec, out_shape=out_shape, cost_est...]
    ppermute x1, waiting for transfers between devices: 6.31 us -> 4.82 us  [gather_clean(): other = lax.ppermute(clean_pair, 'variant', [(0, 1), (1, 0)])]
    select_n x1, other arithmetic: 0.07 us -> 1.1 us  [gather_clean(): first = jnp.where(variant_index == 0, clean_pair, other)]
  transfers between devices with their start and end apart: 3 -> 3, of which waited for: 3 -> 2; matrix products, arithmetic and copies ran while one was open for 5% -> 7% of each run, Pallas kernels for 0% -> 28%
where the time goes in v2:
time: 83.3 us; the launch traced here: 83 us
  Pallas kernels  32.5 us (39%)
  waiting for transfers between devices  26.3 us (32%)
  starting transfers between devices  11.3 us (14%)
  local copies, waits for them, and re-layouts  5.82 us (7%)
  other arithmetic  3.87 us (5%)
  between operations  3.2 us (4%)
    pallas_call x3, Pallas kernels, attend_chunk(): pl.pallas_call(kernel, grid_spec=grid_spec, out_shape=out_shape, cost_est...  32.5 us
    ppermute x2, waiting for transfers between devices, shifted(): return lax.ppermute(shard, axis, pairs)  21.5 us
    ppermute x2, starting transfers between devices, shifted(): return lax.ppermute(shard, axis, pairs)  8.24 us
    ppermute x1, waiting for transfers between devices, gather_clean(): other = lax.ppermute(clean_pair, 'variant', [(0, 1), (1, 0)])  4.82 us
    ppermute x1, starting transfers between devices, gather_clean(): other = lax.ppermute(clean_pair, 'variant', [(0, 1), (1, 0)])  3.03 us
  transfers between devices with their start and end apart: 3, of which 2 were waited for; matrix products, arithmetic and copies ran while one was open for 7% of the time, Pallas kernels for 28%

profile of v2, /device:TPU:0, one launch (start us, length us, event | category | flops | bytes accessed | tf_op | source)
XLA Modules:
  0.0 83.0 jit_solution(615637346927570476)
XLA Ops:
  0.0 0.0 copy-start
  0.0 0.0 copy-start.1
  0.0 1.2 %pad_maximum_fusion = bf16[2,256,512]{2,1,0:T(8,128)(2,1)S(1)} fusion(bf16[1,256,512]{2,1,0:T(8,128)(2,1)} %bitcast.24, bf16[1,256,512]{2,1,0:T(8,128)(2,1)} %bitcast.26), kind=kLoop, calls=%fused_computation.7 | loop fusion | flops 262144 | bytes 1048576 | tf_op jit(solution)/shard_map/stack | solution.py:153
  1.2 3.0 %collective-permute-start = (bf16[2,256,512]{2,1,0:T(8,128)(2,1)S(1)}, bf16[2,256,512]{2,1,0:T(8,128)(2,1)S(1)}, u32[]{:S(2)}, u32[]{:S(2)}) collective-permute-start(bf16[2,256,512]{2,1,0:T(8,128)(2,1)S(1)} %pad_maximum_fusion), channel_id=1, source_target_pairs={{0,2},{2,0},{1,3},{3,1},{4,6},{6,4},{5,7},{7,5},{8,10},{10,8},{9,1... | collective-permute-start | bytes 1572872 | tf_op jit(solution)/shard_map/ppermute | solution.py:143
  4.9 1.3 %fusion.5 = (s32[1,1]{1,0:T(1,128)}, s32[1,1]{1,0:T(1,128)}) fusion(s32[1,2]{1,0:T(1,128)} %param.14), kind=kLoop, calls=%fused_computation.19 | loop fusion | bytes 16 | tf_op jit(solution)/shard_map/slice | solution.py:159
  6.2 1.3 %fusion.4 = (s32[1,1]{1,0:T(1,128)}, s32[1,1]{1,0:T(1,128)}) fusion(s32[1,2]{1,0:T(1,128)} %param.15), kind=kLoop, calls=%fused_computation.18 | loop fusion | bytes 16 | tf_op jit(solution)/shard_map/slice | solution.py:161
  10.0 1.3 %fusion.2 = pred[512]{0:T(512)(128)(4,1)S(1)} fusion(s32[]{:T(128)S(6)} %add.7, s32[]{:T(128)} %bitcast.3, s32[]{:T(128)S(6)} %add.6, s32[]{:T(128)} %bitcast.1, pred[]{:T(512)S(6)} %eq.7), kind=kLoop, calls=%fused_computation.16 | loop fusion | flops 4096 | bytes 529 | tf_op jit(solution)/shard_map/and | solution.py:163
  11.3 4.8 %collective-permute-done = bf16[2,256,512]{2,1,0:T(8,128)(2,1)S(1)} collective-permute-done((bf16[2,256,512]{2,1,0:T(8,128)(2,1)S(1)}, bf16[2,256,512]{2,1,0:T(8,128)(2,1)S(1)}, u32[]{:S(2)}, u32[]{:S(2)}) %collective-permute-start) | collective-permute-done | bytes 524320 | tf_op jit(solution)/shard_map/ppermute | solution.py:143
  16.1 1.1 %broadcast_select_fusion.1 = (bf16[2,256,512]{2,1,0:T(8,128)(2,1)S(1)}, bf16[2,256,512]{2,1,0:T(8,128)(2,1)S(1)}) fusion(bf16[2,256,512]{2,1,0:T(8,128)(2,1)S(1)} %collective-permute-done, pred[]{:T(512)S(6)} %eq.8, bf16[1,256,512]{2,1,0:T(8,128)(2,1)} %bitcast.25, bf16[1,256,512]{2,1,0:T(8,128)(2,1)} %bitcast.27), kind=kLoop, calls=%fused_computation.9 | loop fusion | flops 786432 | bytes 2097153 | tf_op jit(solution)/shard_map/jit(_where)/select_n | solution.py:144
  17.2 0.0 copy-done
  17.2 0.0 copy-done.1
  17.3 0.3 maximum_select_fusion
  17.6 3.8 %collective-permute-start.1 = (bf16[2,512,512]{2,1,0:T(8,128)(2,1)S(1)}, bf16[2,512,512]{2,1,0:T(8,128)(2,1)S(1)}, u32[]{:S(2)}, u32[]{:S(2)}) collective-permute-start(bf16[2,512,512]{2,1,0:T(8,128)(2,1)S(1)} %maximum_select_fusion), channel_id=1, source_target_pairs={{0,4},{4,8},{8,12},{1,5},{5,9},{9,13},{2,6},{6,10},{10,14},{3,7},{... | collective-permute-start | bytes 3145736 | tf_op jit(solution)/shard_map/ppermute | solution.py:19
  21.4 21.5 %collective-permute-done.1 = bf16[2,512,512]{2,1,0:T(8,128)(2,1)S(1)} collective-permute-done((bf16[2,512,512]{2,1,0:T(8,128)(2,1)S(1)}, bf16[2,512,512]{2,1,0:T(8,128)(2,1)S(1)}, u32[]{:S(2)}, u32[]{:S(2)}) %collective-permute-start.1) | collective-permute-done | bytes 1048608 | tf_op jit(solution)/shard_map/ppermute | solution.py:19
  42.9 4.4 %collective-permute-start.2 = (bf16[2,512,512]{2,1,0:T(8,128)(2,1)S(1)}, bf16[2,512,512]{2,1,0:T(8,128)(2,1)S(1)}, u32[]{:S(2)}, u32[]{:S(2)}) collective-permute-start(bf16[2,512,512]{2,1,0:T(8,128)(2,1)S(1)} %collective-permute-done.1), channel_id=1, source_target_pairs={{0,4},{4,8},{8,12},{1,5},{5,9},{9,13},{2,6},{6,10},{10,14},{3,7},{... | collective-permute-start | bytes 3145736 | tf_op jit(solution)/shard_map/ppermute | solution.py:19
  47.3 1.0 %slice_bitcast_fusion = (bf16[512,512]{1,0:T(8,128)(2,1)}, bf16[512,512]{1,0:T(8,128)(2,1)}) fusion(bf16[2,512,512]{2,1,0:T(8,128)(2,1)S(1)} %maximum_select_fusion), kind=kLoop, calls=%fused_computation.1 | loop fusion | bytes 2097152 | tf_op jit(solution)/shard_map/squeeze | solution.py:168
  48.4 10.9 %shard_map.82 = (f32[512,8]{1,0:T(8,128)}, f32[512,8]{1,0:T(8,128)}, f32[512,1024]{1,0:T(8,128)}) custom-call(s32[1]{0:T(128)} %bitcast.first_ref, bf16[512,1024]{1,0:T(8,128)(2,1)} %q_ref.5, bf16[512,512]{1,0:T(8,128)(2,1)} %get-tuple-element.18.k_ref, bf16[512,512]{1,0:T(8,128)(2,1)} %get-tuple-element.17.v_ref), custom_call_target="tpu_custom_call" | custom-call | flops 1207959552 | bytes 4194304 | tf_op jit(solution)/shard_map/pallas_call | solution.py:129
  59.2 1.0 %slice_bitcast_fusion.2 = (bf16[512,512]{1,0:T(8,128)(2,1)}, bf16[512,512]{1,0:T(8,128)(2,1)}) fusion(bf16[2,512,512]{2,1,0:T(8,128)(2,1)S(1)} %collective-permute-done.1), kind=kLoop, calls=%fused_computation.3 | loop fusion | bytes 2097152 | tf_op jit(solution)/shard_map/squeeze | solution.py:169
  60.3 12.2 %shard_map.83 = (f32[512,8]{1,0:T(8,128)}, f32[512,8]{1,0:T(8,128)}, f32[512,1024]{1,0:T(8,128)}) custom-call(s32[1]{0:T(128)} %bitcast.first_ref, bf16[512,1024]{1,0:T(8,128)(2,1)} %q_ref.5, bf16[512,512]{1,0:T(8,128)(2,1)} %get-tuple-element.20.k_ref, bf16[512,512]{1,0:T(8,128)(2,1)} %get-tuple-element.19.v_ref, f32[512,8]{1,0:T(8,128)} %get-tuple-element.11.rest_0_, ...), custom_call_target="tpu_custom_call" | custom-call | flops 1073741824 | bytes 6291456 | tf_op jit(solution)/shard_map/pallas_call | solution.py:129
  72.5 0.0 collective-permute-done.2
  72.5 1.0 %slice_bitcast_fusion.4 = (bf16[512,512]{1,0:T(8,128)(2,1)}, bf16[512,512]{1,0:T(8,128)(2,1)}) fusion(bf16[2,512,512]{2,1,0:T(8,128)(2,1)S(1)} %collective-permute-done.2), kind=kLoop, calls=%fused_computation.5 | loop fusion | bytes 2097152 | tf_op jit(solution)/shard_map/squeeze | solution.py:170
  73.6 9.4 %shard_map.84 = bf16[512,1024]{1,0:T(8,128)(2,1)} custom-call(s32[1]{0:T(128)} %bitcast.first_ref, bf16[512,1024]{1,0:T(8,128)(2,1)} %q_ref.5, bf16[512,512]{1,0:T(8,128)(2,1)} %get-tuple-element.22.k_ref, bf16[512,512]{1,0:T(8,128)(2,1)} %get-tuple-element.21.v_ref, f32[512,8]{1,0:T(8,128)} %get-tuple-element.14.rest_0_, ...), custom_call_target="tpu_custom_call" | custom-call | flops 1207959552 | bytes 6291456 | tf_op jit(solution)/shard_map/pallas_call | solution.py:129
Async XLA Ops:
  0.0 17.2 %copy-start = (bf16[512,512]{1,0:T(8,128)(2,1)S(1)}, bf16[512,512]{1,0:T(8,128)(2,1)}, u32[]{:S(2)}) copy-start(bf16[512,512]{1,0:T(8,128)(2,1)} %param.10) | copy-start | bytes 1572868
  0.0 17.2 %copy-start.1 = (bf16[512,512]{1,0:T(8,128)(2,1)S(1)}, bf16[512,512]{1,0:T(8,128)(2,1)}, u32[]{:S(2)}) copy-start(bf16[512,512]{1,0:T(8,128)(2,1)} %param.9) | copy-start | bytes 1572868
  1.2 15.0 %collective-permute-start = (bf16[2,256,512]{2,1,0:T(8,128)(2,1)S(1)}, bf16[2,256,512]{2,1,0:T(8,128)(2,1)S(1)}, u32[]{:S(2)}, u32[]{:S(2)}) collective-permute-start(bf16[2,256,512]{2,1,0:T(8,128)(2,1)S(1)} %pad_maximum_fusion), channel_id=1, source_target_pairs={{0,2},{2,0},{1,3},{3,1},{4,6},{6,4},{5,7},{7,5},{8,10},{10,8},{9,1... | collective-permute-start | bytes 1572872 | tf_op jit(solution)/shard_map/ppermute | solution.py:143
  17.6 25.3 %collective-permute-start.1 = (bf16[2,512,512]{2,1,0:T(8,128)(2,1)S(1)}, bf16[2,512,512]{2,1,0:T(8,128)(2,1)S(1)}, u32[]{:S(2)}, u32[]{:S(2)}) collective-permute-start(bf16[2,512,512]{2,1,0:T(8,128)(2,1)S(1)} %maximum_select_fusion), channel_id=1, source_target_pairs={{0,4},{4,8},{8,12},{1,5},{5,9},{9,13},{2,6},{6,10},{10,14},{3,7},{... | collective-permute-start | bytes 3145736 | tf_op jit(solution)/shard_map/ppermute | solution.py:19
  42.9 29.7 %collective-permute-start.2 = (bf16[2,512,512]{2,1,0:T(8,128)(2,1)S(1)}, bf16[2,512,512]{2,1,0:T(8,128)(2,1)S(1)}, u32[]{:S(2)}, u32[]{:S(2)}) collective-permute-start(bf16[2,512,512]{2,1,0:T(8,128)(2,1)S(1)} %collective-permute-done.1), channel_id=1, source_target_pairs={{0,4},{4,8},{8,12},{1,5},{5,9},{9,13},{2,6},{6,10},{10,14},{3,7},{... | collective-permute-start | bytes 3145736 | tf_op jit(solution)/shard_map/ppermute | solution.py:19

commit v3 on v2

v3 whole, which is shorter than its diff:
```python
import jax
import jax.numpy as jnp
from jax import lax
from jax.experimental import pallas as pl
from jax.experimental.pallas import tpu as pltpu
from jax.sharding import PartitionSpec as P


HEAD_DIM = 128
WINDOW = 1024
QUERY_BLOCK = 128

query_scale = 168.0 ** (-0.5)
log2_scale = query_scale * 1.4426950408889634
masked_score = -1e30


def shifted(shard, axis, by):
    devices = lax.axis_size(axis)
    pairs = [(i, i + by) for i in range(devices) if 0 <= i + by < devices]
    return lax.ppermute(shard, axis, pairs)


def chunk_kernel(chunk, first, last, rows, query_block, group):
    blocks = rows // query_block

    def kernel(first_ref, q_ref, k_ref, v_ref, *rest):
        if first:
            m_out, l_out, acc_out = rest
        elif last:
            m_in, l_in, acc_in, o_ref = rest
        else:
            m_in, l_in, acc_in, m_out, l_out, acc_out = rest
        head = pl.program_id(0)
        first_row = first_ref[0]
        stat_cols = (m_out if first else m_in).shape[1]
        diag_shape = (query_block, query_block)
        diag_row = lax.broadcasted_iota(jnp.int32, diag_shape, 0)
        diag_col = lax.broadcasted_iota(jnp.int32, diag_shape, 1)
        diag_allowed = diag_col <= diag_row if chunk == 2 else diag_col > diag_row
        lane = lax.broadcasted_iota(jnp.int32, (query_block, stat_cols), 1)

        def compute():
            for block in range(blocks):
                r0 = block * query_block
                if chunk == 2:
                    pieces = [(0, r0, False), (r0, r0 + query_block, True)]
                elif chunk == 1:
                    pieces = [(0, rows, False)]
                else:
                    pieces = [(r0, r0 + query_block, True), (r0 + query_block, rows, False)]
                pieces = [piece for piece in pieces if piece[1] > piece[0]]
                qrows = slice(r0, r0 + query_block)
                if not first:
                    m_block = m_in[qrows, :]
                    l_block = l_in[qrows, :]
                if not last:
                    m_keep = m_out[qrows, :]
                    l_keep = l_out[qrows, :]
                for g in range(group):
                    pick = lane == group * head + g
                    cols = slice(g * HEAD_DIM, (g + 1) * HEAD_DIM)
                    query = q_ref[qrows, cols]
                    scores = []
                    for k0, k1, masked in pieces:
                        s = lax.dot_general(
                            query, k_ref[k0:k1, :], (((1,), (1,)), ((), ())),
                            preferred_element_type=jnp.float32,
                        ) * log2_scale
                        if masked:
                            s = jnp.where(diag_allowed, s, masked_score)
                        scores.append(s)
                    block_max = scores[0].max(axis=1, keepdims=True)
                    for s in scores[1:]:
                        block_max = jnp.maximum(block_max, s.max(axis=1, keepdims=True))
                    if first:
                        m_new = block_max
                    else:
                        m_prev = jnp.sum(jnp.where(pick, m_block, 0.0), axis=1, keepdims=True)
                        l_prev = jnp.sum(jnp.where(pick, l_block, 0.0), axis=1, keepdims=True)
                        m_new = jnp.maximum(m_prev, block_max)
                        alpha = jnp.exp2(m_prev - m_new)
                    l_part = None
                    pv = None
                    for (k0, k1, masked), s in zip(pieces, scores):
                        p = jnp.exp2(s - m_new)
                        part = p.sum(axis=1, keepdims=True)
                        l_part = part if l_part is None else l_part + part
                        term = jnp.dot(p.astype(jnp.bfloat16), v_ref[k0:k1, :],
                                       preferred_element_type=jnp.float32)
                        pv = term if pv is None else pv + term
                    if first:
                        l_new = l_part
                        acc_new = pv
                    else:
                        l_new = alpha * l_prev + l_part
                        acc_new = alpha * acc_in[qrows, cols] + pv
                    if last:
                        o_ref[qrows, cols] = (acc_new / l_new).astype(o_ref.dtype)
                    else:
                        acc_out[qrows, cols] = acc_new
                        m_keep = jnp.where(pick, m_new, m_keep)
                        l_keep = jnp.where(pick, l_new, l_keep)
                if not last:
                    m_out[qrows, :] = m_keep
                    l_out[qrows, :] = l_keep

        def passthrough():
            if last:
                all_lanes = lax.broadcasted_iota(jnp.int32, (rows, stat_cols), 1)
                l_all = l_in[...]
                for g in range(group):
                    cols = slice(g * HEAD_DIM, (g + 1) * HEAD_DIM)
                    l_prev = jnp.sum(jnp.where(all_lanes == group * head + g, l_all, 0.0),
                                     axis=1, keepdims=True)
                    o_ref[:, cols] = (acc_in[:, cols] / l_prev).astype(o_ref.dtype)
            else:
                m_out[...] = m_in[...]
                l_out[...] = l_in[...]
                acc_out[...] = acc_in[...]

        if chunk == 2:
            compute()
        else:
            valid = first_row >= (2 - chunk) * rows
            pl.when(valid)(compute)
            pl.when(jnp.logical_not(valid))(passthrough)

    return kernel


def attend_chunk(chunk, queries, key_rows, value_rows, first_row, state):
    rows, key_cols = key_rows.shape
    query_cols = queries.shape[1]
    kv_heads = key_cols // HEAD_DIM
    group = query_cols // key_cols
    heads = kv_heads * group
    first = state is None
    last = chunk == 0
    kernel = chunk_kernel(chunk, first, last, rows, QUERY_BLOCK, group)
    q_spec = pl.BlockSpec((rows, group * HEAD_DIM), lambda h, f: (0, h))
    kv_spec = pl.BlockSpec((rows, HEAD_DIM), lambda h, f: (0, h))
    stat_spec = pl.BlockSpec((rows, heads), lambda h, f: (0, 0))
    state_specs = [stat_spec, stat_spec, q_spec]
    in_specs = [q_spec, kv_spec, kv_spec] + ([] if first else state_specs)
    stat_shape = jax.ShapeDtypeStruct((rows, heads), jnp.float32)
    if last:
        out_specs = q_spec
        out_shape = jax.ShapeDtypeStruct((rows, query_cols), jnp.bfloat16)
    else:
        out_specs = state_specs
        out_shape = [stat_shape, stat_shape, jax.ShapeDtypeStruct((rows, query_cols), jnp.float32)]
    keys_per_row = rows + QUERY_BLOCK // 2 if chunk != 1 else rows
    cost = pl.CostEstimate(
        flops=4 * heads * rows * keys_per_row * HEAD_DIM,
        transcendentals=heads * rows * keys_per_row,
        bytes_accessed=rows * query_cols * (2 + 4 + (0 if first else 4)) + 4 * rows * key_cols,
    )
    grid_spec = pltpu.PrefetchScalarGridSpec(
        num_scalar_prefetch=1,
        grid=(kv_heads,),
        in_specs=in_specs,
        out_specs=out_specs,
    )
    return pl.pallas_call(
        kernel,
        grid_spec=grid_spec,
        out_shape=out_shape,
        cost_estimate=cost,
        compiler_params=pltpu.CompilerParams(dimension_semantics=("arbitrary",)),
    )(first_row.reshape(1), queries, key_rows, value_rows, *([] if first else state))


def swap_variant(half):
    variants = lax.axis_size("variant")
    return lax.ppermute(half, "variant", [(i, (i + 1) % variants) for i in range(variants)])


def halves_in_order(own, other, variant_index):
    return jnp.where(
        variant_index == 0,
        jnp.concatenate([own, other], axis=1),
        jnp.concatenate([other, own], axis=1),
    )


def shard_body(queries, keys, values, clean_keys, clean_values, owner_shard, span_offset, span_length):
    row_count = keys.shape[0]
    assert WINDOW == 2 * row_count
    shard_index = lax.axis_index("seq")
    first_row = (shard_index * row_count).astype(jnp.int32)
    position = lax.broadcasted_iota(jnp.int32, (row_count,), 0)
    inside = jnp.zeros((row_count,), bool)
    for span_index in range(span_offset.shape[1]):
        start = span_offset[0, span_index]
        inside = inside | (
            (position >= start) & (position < start + span_length[0, span_index])
        )
    inside = inside & (owner_shard[0] == shard_index)
    corrupt_pair = jnp.stack([keys, values])
    clean_own = jnp.stack([clean_keys, clean_values])
    if lax.axis_size("variant") != 2:
        clean_full = lax.all_gather(clean_own, "variant", axis=1, tiled=True)
        patched = jnp.where(inside[None, :, None], clean_full, corrupt_pair)
        near = shifted(patched, "seq", 1)
        far = shifted(near, "seq", 1)
    else:
        half = row_count // 2
        variant_index = lax.axis_index("variant")
        lo, hi = corrupt_pair[:, :half], corrupt_pair[:, half:]
        inside_lo, inside_hi = inside[:half], inside[half:]
        corrupt_own = jnp.where(variant_index == 0, lo, hi)
        corrupt_other = jnp.where(variant_index == 0, hi, lo)
        inside_own = jnp.where(variant_index == 0, inside_lo, inside_hi)
        inside_other = jnp.where(variant_index == 0, inside_hi, inside_lo)
        own_half = jnp.where(inside_own[None, :, None], clean_own, corrupt_own)
        own_half, clean_own = lax.optimization_barrier((own_half, clean_own))
        near_own = shifted(own_half, "seq", 1)
        clean_other = swap_variant(clean_own)
        other_half = jnp.where(inside_other[None, :, None], clean_other, corrupt_other)
        near_other = shifted(other_half, "seq", 1)
        far_own = shifted(near_own, "seq", 1)
        far_other = shifted(near_other, "seq", 1)
        patched = halves_in_order(own_half, other_half, variant_index)
        near = halves_in_order(near_own, near_other, variant_index)
        far = halves_in_order(far_own, far_other, variant_index)
    state = attend_chunk(2, queries, patched[0], patched[1], first_row, None)
    state = attend_chunk(1, queries, near[0], near[1], first_row, state)
    result = attend_chunk(0, queries, far[0], far[1], first_row, state)
    return result[None]


def solution(mesh):
    placed = (
        P(("groups", "seq"), "mp"),
        P(("groups", "seq"), "mp"),
        P(("groups", "seq"), "mp"),
        P(("groups", "seq", "variant"), "mp"),
        P(("groups", "seq", "variant"), "mp"),
        P(("groups", "variant")),
        P(("groups", "variant"), None),
        P(("groups", "variant"), None),
    )
    return jax.shard_map(
        shard_body,
        mesh=mesh,
        in_specs=placed,
        out_specs=P("variant", ("groups", "seq"), "mp"),
        check_vma=False,
    )
```

time: 83.3 us -> 79.3 us (0.952)
  the two profiles are of different devices: /device:TPU:0 before, /device:TPU:16 now
where the time goes in v3:
time: 79.3 us; the launch traced here: 78.8 us
  Pallas kernels  32.8 us (41%)
  waiting for transfers between devices  17.6 us (22%)
  starting transfers between devices  14.8 us (19%)
  local copies, waits for them, and re-layouts  5.88 us (7%)
  other arithmetic  4.38 us (6%)
  between operations  3.34 us (4%)
    pallas_call x3, Pallas kernels, attend_chunk(): pl.pallas_call(kernel, grid_spec=grid_spec, out_shape=out_shape, cost_est...  32.8 us
    ppermute x4, starting transfers between devices, shifted(): return lax.ppermute(shard, axis, pairs)  13.3 us
    ppermute x4, waiting for transfers between devices, shifted(): return lax.ppermute(shard, axis, pairs)  8.87 us
    ppermute x1, waiting for transfers between devices, swap_variant(): lax.ppermute(half, 'variant', [(i, (i + 1) % variants) for i in range(var...  8.69 us
  transfers between devices with their start and end apart: 5, of which 2 were waited for; matrix products, arithmetic and copies ran while one was open for 4% of the time, Pallas kernels for 29%

profile of v3, /device:TPU:16, one launch (start us, length us, event | category | flops | bytes accessed | tf_op | source)
XLA Modules:
  0.0 78.8 jit_solution(13443053234500996323)
XLA Ops:
  0.0 0.0 copy-start
  0.0 0.0 copy-start.1
  0.7 1.4 %fusion.6 = (s32[1,1]{1,0:T(1,128)}, s32[1,1]{1,0:T(1,128)}) fusion(s32[1,2]{1,0:T(1,128)} %param.14), kind=kLoop, calls=%fused_computation.27 | loop fusion | bytes 16 | tf_op jit(solution)/shard_map/slice | solution.py:195
  2.1 1.4 %fusion.5 = (s32[1,1]{1,0:T(1,128)}, s32[1,1]{1,0:T(1,128)}) fusion(s32[1,2]{1,0:T(1,128)} %param.15), kind=kLoop, calls=%fused_computation.26 | loop fusion | bytes 16 | tf_op jit(solution)/shard_map/slice | solution.py:197
  6.0 1.3 %fusion.3 = pred[512]{0:T(512)(128)(4,1)S(1)} fusion(s32[]{:T(128)S(6)} %add.7, s32[]{:T(128)} %bitcast.3, s32[]{:T(128)S(6)} %add.6, s32[]{:T(128)} %bitcast.1, pred[]{:T(512)S(6)} %eq.5), kind=kLoop, calls=%fused_computation.22 | loop fusion | flops 4096 | bytes 529 | tf_op jit(solution)/shard_map/and | solution.py:199
  7.3 1.6 %pad_maximum_fusion.1 = (bf16[2,256,512]{2,1,0:T(8,128)(2,1)S(1)}, bf16[2,256,512]{2,1,0:T(8,128)(2,1)S(1)}) fusion(bf16[1,256,512]{2,1,0:T(8,128)(2,1)} %bitcast.28, bf16[1,256,512]{2,1,0:T(8,128)(2,1)} %bitcast.29, bf16[1,512,512]{2,1,0:T(8,128)(2,1)} %bitcast.24, bf16[1,512,512]{2,1,0:T(8,128)(2,1)} %bitcast.26, pred[]{:T(512)S(6)} %eq.4, ...), kind=kLoop, calls=%fused_computation.13 | loop fusion | flops 3670016 | bytes 2621697 | tf_op jit(solution)/shard_map/stack | solution.py:201
  8.9 1.6 %collective-permute-start.2 = (bf16[2,256,512]{2,1,0:T(8,128)(2,1)S(1)}, bf16[2,256,512]{2,1,0:T(8,128)(2,1)S(1)}, u32[]{:S(2)}, u32[]{:S(2)}) collective-permute-start(bf16[2,256,512]{2,1,0:T(8,128)(2,1)S(1)} %get-tuple-element.14), channel_id=1, source_target_pairs={{0,2},{2,0},{1,3},{3,1},{4,6},{6,4},{5,7},{7,5},{8,10},{10,8},{9,1... | collective-permute-start | bytes 1572872 | tf_op jit(solution)/shard_map/ppermute | solution.py:176
  10.4 3.5 %collective-permute-start = (bf16[2,256,512]{2,1,0:T(8,128)(2,1)S(1)}, bf16[2,256,512]{2,1,0:T(8,128)(2,1)S(1)}, u32[]{:S(2)}, u32[]{:S(2)}) collective-permute-start(bf16[2,256,512]{2,1,0:T(8,128)(2,1)S(1)} %get-tuple-element.13), channel_id=1, source_target_pairs={{0,4},{4,8},{8,12},{1,5},{5,9},{9,13},{2,6},{6,10},{10,14},{3,7},{... | collective-permute-start | bytes 1572872 | tf_op jit(solution)/shard_map/ppermute | solution.py:21
  13.9 8.7 %collective-permute-done.2 = bf16[2,256,512]{2,1,0:T(8,128)(2,1)S(1)} collective-permute-done((bf16[2,256,512]{2,1,0:T(8,128)(2,1)S(1)}, bf16[2,256,512]{2,1,0:T(8,128)(2,1)S(1)}, u32[]{:S(2)}, u32[]{:S(2)}) %collective-permute-start.2) | collective-permute-done | bytes 524320 | tf_op jit(solution)/shard_map/ppermute | solution.py:176
  22.6 0.0 copy-done
  22.6 0.0 copy-done.1
  22.6 0.2 select_select_fusion
  22.8 3.5 %collective-permute-start.3 = (bf16[2,256,512]{2,1,0:T(8,128)(2,1)S(1)}, bf16[2,256,512]{2,1,0:T(8,128)(2,1)S(1)}, u32[]{:S(2)}, u32[]{:S(2)}) collective-permute-start(bf16[2,256,512]{2,1,0:T(8,128)(2,1)S(1)} %select_select_fusion), channel_id=1, source_target_pairs={{0,4},{4,8},{8,12},{1,5},{5,9},{9,13},{2,6},{6,10},{10,14},{3,7},{... | collective-permute-start | bytes 1572872 | tf_op jit(solution)/shard_map/ppermute | solution.py:21
  26.3 0.0 collective-permute-done
  26.3 2.8 %collective-permute-start.1 = (bf16[2,256,512]{2,1,0:T(8,128)(2,1)S(1)}, bf16[2,256,512]{2,1,0:T(8,128)(2,1)S(1)}, u32[]{:S(2)}, u32[]{:S(2)}) collective-permute-start(bf16[2,256,512]{2,1,0:T(8,128)(2,1)S(1)} %collective-permute-done), channel_id=1, source_target_pairs={{0,4},{4,8},{8,12},{1,5},{5,9},{9,13},{2,6},{6,10},{10,14},{3,7},{... | collective-permute-start | bytes 1572872 | tf_op jit(solution)/shard_map/ppermute | solution.py:21
  29.2 0.4 maximum_select_fusion.2
  29.6 1.0 %slice_bitcast_fusion = (bf16[512,512]{1,0:T(8,128)(2,1)}, bf16[512,512]{1,0:T(8,128)(2,1)}) fusion(bf16[2,512,512]{2,1,0:T(8,128)(2,1)S(1)} %maximum_select_fusion.2), kind=kLoop, calls=%fused_computation.6 | loop fusion | bytes 2097152 | tf_op jit(solution)/shard_map/squeeze | solution.py:227
  30.7 8.9 %collective-permute-done.3 = bf16[2,256,512]{2,1,0:T(8,128)(2,1)S(1)} collective-permute-done((bf16[2,256,512]{2,1,0:T(8,128)(2,1)S(1)}, bf16[2,256,512]{2,1,0:T(8,128)(2,1)S(1)}, u32[]{:S(2)}, u32[]{:S(2)}) %collective-permute-start.3) | collective-permute-done | bytes 524320 | tf_op jit(solution)/shard_map/ppermute | solution.py:21
  39.5 3.5 %collective-permute-start.4 = (bf16[2,256,512]{2,1,0:T(8,128)(2,1)S(1)}, bf16[2,256,512]{2,1,0:T(8,128)(2,1)S(1)}, u32[]{:S(2)}, u32[]{:S(2)}) collective-permute-start(bf16[2,256,512]{2,1,0:T(8,128)(2,1)S(1)} %collective-permute-done.3), channel_id=1, source_target_pairs={{0,4},{4,8},{8,12},{1,5},{5,9},{9,13},{2,6},{6,10},{10,14},{3,7},{... | collective-permute-start | bytes 1572872 | tf_op jit(solution)/shard_map/ppermute | solution.py:21
  43.0 11.1 %shard_map.82 = (f32[512,8]{1,0:T(8,128)}, f32[512,8]{1,0:T(8,128)}, f32[512,1024]{1,0:T(8,128)}) custom-call(s32[1]{0:T(128)} %bitcast.first_ref, bf16[512,1024]{1,0:T(8,128)(2,1)} %q_ref.5, bf16[512,512]{1,0:T(8,128)(2,1)} %get-tuple-element.22.k_ref, bf16[512,512]{1,0:T(8,128)(2,1)} %get-tuple-element.21.v_ref), custom_call_target="tpu_custom_call" | custom-call | flops 1207959552 | bytes 4194304 | tf_op jit(solution)/shard_map/pallas_call | solution.py:165
  54.1 0.4 maximum_select_fusion.1
  54.5 1.0 %slice_bitcast_fusion.2 = (bf16[512,512]{1,0:T(8,128)(2,1)}, bf16[512,512]{1,0:T(8,128)(2,1)}) fusion(bf16[2,512,512]{2,1,0:T(8,128)(2,1)S(1)} %maximum_select_fusion.1), kind=kLoop, calls=%fused_computation.8 | loop fusion | bytes 2097152 | tf_op jit(solution)/shard_map/squeeze | solution.py:228
  55.6 11.9 %shard_map.83 = (f32[512,8]{1,0:T(8,128)}, f32[512,8]{1,0:T(8,128)}, f32[512,1024]{1,0:T(8,128)}) custom-call(s32[1]{0:T(128)} %bitcast.first_ref, bf16[512,1024]{1,0:T(8,128)(2,1)} %q_ref.5, bf16[512,512]{1,0:T(8,128)(2,1)} %get-tuple-element.24.k_ref, bf16[512,512]{1,0:T(8,128)(2,1)} %get-tuple-element.23.v_ref, f32[512,8]{1,0:T(8,128)} %get-tuple-element.15.rest_0_, ...), custom_call_target="tpu_custom_call" | custom-call | flops 1073741824 | bytes 6291456 | tf_op jit(solution)/shard_map/pallas_call | solution.py:165
  67.5 0.0 collective-permute-done.1
  67.5 0.0 collective-permute-done.4
  67.5 0.4 maximum_select_fusion
  67.9 1.0 %slice_bitcast_fusion.4 = (bf16[512,512]{1,0:T(8,128)(2,1)}, bf16[512,512]{1,0:T(8,128)(2,1)}) fusion(bf16[2,512,512]{2,1,0:T(8,128)(2,1)S(1)} %maximum_select_fusion), kind=kLoop, calls=%fused_computation.10 | loop fusion | bytes 2097152 | tf_op jit(solution)/shard_map/squeeze | solution.py:229
  69.0 9.8 %shard_map.84 = bf16[512,1024]{1,0:T(8,128)(2,1)} custom-call(s32[1]{0:T(128)} %bitcast.first_ref, bf16[512,1024]{1,0:T(8,128)(2,1)} %q_ref.5, bf16[512,512]{1,0:T(8,128)(2,1)} %get-tuple-element.26.k_ref, bf16[512,512]{1,0:T(8,128)(2,1)} %get-tuple-element.25.v_ref, f32[512,8]{1,0:T(8,128)} %get-tuple-element.18.rest_0_, ...), custom_call_target="tpu_custom_call" | custom-call | flops 1207959552 | bytes 6291456 | tf_op jit(solution)/shard_map/pallas_call | solution.py:165
  (1 shorter events, 0.0 us)
Async XLA Ops:
  0.0 22.6 %copy-start = (bf16[512,512]{1,0:T(8,128)(2,1)S(1)}, bf16[512,512]{1,0:T(8,128)(2,1)}, u32[]{:S(2)}) copy-start(bf16[512,512]{1,0:T(8,128)(2,1)} %param.10) | copy-start | bytes 1572868
  0.0 22.6 %copy-start.1 = (bf16[512,512]{1,0:T(8,128)(2,1)S(1)}, bf16[512,512]{1,0:T(8,128)(2,1)}, u32[]{:S(2)}) copy-start(bf16[512,512]{1,0:T(8,128)(2,1)} %param.9) | copy-start | bytes 1572868
  8.9 13.7 %collective-permute-start.2 = (bf16[2,256,512]{2,1,0:T(8,128)(2,1)S(1)}, bf16[2,256,512]{2,1,0:T(8,128)(2,1)S(1)}, u32[]{:S(2)}, u32[]{:S(2)}) collective-permute-start(bf16[2,256,512]{2,1,0:T(8,128)(2,1)S(1)} %get-tuple-element.14), channel_id=1, source_target_pairs={{0,2},{2,0},{1,3},{3,1},{4,6},{6,4},{5,7},{7,5},{8,10},{10,8},{9,1... | collective-permute-start | bytes 1572872 | tf_op jit(solution)/shard_map/ppermute | solution.py:176
  10.4 15.9 %collective-permute-start = (bf16[2,256,512]{2,1,0:T(8,128)(2,1)S(1)}, bf16[2,256,512]{2,1,0:T(8,128)(2,1)S(1)}, u32[]{:S(2)}, u32[]{:S(2)}) collective-permute-start(bf16[2,256,512]{2,1,0:T(8,128)(2,1)S(1)} %get-tuple-element.13), channel_id=1, source_target_pairs={{0,4},{4,8},{8,12},{1,5},{5,9},{9,13},{2,6},{6,10},{10,14},{3,7},{... | collective-permute-start | bytes 1572872 | tf_op jit(solution)/shard_map/ppermute | solution.py:21
  22.8 16.7 %collective-permute-start.3 = (bf16[2,256,512]{2,1,0:T(8,128)(2,1)S(1)}, bf16[2,256,512]{2,1,0:T(8,128)(2,1)S(1)}, u32[]{:S(2)}, u32[]{:S(2)}) collective-permute-start(bf16[2,256,512]{2,1,0:T(8,128)(2,1)S(1)} %select_select_fusion), channel_id=1, source_target_pairs={{0,4},{4,8},{8,12},{1,5},{5,9},{9,13},{2,6},{6,10},{10,14},{3,7},{... | collective-permute-start | bytes 1572872 | tf_op jit(solution)/shard_map/ppermute | solution.py:21
  26.3 41.1 %collective-permute-start.1 = (bf16[2,256,512]{2,1,0:T(8,128)(2,1)S(1)}, bf16[2,256,512]{2,1,0:T(8,128)(2,1)S(1)}, u32[]{:S(2)}, u32[]{:S(2)}) collective-permute-start(bf16[2,256,512]{2,1,0:T(8,128)(2,1)S(1)} %collective-permute-done), channel_id=1, source_target_pairs={{0,4},{4,8},{8,12},{1,5},{5,9},{9,13},{2,6},{6,10},{10,14},{3,7},{... | collective-permute-start | bytes 1572872 | tf_op jit(solution)/shard_map/ppermute | solution.py:21
  39.5 28.0 %collective-permute-start.4 = (bf16[2,256,512]{2,1,0:T(8,128)(2,1)S(1)}, bf16[2,256,512]{2,1,0:T(8,128)(2,1)S(1)}, u32[]{:S(2)}, u32[]{:S(2)}) collective-permute-start(bf16[2,256,512]{2,1,0:T(8,128)(2,1)S(1)} %collective-permute-done.3), channel_id=1, source_target_pairs={{0,4},{4,8},{8,12},{1,5},{5,9},{9,13},{2,6},{6,10},{10,14},{3,7},{... | collective-permute-start | bytes 1572872 | tf_op jit(solution)/shard_map/ppermute | solution.py:21

commit v4 on v3

--- a/solution.py
+++ b/solution.py
@@ -21,7 +21,15 @@
     return lax.ppermute(shard, axis, pairs)
 
 
-def chunk_kernel(chunk, first, last, rows, query_block, group):
+def row_reduce(x, combine, reduce):
+    lanes = 128
+    partial = x[:, :lanes]
+    for start in range(lanes, x.shape[1], lanes):
+        partial = combine(partial, x[:, start:start + lanes])
+    return reduce(partial, axis=1, keepdims=True)
+
+
+def chunk_kernel(chunk, first, last, rows, key_rows, query_block, group):
     blocks = rows // query_block
 
     def kernel(first_ref, q_ref, k_ref, v_ref, *rest):
@@ -46,7 +54,7 @@
                 if chunk == 2:
                     pieces = [(0, r0, False), (r0, r0 + query_block, True)]
                 elif chunk == 1:
-                    pieces = [(0, rows, False)]
+                    pieces = [(0, key_rows, False)]
                 else:
                     pieces = [(r0, r0 + query_block, True), (r0 + query_block, rows, False)]
                 pieces = [piece for piece in pieces if piece[1] > piece[0]]
@@ -70,9 +78,8 @@
                         if masked:
                             s = jnp.where(diag_allowed, s, masked_score)
                         scores.append(s)
-                    block_max = scores[0].max(axis=1, keepdims=True)
-                    for s in scores[1:]:
-                        block_max = jnp.maximum(block_max, s.max(axis=1, keepdims=True))
+                    block_max = row_reduce(jnp.concatenate(scores, axis=1) if len(scores) > 1 else scores[0],
+                                           jnp.maximum, jnp.max)
                     if first:
                         m_new = block_max
                     else:
@@ -84,7 +91,7 @@
                     pv = None
                     for (k0, k1, masked), s in zip(pieces, scores):
                         p = jnp.exp2(s - m_new)
-                        part = p.sum(axis=1, keepdims=True)
+                        part = row_reduce(p, jnp.add, jnp.sum)
                         l_part = part if l_part is None else l_part + part
                         term = jnp.dot(p.astype(jnp.bfloat16), v_ref[k0:k1, :],
                                        preferred_element_type=jnp.float32)
@@ -130,16 +137,16 @@
 
 
 def attend_chunk(chunk, queries, key_rows, value_rows, first_row, state):
-    rows, key_cols = key_rows.shape
-    query_cols = queries.shape[1]
+    key_count, key_cols = key_rows.shape
+    rows, query_cols = queries.shape
     kv_heads = key_cols // HEAD_DIM
     group = query_cols // key_cols
     heads = kv_heads * group
     first = state is None
     last = chunk == 0
-    kernel = chunk_kernel(chunk, first, last, rows, QUERY_BLOCK, group)
+    kernel = chunk_kernel(chunk, first, last, rows, key_count, QUERY_BLOCK, group)
     q_spec = pl.BlockSpec((rows, group * HEAD_DIM), lambda h, f: (0, h))
-    kv_spec = pl.BlockSpec((rows, HEAD_DIM), lambda h, f: (0, h))
+    kv_spec = pl.BlockSpec((key_count, HEAD_DIM), lambda h, f: (0, h))
     stat_spec = pl.BlockSpec((rows, heads), lambda h, f: (0, 0))
     state_specs = [stat_spec, stat_spec, q_spec]
     in_specs = [q_spec, kv_spec, kv_spec] + ([] if first else state_specs)
@@ -150,11 +157,11 @@
     else:
         out_specs = state_specs
         out_shape = [stat_shape, stat_shape, jax.ShapeDtypeStruct((rows, query_cols), jnp.float32)]
-    keys_per_row = rows + QUERY_BLOCK // 2 if chunk != 1 else rows
+    keys_per_row = rows // 2 + QUERY_BLOCK // 2 if chunk != 1 else key_count
     cost = pl.CostEstimate(
         flops=4 * heads * rows * keys_per_row * HEAD_DIM,
         transcendentals=heads * rows * keys_per_row,
-        bytes_accessed=rows * query_cols * (2 + 4 + (0 if first else 4)) + 4 * rows * key_cols,
+        bytes_accessed=rows * query_cols * (2 + 4 + (0 if first else 4)) + 4 * key_count * key_cols,
     )
     grid_spec = pltpu.PrefetchScalarGridSpec(
         num_scalar_prefetch=1,
@@ -204,6 +211,7 @@
         patched = jnp.where(inside[None, :, None], clean_full, corrupt_pair)
         near = shifted(patched, "seq", 1)
         far = shifted(near, "seq", 1)
+        near_parts = (near,)
     else:
         half = row_count // 2
         variant_index = lax.axis_index("variant")
@@ -222,10 +230,11 @@
         far_own = shifted(near_own, "seq", 1)
         far_other = shifted(near_other, "seq", 1)
         patched = halves_in_order(own_half, other_half, variant_index)
-        near = halves_in_order(near_own, near_other, variant_index)
         far = halves_in_order(far_own, far_other, variant_index)
+        near_parts = (near_own, near_other)
     state = attend_chunk(2, queries, patched[0], patched[1], first_row, None)
-    state = attend_chunk(1, queries, near[0], near[1], first_row, state)
+    for part in near_parts:
+        state = attend_chunk(1, queries, part[0], part[1], first_row, state)
     result = attend_chunk(0, queries, far[0], far[1], first_row, state)
     return result[None]
 

time: 79.3 us -> 71.9 us (0.907)
  the two profiles are of different devices: /device:TPU:16 before, /device:TPU:20 now
where the time goes in v4:
time: 71.9 us; the launch traced here: 71.3 us
  Pallas kernels  34.2 us (48%)
  starting transfers between devices  13.3 us (18%)
  waiting for transfers between devices  10.2 us (14%)
  local copies, waits for them, and re-layouts  6.48 us (9%)
  other arithmetic  3.86 us (5%)
  between operations  3.31 us (5%)
    pallas_call x4, Pallas kernels, attend_chunk(): pl.pallas_call(kernel, grid_spec=grid_spec, out_shape=out_shape, cost_est...  34.2 us
    ppermute x4, starting transfers between devices, shifted(): return lax.ppermute(shard, axis, pairs)  11.7 us
    ppermute x1, waiting for transfers between devices, swap_variant(): lax.ppermute(half, 'variant', [(i, (i + 1) % variants) for i in range(var...  8.69 us
    squeeze x2, local copies, waits for them, and re-layouts, shard_body(): state = attend_chunk(1, queries, part[0], part[1], first_row, state)  1.69 us
    another operation x1, other arithmetic, shard_body(): clean_own = jnp.stack([clean_keys, clean_values])  1.57 us
    ppermute x1, starting transfers between devices, swap_variant(): lax.ppermute(half, 'variant', [(i, (i + 1) % variants) for i in range(var...  1.56 us
    ppermute x4, waiting for transfers between devices, shifted(): return lax.ppermute(shard, axis, pairs)  1.52 us
  transfers between devices with their start and end apart: 5, of which 2 were waited for; matrix products, arithmetic and copies ran while one was open for 5% of the time, Pallas kernels for 34%

profile of v4, /device:TPU:20, one launch (start us, length us, event | category | flops | bytes accessed | tf_op | source)
XLA Modules:
  0.0 71.3 jit_solution(6564429131201599172)
XLA Ops:
  0.0 0.0 copy-start.1
  0.0 0.0 copy-start
  0.0 1.3 %fusion.6 = (s32[1,1]{1,0:T(1,128)}, s32[1,1]{1,0:T(1,128)}) fusion(s32[1,2]{1,0:T(1,128)} %param.14), kind=kLoop, calls=%fused_computation.28 | loop fusion | bytes 16 | tf_op jit(solution)/shard_map/slice | solution.py:202
  1.3 1.4 %fusion.5 = (s32[1,1]{1,0:T(1,128)}, s32[1,1]{1,0:T(1,128)}) fusion(s32[1,2]{1,0:T(1,128)} %param.15), kind=kLoop, calls=%fused_computation.27 | loop fusion | bytes 16 | tf_op jit(solution)/shard_map/slice | solution.py:204
  5.9 1.2 %fusion.3 = pred[512]{0:T(512)(128)(4,1)S(1)} fusion(s32[]{:T(128)S(6)} %add.7, s32[]{:T(128)} %bitcast.3, s32[]{:T(128)S(6)} %add.6, s32[]{:T(128)} %bitcast.1, pred[]{:T(512)S(6)} %eq.5), kind=kLoop, calls=%fused_computation.23 | loop fusion | flops 4096 | bytes 529 | tf_op jit(solution)/shard_map/and | solution.py:206
  7.1 1.6 %pad_maximum_fusion.1 = (bf16[2,256,512]{2,1,0:T(8,128)(2,1)S(1)}, bf16[2,256,512]{2,1,0:T(8,128)(2,1)S(1)}) fusion(bf16[1,256,512]{2,1,0:T(8,128)(2,1)} %bitcast.32, bf16[1,256,512]{2,1,0:T(8,128)(2,1)} %bitcast.33, bf16[1,512,512]{2,1,0:T(8,128)(2,1)} %bitcast.28, bf16[1,512,512]{2,1,0:T(8,128)(2,1)} %bitcast.30, pred[]{:T(512)S(6)} %eq.4, ...), kind=kLoop, calls=%fused_computation.10 | loop fusion | flops 3670016 | bytes 2621697 | tf_op jit(solution)/shard_map/stack | solution.py:208
  8.7 1.6 %collective-permute-start.2 = (bf16[2,256,512]{2,1,0:T(8,128)(2,1)S(1)}, bf16[2,256,512]{2,1,0:T(8,128)(2,1)S(1)}, u32[]{:S(2)}, u32[]{:S(2)}) collective-permute-start(bf16[2,256,512]{2,1,0:T(8,128)(2,1)S(1)} %get-tuple-element.17), channel_id=1, source_target_pairs={{0,2},{2,0},{1,3},{3,1},{4,6},{6,4},{5,7},{7,5},{8,10},{10,8},{9,1... | collective-permute-start | bytes 1572872 | tf_op jit(solution)/shard_map/ppermute | solution.py:183
  10.3 3.5 %collective-permute-start = (bf16[2,256,512]{2,1,0:T(8,128)(2,1)S(1)}, bf16[2,256,512]{2,1,0:T(8,128)(2,1)S(1)}, u32[]{:S(2)}, u32[]{:S(2)}) collective-permute-start(bf16[2,256,512]{2,1,0:T(8,128)(2,1)S(1)} %get-tuple-element.16), channel_id=1, source_target_pairs={{0,4},{4,8},{8,12},{1,5},{5,9},{9,13},{2,6},{6,10},{10,14},{3,7},{... | collective-permute-start | bytes 1572872 | tf_op jit(solution)/shard_map/ppermute | solution.py:21
  13.8 8.7 %collective-permute-done.2 = bf16[2,256,512]{2,1,0:T(8,128)(2,1)S(1)} collective-permute-done((bf16[2,256,512]{2,1,0:T(8,128)(2,1)S(1)}, bf16[2,256,512]{2,1,0:T(8,128)(2,1)S(1)}, u32[]{:S(2)}, u32[]{:S(2)}) %collective-permute-start.2) | collective-permute-done | bytes 524320 | tf_op jit(solution)/shard_map/ppermute | solution.py:183
  22.4 0.0 copy-done.1
  22.5 0.0 copy-done
  22.5 0.2 select_select_fusion
  22.7 3.5 %collective-permute-start.3 = (bf16[2,256,512]{2,1,0:T(8,128)(2,1)S(1)}, bf16[2,256,512]{2,1,0:T(8,128)(2,1)S(1)}, u32[]{:S(2)}, u32[]{:S(2)}) collective-permute-start(bf16[2,256,512]{2,1,0:T(8,128)(2,1)S(1)} %select_select_fusion), channel_id=1, source_target_pairs={{0,4},{4,8},{8,12},{1,5},{5,9},{9,13},{2,6},{6,10},{10,14},{3,7},{... | collective-permute-start | bytes 1572872 | tf_op jit(solution)/shard_map/ppermute | solution.py:21
  26.2 0.0 collective-permute-done
  26.2 2.8 %collective-permute-start.1 = (bf16[2,256,512]{2,1,0:T(8,128)(2,1)S(1)}, bf16[2,256,512]{2,1,0:T(8,128)(2,1)S(1)}, u32[]{:S(2)}, u32[]{:S(2)}) collective-permute-start(bf16[2,256,512]{2,1,0:T(8,128)(2,1)S(1)} %collective-permute-done), channel_id=1, source_target_pairs={{0,4},{4,8},{8,12},{1,5},{5,9},{9,13},{2,6},{6,10},{10,14},{3,7},{... | collective-permute-start | bytes 1572872 | tf_op jit(solution)/shard_map/ppermute | solution.py:21
  29.0 0.4 maximum_select_fusion.1
  29.5 1.0 %slice_bitcast_fusion = (bf16[512,512]{1,0:T(8,128)(2,1)}, bf16[512,512]{1,0:T(8,128)(2,1)}) fusion(bf16[2,512,512]{2,1,0:T(8,128)(2,1)S(1)} %maximum_select_fusion.1), kind=kLoop, calls=%fused_computation.5 | loop fusion | bytes 2097152 | tf_op jit(solution)/shard_map/squeeze | solution.py:235
  30.5 11.0 %shard_map.82 = (f32[512,8]{1,0:T(8,128)}, f32[512,8]{1,0:T(8,128)}, f32[512,1024]{1,0:T(8,128)}) custom-call(s32[1]{0:T(128)} %bitcast.first_ref, bf16[512,1024]{1,0:T(8,128)(2,1)} %q_ref.7, bf16[512,512]{1,0:T(8,128)(2,1)} %get-tuple-element.28.k_ref, bf16[512,512]{1,0:T(8,128)(2,1)} %get-tuple-element.27.v_ref), custom_call_target="tpu_custom_call" | custom-call | flops 671088640 | bytes 4194304 | tf_op jit(solution)/shard_map/pallas_call | solution.py:172
  41.5 0.0 collective-permute-done.3
  41.5 1.9 %collective-permute-start.4 = (bf16[2,256,512]{2,1,0:T(8,128)(2,1)S(1)}, bf16[2,256,512]{2,1,0:T(8,128)(2,1)S(1)}, u32[]{:S(2)}, u32[]{:S(2)}) collective-permute-start(bf16[2,256,512]{2,1,0:T(8,128)(2,1)S(1)} %collective-permute-done.3), channel_id=1, source_target_pairs={{0,4},{4,8},{8,12},{1,5},{5,9},{9,13},{2,6},{6,10},{10,14},{3,7},{... | collective-permute-start | bytes 1572872 | tf_op jit(solution)/shard_map/ppermute | solution.py:21
  43.5 0.8 %slice_bitcast_fusion.4 = (bf16[256,512]{1,0:T(8,128)(2,1)}, bf16[256,512]{1,0:T(8,128)(2,1)}) fusion(bf16[2,256,512]{2,1,0:T(8,128)(2,1)S(1)} %collective-permute-done), kind=kLoop, calls=%fused_computation.13 | loop fusion | bytes 1048576 | tf_op jit(solution)/shard_map/squeeze | solution.py:237
  44.3 6.6 %shard_map.83 = (f32[512,8]{1,0:T(8,128)}, f32[512,8]{1,0:T(8,128)}, f32[512,1024]{1,0:T(8,128)}) custom-call(s32[1]{0:T(128)} %bitcast.first_ref, bf16[512,1024]{1,0:T(8,128)(2,1)} %q_ref.7, bf16[256,512]{1,0:T(8,128)(2,1)} %get-tuple-element.32.k_ref, bf16[256,512]{1,0:T(8,128)(2,1)} %get-tuple-element.31.v_ref, f32[512,8]{1,0:T(8,128)} %get-tuple-element.18.rest_0_, ...), custom_call_target="tpu_custom_call" | custom-call | flops 536870912 | bytes 5767168 | tf_op jit(solution)/shard_map/pallas_call | solution.py:172
  50.9 0.8 %slice_bitcast_fusion.6 = (bf16[256,512]{1,0:T(8,128)(2,1)}, bf16[256,512]{1,0:T(8,128)(2,1)}) fusion(bf16[2,256,512]{2,1,0:T(8,128)(2,1)S(1)} %collective-permute-done.3), kind=kLoop, calls=%fused_computation.15 | loop fusion | bytes 1048576 | tf_op jit(solution)/shard_map/squeeze | solution.py:237
  51.8 6.6 %shard_map.84 = (f32[512,8]{1,0:T(8,128)}, f32[512,8]{1,0:T(8,128)}, f32[512,1024]{1,0:T(8,128)}) custom-call(s32[1]{0:T(128)} %bitcast.first_ref, bf16[512,1024]{1,0:T(8,128)(2,1)} %q_ref.7, bf16[256,512]{1,0:T(8,128)(2,1)} %get-tuple-element.34.k_ref, bf16[256,512]{1,0:T(8,128)(2,1)} %get-tuple-element.33.v_ref, f32[512,8]{1,0:T(8,128)} %get-tuple-element.21.rest_0_, ...), custom_call_target="tpu_custom_call" | custom-call | flops 536870912 | bytes 5767168 | tf_op jit(solution)/shard_map/pallas_call | solution.py:172
  58.3 0.0 collective-permute-done.1
  58.3 1.5 %collective-permute-done.4 = bf16[2,256,512]{2,1,0:T(8,128)(2,1)S(1)} collective-permute-done((bf16[2,256,512]{2,1,0:T(8,128)(2,1)S(1)}, bf16[2,256,512]{2,1,0:T(8,128)(2,1)S(1)}, u32[]{:S(2)}, u32[]{:S(2)}) %collective-permute-start.4) | collective-permute-done | bytes 524320 | tf_op jit(solution)/shard_map/ppermute | solution.py:21
  59.8 0.4 maximum_select_fusion
  60.3 1.1 %slice_bitcast_fusion.2 = (bf16[512,512]{1,0:T(8,128)(2,1)}, bf16[512,512]{1,0:T(8,128)(2,1)}) fusion(bf16[2,512,512]{2,1,0:T(8,128)(2,1)S(1)} %maximum_select_fusion), kind=kLoop, calls=%fused_computation.7 | loop fusion | bytes 2097152 | tf_op jit(solution)/shard_map/squeeze | solution.py:238
  61.3 10.0 %shard_map.85 = bf16[512,1024]{1,0:T(8,128)(2,1)} custom-call(s32[1]{0:T(128)} %bitcast.first_ref, bf16[512,1024]{1,0:T(8,128)(2,1)} %q_ref.7, bf16[512,512]{1,0:T(8,128)(2,1)} %get-tuple-element.30.k_ref, bf16[512,512]{1,0:T(8,128)(2,1)} %get-tuple-element.29.v_ref, f32[512,8]{1,0:T(8,128)} %get-tuple-element.24.rest_0_, ...), custom_call_target="tpu_custom_call" | custom-call | flops 671088640 | bytes 6291456 | tf_op jit(solution)/shard_map/pallas_call | solution.py:172
  (1 shorter events, 0.0 us)
Async XLA Ops:
  0.0 22.4 %copy-start.1 = (bf16[512,512]{1,0:T(8,128)(2,1)S(1)}, bf16[512,512]{1,0:T(8,128)(2,1)}, u32[]{:S(2)}) copy-start(bf16[512,512]{1,0:T(8,128)(2,1)} %param.9) | copy-start | bytes 1572868
  0.0 22.4 %copy-start = (bf16[512,512]{1,0:T(8,128)(2,1)S(1)}, bf16[512,512]{1,0:T(8,128)(2,1)}, u32[]{:S(2)}) copy-start(bf16[512,512]{1,0:T(8,128)(2,1)} %param.10) | copy-start | bytes 1572868
  8.7 13.7 %collective-permute-start.2 = (bf16[2,256,512]{2,1,0:T(8,128)(2,1)S(1)}, bf16[2,256,512]{2,1,0:T(8,128)(2,1)S(1)}, u32[]{:S(2)}, u32[]{:S(2)}) collective-permute-start(bf16[2,256,512]{2,1,0:T(8,128)(2,1)S(1)} %get-tuple-element.17), channel_id=1, source_target_pairs={{0,2},{2,0},{1,3},{3,1},{4,6},{6,4},{5,7},{7,5},{8,10},{10,8},{9,1... | collective-permute-start | bytes 1572872 | tf_op jit(solution)/shard_map/ppermute | solution.py:183
  10.3 15.9 %collective-permute-start = (bf16[2,256,512]{2,1,0:T(8,128)(2,1)S(1)}, bf16[2,256,512]{2,1,0:T(8,128)(2,1)S(1)}, u32[]{:S(2)}, u32[]{:S(2)}) collective-permute-start(bf16[2,256,512]{2,1,0:T(8,128)(2,1)S(1)} %get-tuple-element.16), channel_id=1, source_target_pairs={{0,4},{4,8},{8,12},{1,5},{5,9},{9,13},{2,6},{6,10},{10,14},{3,7},{... | collective-permute-start | bytes 1572872 | tf_op jit(solution)/shard_map/ppermute | solution.py:21
  22.7 18.9 %collective-permute-start.3 = (bf16[2,256,512]{2,1,0:T(8,128)(2,1)S(1)}, bf16[2,256,512]{2,1,0:T(8,128)(2,1)S(1)}, u32[]{:S(2)}, u32[]{:S(2)}) collective-permute-start(bf16[2,256,512]{2,1,0:T(8,128)(2,1)S(1)} %select_select_fusion), channel_id=1, source_target_pairs={{0,4},{4,8},{8,12},{1,5},{5,9},{9,13},{2,6},{6,10},{10,14},{3,7},{... | collective-permute-start | bytes 1572872 | tf_op jit(solution)/shard_map/ppermute | solution.py:21
  26.2 32.2 %collective-permute-start.1 = (bf16[2,256,512]{2,1,0:T(8,128)(2,1)S(1)}, bf16[2,256,512]{2,1,0:T(8,128)(2,1)S(1)}, u32[]{:S(2)}, u32[]{:S(2)}) collective-permute-start(bf16[2,256,512]{2,1,0:T(8,128)(2,1)S(1)} %collective-permute-done), channel_id=1, source_target_pairs={{0,4},{4,8},{8,12},{1,5},{5,9},{9,13},{2,6},{6,10},{10,14},{3,7},{... | collective-permute-start | bytes 1572872 | tf_op jit(solution)/shard_map/ppermute | solution.py:21
  41.5 18.3 %collective-permute-start.4 = (bf16[2,256,512]{2,1,0:T(8,128)(2,1)S(1)}, bf16[2,256,512]{2,1,0:T(8,128)(2,1)S(1)}, u32[]{:S(2)}, u32[]{:S(2)}) collective-permute-start(bf16[2,256,512]{2,1,0:T(8,128)(2,1)S(1)} %collective-permute-done.3), channel_id=1, source_target_pairs={{0,4},{4,8},{8,12},{1,5},{5,9},{9,13},{2,6},{6,10},{10,14},{3,7},{... | collective-permute-start | bytes 1572872 | tf_op jit(solution)/shard_map/ppermute | solution.py:21

commit v5 on v4

--- a/solution.py
+++ b/solution.py
@@ -196,14 +196,10 @@
     assert WINDOW == 2 * row_count
     shard_index = lax.axis_index("seq")
     first_row = (shard_index * row_count).astype(jnp.int32)
-    position = lax.broadcasted_iota(jnp.int32, (row_count,), 0)
-    inside = jnp.zeros((row_count,), bool)
-    for span_index in range(span_offset.shape[1]):
-        start = span_offset[0, span_index]
-        inside = inside | (
-            (position >= start) & (position < start + span_length[0, span_index])
-        )
-    inside = inside & (owner_shard[0] == shard_index)
+    position = lax.broadcasted_iota(jnp.int32, (row_count, span_offset.shape[1]), 0)
+    in_span = (position >= span_offset) & (position < span_offset + span_length)
+    in_span = in_span & (owner_shard[:, None] == shard_index)
+    inside = jnp.any(in_span, axis=1)
     corrupt_pair = jnp.stack([keys, values])
     clean_own = jnp.stack([clean_keys, clean_values])
     if lax.axis_size("variant") != 2:

time: 71.9 us -> 66.8 us (0.929)
  the two profiles are of different devices: /device:TPU:20 before, /device:TPU:24 now
where the time goes in v5:
time: 66.8 us; the launch traced here: 66.3 us
  Pallas kernels  34.2 us (51%)
  waiting for transfers between devices  16.8 us (25%)
  starting transfers between devices  6.69 us (10%)
  other arithmetic  4.08 us (6%)
  local copies, waits for them, and re-layouts  3.75 us (6%)
  between operations  0.81 us (1%)
    pallas_call x4, Pallas kernels, attend_chunk(): pl.pallas_call(kernel, grid_spec=grid_spec, out_shape=out_shape, cost_est...  34.2 us
    ppermute x1, waiting for transfers between devices, swap_variant(): lax.ppermute(half, 'variant', [(i, (i + 1) % variants) for i in range(var...  10.9 us
    ppermute x4, waiting for transfers between devices, shifted(): return lax.ppermute(shard, axis, pairs)  5.93 us
    ppermute x4, starting transfers between devices, shifted(): return lax.ppermute(shard, axis, pairs)  5.13 us
    squeeze x2, local copies, waits for them, and re-layouts, shard_body(): state = attend_chunk(1, queries, part[0], part[1], first_row, state)  1.67 us
    another operation x1, other arithmetic, shard_body(): clean_own = jnp.stack([clean_keys, clean_values])  1.56 us
    ppermute x1, starting transfers between devices, swap_variant(): lax.ppermute(half, 'variant', [(i, (i + 1) % variants) for i in range(var...  1.56 us
  transfers between devices with their start and end apart: 5, of which 3 were waited for; matrix products, arithmetic and copies ran while one was open for 5% of the time, Pallas kernels for 37%

profile of v5, /device:TPU:24, one launch (start us, length us, event | category | flops | bytes accessed | tf_op | source)
XLA Modules:
  0.0 66.3 jit_solution(8899393911119606421)
XLA Ops:
  0.0 0.0 copy-start.1
  0.0 0.0 copy-start
  0.7 0.7 %add_bitcast_fusion = s32[2]{0:T(128)S(1)} fusion(s32[1,2]{1,0:T(1,128)} %param.14, s32[1,2]{1,0:T(1,128)} %param.15), kind=kLoop, calls=%fused_computation.20 | loop fusion | flops 2 | bytes 24 | tf_op jit(solution)/shard_map/lt | solution.py:200
  1.4 0.7 %and_reduce_fusion = pred[512]{0:T(512)(128)(4,1)S(1)} fusion(pred[]{:T(512)} %bitcast.5, s32[2]{0:T(128)S(1)} %add_bitcast_fusion, s32[2]{0:T(128)} %bitcast.35), kind=kLoop, calls=%fused_computation.17 | loop fusion | flops 4608 | bytes 529 | tf_op jit(solution)/shard_map/reduce_or | solution.py:202
  2.2 1.6 %pad_maximum_fusion.1 = (bf16[2,256,512]{2,1,0:T(8,128)(2,1)S(1)}, bf16[2,256,512]{2,1,0:T(8,128)(2,1)S(1)}) fusion(bf16[1,256,512]{2,1,0:T(8,128)(2,1)} %bitcast.33, bf16[1,256,512]{2,1,0:T(8,128)(2,1)} %bitcast.34, bf16[1,512,512]{2,1,0:T(8,128)(2,1)} %bitcast.29, bf16[1,512,512]{2,1,0:T(8,128)(2,1)} %bitcast.31, pred[]{:T(512)S(6)} %eq.6, ...), kind=kLoop, calls=%fused_computation.10 | loop fusion | flops 3670016 | bytes 2621697 | tf_op jit(solution)/shard_map/stack | solution.py:204
  3.8 1.6 %collective-permute-start.2 = (bf16[2,256,512]{2,1,0:T(8,128)(2,1)S(1)}, bf16[2,256,512]{2,1,0:T(8,128)(2,1)S(1)}, u32[]{:S(2)}, u32[]{:S(2)}) collective-permute-start(bf16[2,256,512]{2,1,0:T(8,128)(2,1)S(1)} %get-tuple-element.17), channel_id=1, source_target_pairs={{0,2},{2,0},{1,3},{3,1},{4,6},{6,4},{5,7},{7,5},{8,10},{10,8},{9,1... | collective-permute-start | bytes 1572872 | tf_op jit(solution)/shard_map/ppermute | solution.py:183
  5.3 1.3 %collective-permute-start = (bf16[2,256,512]{2,1,0:T(8,128)(2,1)S(1)}, bf16[2,256,512]{2,1,0:T(8,128)(2,1)S(1)}, u32[]{:S(2)}, u32[]{:S(2)}) collective-permute-start(bf16[2,256,512]{2,1,0:T(8,128)(2,1)S(1)} %get-tuple-element.16), channel_id=1, source_target_pairs={{0,4},{4,8},{8,12},{1,5},{5,9},{9,13},{2,6},{6,10},{10,14},{3,7},{... | collective-permute-start | bytes 1572872 | tf_op jit(solution)/shard_map/ppermute | solution.py:21
  6.6 10.9 %collective-permute-done.2 = bf16[2,256,512]{2,1,0:T(8,128)(2,1)S(1)} collective-permute-done((bf16[2,256,512]{2,1,0:T(8,128)(2,1)S(1)}, bf16[2,256,512]{2,1,0:T(8,128)(2,1)S(1)}, u32[]{:S(2)}, u32[]{:S(2)}) %collective-permute-start.2) | collective-permute-done | bytes 524320 | tf_op jit(solution)/shard_map/ppermute | solution.py:183
  17.5 0.0 copy-done.1
  17.5 0.0 copy-done
  17.5 0.2 select_select_fusion
  17.7 1.3 %collective-permute-start.3 = (bf16[2,256,512]{2,1,0:T(8,128)(2,1)S(1)}, bf16[2,256,512]{2,1,0:T(8,128)(2,1)S(1)}, u32[]{:S(2)}, u32[]{:S(2)}) collective-permute-start(bf16[2,256,512]{2,1,0:T(8,128)(2,1)S(1)} %select_select_fusion), channel_id=1, source_target_pairs={{0,4},{4,8},{8,12},{1,5},{5,9},{9,13},{2,6},{6,10},{10,14},{3,7},{... | collective-permute-start | bytes 1572872 | tf_op jit(solution)/shard_map/ppermute | solution.py:21
  19.0 1.6 %collective-permute-done = bf16[2,256,512]{2,1,0:T(8,128)(2,1)S(1)} collective-permute-done((bf16[2,256,512]{2,1,0:T(8,128)(2,1)S(1)}, bf16[2,256,512]{2,1,0:T(8,128)(2,1)S(1)}, u32[]{:S(2)}, u32[]{:S(2)}) %collective-permute-start) | collective-permute-done | bytes 524320 | tf_op jit(solution)/shard_map/ppermute | solution.py:21
  20.6 1.3 %collective-permute-start.1 = (bf16[2,256,512]{2,1,0:T(8,128)(2,1)S(1)}, bf16[2,256,512]{2,1,0:T(8,128)(2,1)S(1)}, u32[]{:S(2)}, u32[]{:S(2)}) collective-permute-start(bf16[2,256,512]{2,1,0:T(8,128)(2,1)S(1)} %collective-permute-done), channel_id=1, source_target_pairs={{0,4},{4,8},{8,12},{1,5},{5,9},{9,13},{2,6},{6,10},{10,14},{3,7},{... | collective-permute-start | bytes 1572872 | tf_op jit(solution)/shard_map/ppermute | solution.py:21
  21.9 0.4 maximum_select_fusion.1
  22.3 1.0 %slice_bitcast_fusion = (bf16[512,512]{1,0:T(8,128)(2,1)}, bf16[512,512]{1,0:T(8,128)(2,1)}) fusion(bf16[2,512,512]{2,1,0:T(8,128)(2,1)S(1)} %maximum_select_fusion.1), kind=kLoop, calls=%fused_computation.5 | loop fusion | bytes 2097152 | tf_op jit(solution)/shard_map/squeeze | solution.py:231
  23.3 11.0 %shard_map.82 = (f32[512,8]{1,0:T(8,128)}, f32[512,8]{1,0:T(8,128)}, f32[512,1024]{1,0:T(8,128)}) custom-call(s32[1]{0:T(128)} %bitcast.first_ref, bf16[512,1024]{1,0:T(8,128)(2,1)} %q_ref.7, bf16[512,512]{1,0:T(8,128)(2,1)} %get-tuple-element.28.k_ref, bf16[512,512]{1,0:T(8,128)(2,1)} %get-tuple-element.27.v_ref), custom_call_target="tpu_custom_call" | custom-call | flops 671088640 | bytes 4194304 | tf_op jit(solution)/shard_map/pallas_call | solution.py:172
  34.4 0.0 collective-permute-done.3
  34.4 1.3 %collective-permute-start.4 = (bf16[2,256,512]{2,1,0:T(8,128)(2,1)S(1)}, bf16[2,256,512]{2,1,0:T(8,128)(2,1)S(1)}, u32[]{:S(2)}, u32[]{:S(2)}) collective-permute-start(bf16[2,256,512]{2,1,0:T(8,128)(2,1)S(1)} %collective-permute-done.3), channel_id=1, source_target_pairs={{0,4},{4,8},{8,12},{1,5},{5,9},{9,13},{2,6},{6,10},{10,14},{3,7},{... | collective-permute-start | bytes 1572872 | tf_op jit(solution)/shard_map/ppermute | solution.py:21
  35.7 0.8 %slice_bitcast_fusion.4 = (bf16[256,512]{1,0:T(8,128)(2,1)}, bf16[256,512]{1,0:T(8,128)(2,1)}) fusion(bf16[2,256,512]{2,1,0:T(8,128)(2,1)S(1)} %collective-permute-done), kind=kLoop, calls=%fused_computation.13 | loop fusion | bytes 1048576 | tf_op jit(solution)/shard_map/squeeze | solution.py:233
  36.5 6.6 %shard_map.83 = (f32[512,8]{1,0:T(8,128)}, f32[512,8]{1,0:T(8,128)}, f32[512,1024]{1,0:T(8,128)}) custom-call(s32[1]{0:T(128)} %bitcast.first_ref, bf16[512,1024]{1,0:T(8,128)(2,1)} %q_ref.7, bf16[256,512]{1,0:T(8,128)(2,1)} %get-tuple-element.32.k_ref, bf16[256,512]{1,0:T(8,128)(2,1)} %get-tuple-element.31.v_ref, f32[512,8]{1,0:T(8,128)} %get-tuple-element.18.rest_0_, ...), custom_call_target="tpu_custom_call" | custom-call | flops 536870912 | bytes 5767168 | tf_op jit(solution)/shard_map/pallas_call | solution.py:172
  43.1 0.8 %slice_bitcast_fusion.6 = (bf16[256,512]{1,0:T(8,128)(2,1)}, bf16[256,512]{1,0:T(8,128)(2,1)}) fusion(bf16[2,256,512]{2,1,0:T(8,128)(2,1)S(1)} %collective-permute-done.3), kind=kLoop, calls=%fused_computation.15 | loop fusion | bytes 1048576 | tf_op jit(solution)/shard_map/squeeze | solution.py:233
  43.9 6.6 %shard_map.84 = (f32[512,8]{1,0:T(8,128)}, f32[512,8]{1,0:T(8,128)}, f32[512,1024]{1,0:T(8,128)}) custom-call(s32[1]{0:T(128)} %bitcast.first_ref, bf16[512,1024]{1,0:T(8,128)(2,1)} %q_ref.7, bf16[256,512]{1,0:T(8,128)(2,1)} %get-tuple-element.34.k_ref, bf16[256,512]{1,0:T(8,128)(2,1)} %get-tuple-element.33.v_ref, f32[512,8]{1,0:T(8,128)} %get-tuple-element.21.rest_0_, ...), custom_call_target="tpu_custom_call" | custom-call | flops 536870912 | bytes 5767168 | tf_op jit(solution)/shard_map/pallas_call | solution.py:172
  50.5 0.0 collective-permute-done.1
  50.5 4.4 %collective-permute-done.4 = bf16[2,256,512]{2,1,0:T(8,128)(2,1)S(1)} collective-permute-done((bf16[2,256,512]{2,1,0:T(8,128)(2,1)S(1)}, bf16[2,256,512]{2,1,0:T(8,128)(2,1)S(1)}, u32[]{:S(2)}, u32[]{:S(2)}) %collective-permute-start.4) | collective-permute-done | bytes 524320 | tf_op jit(solution)/shard_map/ppermute | solution.py:21
  54.9 0.4 maximum_select_fusion
  55.3 1.0 %slice_bitcast_fusion.2 = (bf16[512,512]{1,0:T(8,128)(2,1)}, bf16[512,512]{1,0:T(8,128)(2,1)}) fusion(bf16[2,512,512]{2,1,0:T(8,128)(2,1)S(1)} %maximum_select_fusion), kind=kLoop, calls=%fused_computation.7 | loop fusion | bytes 2097152 | tf_op jit(solution)/shard_map/squeeze | solution.py:234
  56.4 10.0 %shard_map.85 = bf16[512,1024]{1,0:T(8,128)(2,1)} custom-call(s32[1]{0:T(128)} %bitcast.first_ref, bf16[512,1024]{1,0:T(8,128)(2,1)} %q_ref.7, bf16[512,512]{1,0:T(8,128)(2,1)} %get-tuple-element.30.k_ref, bf16[512,512]{1,0:T(8,128)(2,1)} %get-tuple-element.29.v_ref, f32[512,8]{1,0:T(8,128)} %get-tuple-element.24.rest_0_, ...), custom_call_target="tpu_custom_call" | custom-call | flops 671088640 | bytes 6291456 | tf_op jit(solution)/shard_map/pallas_call | solution.py:172
  (1 shorter events, 0.0 us)
Async XLA Ops:
  0.0 17.5 %copy-start.1 = (bf16[512,512]{1,0:T(8,128)(2,1)S(1)}, bf16[512,512]{1,0:T(8,128)(2,1)}, u32[]{:S(2)}) copy-start(bf16[512,512]{1,0:T(8,128)(2,1)} %param.9) | copy-start | bytes 1572868
  0.0 17.5 %copy-start = (bf16[512,512]{1,0:T(8,128)(2,1)S(1)}, bf16[512,512]{1,0:T(8,128)(2,1)}, u32[]{:S(2)}) copy-start(bf16[512,512]{1,0:T(8,128)(2,1)} %param.10) | copy-start | bytes 1572868
  3.8 13.7 %collective-permute-start.2 = (bf16[2,256,512]{2,1,0:T(8,128)(2,1)S(1)}, bf16[2,256,512]{2,1,0:T(8,128)(2,1)S(1)}, u32[]{:S(2)}, u32[]{:S(2)}) collective-permute-start(bf16[2,256,512]{2,1,0:T(8,128)(2,1)S(1)} %get-tuple-element.17), channel_id=1, source_target_pairs={{0,2},{2,0},{1,3},{3,1},{4,6},{6,4},{5,7},{7,5},{8,10},{10,8},{9,1... | collective-permute-start | bytes 1572872 | tf_op jit(solution)/shard_map/ppermute | solution.py:183
  5.3 15.3 %collective-permute-start = (bf16[2,256,512]{2,1,0:T(8,128)(2,1)S(1)}, bf16[2,256,512]{2,1,0:T(8,128)(2,1)S(1)}, u32[]{:S(2)}, u32[]{:S(2)}) collective-permute-start(bf16[2,256,512]{2,1,0:T(8,128)(2,1)S(1)} %get-tuple-element.16), channel_id=1, source_target_pairs={{0,4},{4,8},{8,12},{1,5},{5,9},{9,13},{2,6},{6,10},{10,14},{3,7},{... | collective-permute-start | bytes 1572872 | tf_op jit(solution)/shard_map/ppermute | solution.py:21
  17.7 16.7 %collective-permute-start.3 = (bf16[2,256,512]{2,1,0:T(8,128)(2,1)S(1)}, bf16[2,256,512]{2,1,0:T(8,128)(2,1)S(1)}, u32[]{:S(2)}, u32[]{:S(2)}) collective-permute-start(bf16[2,256,512]{2,1,0:T(8,128)(2,1)S(1)} %select_select_fusion), channel_id=1, source_target_pairs={{0,4},{4,8},{8,12},{1,5},{5,9},{9,13},{2,6},{6,10},{10,14},{3,7},{... | collective-permute-start | bytes 1572872 | tf_op jit(solution)/shard_map/ppermute | solution.py:21
  20.6 29.9 %collective-permute-start.1 = (bf16[2,256,512]{2,1,0:T(8,128)(2,1)S(1)}, bf16[2,256,512]{2,1,0:T(8,128)(2,1)S(1)}, u32[]{:S(2)}, u32[]{:S(2)}) collective-permute-start(bf16[2,256,512]{2,1,0:T(8,128)(2,1)S(1)} %collective-permute-done), channel_id=1, source_target_pairs={{0,4},{4,8},{8,12},{1,5},{5,9},{9,13},{2,6},{6,10},{10,14},{3,7},{... | collective-permute-start | bytes 1572872 | tf_op jit(solution)/shard_map/ppermute | solution.py:21
  34.4 20.5 %collective-permute-start.4 = (bf16[2,256,512]{2,1,0:T(8,128)(2,1)S(1)}, bf16[2,256,512]{2,1,0:T(8,128)(2,1)S(1)}, u32[]{:S(2)}, u32[]{:S(2)}) collective-permute-start(bf16[2,256,512]{2,1,0:T(8,128)(2,1)S(1)} %collective-permute-done.3), channel_id=1, source_target_pairs={{0,4},{4,8},{8,12},{1,5},{5,9},{9,13},{2,6},{6,10},{10,14},{3,7},{... | collective-permute-start | bytes 1572872 | tf_op jit(solution)/shard_map/ppermute | solution.py:21

commit v6 on v5

--- a/solution.py
+++ b/solution.py
@@ -1,3 +1,5 @@
+import functools
+
 import jax
 import jax.numpy as jnp
 from jax import lax
@@ -9,6 +11,7 @@
 HEAD_DIM = 128
 WINDOW = 1024
 QUERY_BLOCK = 128
+MASKED_QUERY_BLOCK = 256
 
 query_scale = 168.0 ** (-0.5)
 log2_scale = query_scale * 1.4426950408889634
@@ -144,7 +147,8 @@
     heads = kv_heads * group
     first = state is None
     last = chunk == 0
-    kernel = chunk_kernel(chunk, first, last, rows, key_count, QUERY_BLOCK, group)
+    query_block = QUERY_BLOCK if chunk == 1 else MASKED_QUERY_BLOCK
+    kernel = chunk_kernel(chunk, first, last, rows, key_count, query_block, group)
     q_spec = pl.BlockSpec((rows, group * HEAD_DIM), lambda h, f: (0, h))
     kv_spec = pl.BlockSpec((key_count, HEAD_DIM), lambda h, f: (0, h))
     stat_spec = pl.BlockSpec((rows, heads), lambda h, f: (0, 0))
@@ -157,7 +161,7 @@
     else:
         out_specs = state_specs
         out_shape = [stat_shape, stat_shape, jax.ShapeDtypeStruct((rows, query_cols), jnp.float32)]
-    keys_per_row = rows // 2 + QUERY_BLOCK // 2 if chunk != 1 else key_count
+    keys_per_row = rows // 2 + query_block // 2 if chunk != 1 else key_count
     cost = pl.CostEstimate(
         flops=4 * heads * rows * keys_per_row * HEAD_DIM,
         transcendentals=heads * rows * keys_per_row,
@@ -176,6 +180,125 @@
         cost_estimate=cost,
         compiler_params=pltpu.CompilerParams(dimension_semantics=("arbitrary",)),
     )(first_row.reshape(1), queries, key_rows, value_rows, *([] if first else state))
+
+
+def far_half_kernel(last, rows, key_rows, query_block, group):
+    blocks = rows // query_block
+
+    def kernel(scalar_ref, q_ref, k_ref, v_ref, m_in, l_in, acc_in, *outs):
+        if last:
+            (o_ref,) = outs
+        else:
+            m_out, l_out, acc_out = outs
+        head = pl.program_id(0)
+        first_row = scalar_ref[0]
+        key_offset = scalar_ref[1]
+        stat_cols = m_in.shape[1]
+        lane = lax.broadcasted_iota(jnp.int32, (query_block, stat_cols), 1)
+        shape = (query_block, key_rows)
+        key_local = key_offset + lax.broadcasted_iota(jnp.int32, shape, 1)
+        query_local = lax.broadcasted_iota(jnp.int32, shape, 0)
+        head_cols = [slice(g * HEAD_DIM, (g + 1) * HEAD_DIM) for g in range(group)]
+        picks = [lane == group * head + g for g in range(group)]
+
+        def block_compute(r0):
+            qrows = slice(r0, r0 + query_block)
+            allowed = key_local > r0 + query_local
+            m_block = m_in[qrows, :]
+            l_block = l_in[qrows, :]
+            if not last:
+                m_keep = m_out[qrows, :]
+                l_keep = l_out[qrows, :]
+            for g, cols in enumerate(head_cols):
+                s = lax.dot_general(
+                    q_ref[qrows, cols], k_ref[...], (((1,), (1,)), ((), ())),
+                    preferred_element_type=jnp.float32,
+                ) * log2_scale
+                s = jnp.where(allowed, s, masked_score)
+                block_max = s.max(axis=1, keepdims=True)
+                m_prev = jnp.sum(jnp.where(picks[g], m_block, 0.0), axis=1, keepdims=True)
+                l_prev = jnp.sum(jnp.where(picks[g], l_block, 0.0), axis=1, keepdims=True)
+                m_new = jnp.maximum(m_prev, block_max)
+                alpha = jnp.exp2(m_prev - m_new)
+                p = jnp.exp2(s - m_new)
+                l_new = alpha * l_prev + p.sum(axis=1, keepdims=True)
+                acc_new = alpha * acc_in[qrows, cols] + jnp.dot(
+                    p.astype(jnp.bfloat16), v_ref[...], preferred_element_type=jnp.float32)
+                if last:
+                    o_ref[qrows, cols] = (acc_new / l_new).astype(o_ref.dtype)
+                else:
+                    acc_out[qrows, cols] = acc_new
+                    m_keep = jnp.where(picks[g], m_new, m_keep)
+                    l_keep = jnp.where(picks[g], l_new, l_keep)
+            if not last:
+                m_out[qrows, :] = m_keep
+                l_out[qrows, :] = l_keep
+
+        def block_pass(r0):
+            qrows = slice(r0, r0 + query_block)
+            m_block = m_in[qrows, :]
+            l_block = l_in[qrows, :]
+            if last:
+                for g, cols in enumerate(head_cols):
+                    l_prev = jnp.sum(jnp.where(picks[g], l_block, 0.0), axis=1, keepdims=True)
+                    o_ref[qrows, cols] = (acc_in[qrows, cols] / l_prev).astype(o_ref.dtype)
+            else:
+                m_keep = m_out[qrows, :]
+                l_keep = l_out[qrows, :]
+                for g, cols in enumerate(head_cols):
+                    m_keep = jnp.where(picks[g], m_block, m_keep)
+                    l_keep = jnp.where(picks[g], l_block, l_keep)
+                    acc_out[qrows, cols] = acc_in[qrows, cols]
+                m_out[qrows, :] = m_keep
+                l_out[qrows, :] = l_keep
+
+        valid_chunk = first_row >= 2 * rows
+        for block in range(blocks):
+            r0 = block * query_block
+            useful = valid_chunk & (key_offset + key_rows - 1 > r0)
+            pl.when(useful)(functools.partial(block_compute, r0))
+            pl.when(jnp.logical_not(useful))(functools.partial(block_pass, r0))
+
+    return kernel
+
+
+def attend_far_half(queries, key_rows, value_rows, first_row, key_offset, state, last):
+    key_count, key_cols = key_rows.shape
+    rows, query_cols = queries.shape
+    kv_heads = key_cols // HEAD_DIM
+    group = query_cols // key_cols
+    heads = kv_heads * group
+    kernel = far_half_kernel(last, rows, key_count, MASKED_QUERY_BLOCK, group)
+    q_spec = pl.BlockSpec((rows, group * HEAD_DIM), lambda h, f: (0, h))
+    kv_spec = pl.BlockSpec((key_count, HEAD_DIM), lambda h, f: (0, h))
+    stat_spec = pl.BlockSpec((rows, heads), lambda h, f: (0, 0))
+    state_specs = [stat_spec, stat_spec, q_spec]
+    stat_shape = jax.ShapeDtypeStruct((rows, heads), jnp.float32)
+    if last:
+        out_specs = q_spec
+        out_shape = jax.ShapeDtypeStruct((rows, query_cols), jnp.bfloat16)
+    else:
+        out_specs = state_specs
+        out_shape = [stat_shape, stat_shape, jax.ShapeDtypeStruct((rows, query_cols), jnp.float32)]
+    cost = pl.CostEstimate(
+        flops=4 * heads * rows * key_count * HEAD_DIM,
+        transcendentals=heads * rows * key_count,
+        bytes_accessed=rows * query_cols * (2 + 4 + 4) + 4 * key_count * key_cols,
+    )
+    grid_spec = pltpu.PrefetchScalarGridSpec(
+        num_scalar_prefetch=1,
+        grid=(kv_heads,),
+        in_specs=[q_spec, kv_spec, kv_spec] + state_specs,
+        out_specs=out_specs,
+    )
+    scalars = jnp.stack([first_row, key_offset]).astype(jnp.int32)
+    return pl.pallas_call(
+        kernel,
+        grid_spec=grid_spec,
+        out_shape=out_shape,
+        cost_estimate=cost,
+        compiler_params=pltpu.CompilerParams(dimension_semantics=("arbitrary",)),
+    )(scalars, queries, key_rows, value_rows, *state)
 
 
 def swap_variant(half):
@@ -208,6 +331,7 @@
         near = shifted(patched, "seq", 1)
         far = shifted(near, "seq", 1)
         near_parts = (near,)
+        far_parts = None
     else:
         half = row_count // 2
         variant_index = lax.axis_index("variant")
@@ -226,12 +350,18 @@
         far_own = shifted(near_own, "seq", 1)
         far_other = shifted(near_other, "seq", 1)
         patched = halves_in_order(own_half, other_half, variant_index)
-        far = halves_in_order(far_own, far_other, variant_index)
         near_parts = (near_own, near_other)
+        far_parts = ((far_own, half * variant_index), (far_other, half * (1 - variant_index)))
     state = attend_chunk(2, queries, patched[0], patched[1], first_row, None)
     for part in near_parts:
         state = attend_chunk(1, queries, part[0], part[1], first_row, state)
-    result = attend_chunk(0, queries, far[0], far[1], first_row, state)
+    if far_parts is None:
+        result = attend_chunk(0, queries, far[0], far[1], first_row, state)
+    else:
+        for part_index, (part, offset) in enumerate(far_parts):
+            state = attend_far_half(queries, part[0], part[1], first_row, offset, state,
+                                    part_index == len(far_parts) - 1)
+        result = state
     return result[None]
 
 

time: 66.8 us -> 66.9 us (level)
  the two profiles are of different devices: /device:TPU:24 before, /device:TPU:16 now
where the time goes in v6:
time: 66.9 us; the launch traced here: 66.3 us
  Pallas kernels  35.9 us (54%)
  starting transfers between devices  12.8 us (19%)
  waiting for transfers between devices  7.44 us (11%)
  other arithmetic  4.9 us (7%)
  local copies, waits for them, and re-layouts  4.41 us (7%)
  between operations  0.83 us (1%)
    pallas_call x3, Pallas kernels, attend_chunk(): pl.pallas_call(kernel, grid_spec=grid_spec, out_shape=out_shape, cost_est...  20.5 us
    pallas_call x2, Pallas kernels, attend_far_half(): pl.pallas_call(kernel, grid_spec=grid_spec, out_shape=out_shape, cost_est...  15.3 us
    ppermute x4, starting transfers between devices, shifted(): return lax.ppermute(shard, axis, pairs)  11.3 us
    ppermute x1, waiting for transfers between devices, swap_variant(): lax.ppermute(half, 'variant', [(i, (i + 1) % variants) for i in range(var...  7.43 us
    squeeze x2, local copies, waits for them, and re-layouts, shard_body(): state = attend_chunk(1, queries, part[0], part[1], first_row, state)  1.68 us
    squeeze x2, local copies, waits for them, and re-layouts, shard_body(): part[1]  1.67 us
    another operation x1, other arithmetic, shard_body(): clean_own = jnp.stack([clean_keys, clean_values])  1.56 us
    ppermute x1, starting transfers between devices, swap_variant(): lax.ppermute(half, 'variant', [(i, (i + 1) % variants) for i in range(var...  1.56 us
  transfers between devices with their start and end apart: 5, of which 1 were waited for; matrix products, arithmetic and copies ran while one was open for 8% of the time, Pallas kernels for 41%

profile of v6, /device:TPU:16, one launch (start us, length us, event | category | flops | bytes accessed | tf_op | source)
XLA Modules:
  0.0 66.3 jit_solution(12794957386497000281)
XLA Ops:
  0.0 0.0 copy-start
  0.0 0.0 copy-start.1
  0.7 0.7 %add_bitcast_fusion = s32[2]{0:T(128)S(1)} fusion(s32[1,2]{1,0:T(1,128)} %param.14, s32[1,2]{1,0:T(1,128)} %param.15), kind=kLoop, calls=%fused_computation.23 | loop fusion | flops 2 | bytes 24 | tf_op jit(solution)/shard_map/lt | solution.py:323
  1.4 0.7 %and_reduce_fusion = pred[512]{0:T(512)(128)(4,1)S(1)} fusion(pred[]{:T(512)} %bitcast.6, s32[2]{0:T(128)S(1)} %add_bitcast_fusion, s32[2]{0:T(128)} %bitcast.41), kind=kLoop, calls=%fused_computation.18 | loop fusion | flops 4608 | bytes 529 | tf_op jit(solution)/shard_map/reduce_or | solution.py:325
  2.2 1.6 %pad_maximum_fusion.1 = (bf16[2,256,512]{2,1,0:T(8,128)(2,1)S(1)}, bf16[2,256,512]{2,1,0:T(8,128)(2,1)S(1)}) fusion(bf16[1,256,512]{2,1,0:T(8,128)(2,1)} %bitcast.39, bf16[1,256,512]{2,1,0:T(8,128)(2,1)} %bitcast.40, bf16[1,512,512]{2,1,0:T(8,128)(2,1)} %bitcast.35, bf16[1,512,512]{2,1,0:T(8,128)(2,1)} %bitcast.37, pred[]{:T(512)S(6)} %eq.6, ...), kind=kLoop, calls=%fused_computation.7 | loop fusion | flops 3670016 | bytes 2621697 | tf_op jit(solution)/shard_map/stack | solution.py:327
  3.8 1.6 %collective-permute-start = (bf16[2,256,512]{2,1,0:T(8,128)(2,1)S(1)}, bf16[2,256,512]{2,1,0:T(8,128)(2,1)S(1)}, u32[]{:S(2)}, u32[]{:S(2)}) collective-permute-start(bf16[2,256,512]{2,1,0:T(8,128)(2,1)S(1)} %get-tuple-element.19), channel_id=1, source_target_pairs={{0,2},{2,0},{1,3},{3,1},{4,6},{6,4},{5,7},{7,5},{8,10},{10,8},{9,1... | collective-permute-start | bytes 1572872 | tf_op jit(solution)/shard_map/ppermute | solution.py:306
  5.3 3.5 %collective-permute-start.3 = (bf16[2,256,512]{2,1,0:T(8,128)(2,1)S(1)}, bf16[2,256,512]{2,1,0:T(8,128)(2,1)S(1)}, u32[]{:S(2)}, u32[]{:S(2)}) collective-permute-start(bf16[2,256,512]{2,1,0:T(8,128)(2,1)S(1)} %get-tuple-element.20), channel_id=1, source_target_pairs={{0,4},{4,8},{8,12},{1,5},{5,9},{9,13},{2,6},{6,10},{10,14},{3,7},{... | collective-permute-start | bytes 1572872 | tf_op jit(solution)/shard_map/ppermute | solution.py:24
  8.8 0.6 pad_add_fusion.1.scalar_ref
  9.4 0.7 %pad_add_fusion.scalar_ref = s32[2]{0:T(128)} fusion(s32[1]{0:T(128)} %bitcast.1, s32[1]{0:T(128)} %bitcast.first_ref), kind=kLoop, calls=%fused_computation.21 | loop fusion | flops 2 | bytes 16 | tf_op jit(solution)/shard_map/stack | solution.py:294
  10.0 7.4 %collective-permute-done = bf16[2,256,512]{2,1,0:T(8,128)(2,1)S(1)} collective-permute-done((bf16[2,256,512]{2,1,0:T(8,128)(2,1)S(1)}, bf16[2,256,512]{2,1,0:T(8,128)(2,1)S(1)}, u32[]{:S(2)}, u32[]{:S(2)}) %collective-permute-start) | collective-permute-done | bytes 524320 | tf_op jit(solution)/shard_map/ppermute | solution.py:306
  17.5 0.0 copy-done
  17.5 0.0 copy-done.1
  17.5 0.2 select_select_fusion
  17.7 3.5 %collective-permute-start.1 = (bf16[2,256,512]{2,1,0:T(8,128)(2,1)S(1)}, bf16[2,256,512]{2,1,0:T(8,128)(2,1)S(1)}, u32[]{:S(2)}, u32[]{:S(2)}) collective-permute-start(bf16[2,256,512]{2,1,0:T(8,128)(2,1)S(1)} %select_select_fusion), channel_id=1, source_target_pairs={{0,4},{4,8},{8,12},{1,5},{5,9},{9,13},{2,6},{6,10},{10,14},{3,7},{... | collective-permute-start | bytes 1572872 | tf_op jit(solution)/shard_map/ppermute | solution.py:24
  21.2 0.4 maximum_select_fusion
  21.6 0.0 collective-permute-done.3
  21.6 2.4 %collective-permute-start.4 = (bf16[2,256,512]{2,1,0:T(8,128)(2,1)S(1)}, bf16[2,256,512]{2,1,0:T(8,128)(2,1)S(1)}, u32[]{:S(2)}, u32[]{:S(2)}) collective-permute-start(bf16[2,256,512]{2,1,0:T(8,128)(2,1)S(1)} %collective-permute-done.3), channel_id=1, source_target_pairs={{0,4},{4,8},{8,12},{1,5},{5,9},{9,13},{2,6},{6,10},{10,14},{3,7},{... | collective-permute-start | bytes 1572872 | tf_op jit(solution)/shard_map/ppermute | solution.py:24
  24.1 1.0 %slice_bitcast_fusion = (bf16[512,512]{1,0:T(8,128)(2,1)}, bf16[512,512]{1,0:T(8,128)(2,1)}) fusion(bf16[2,512,512]{2,1,0:T(8,128)(2,1)S(1)} %maximum_select_fusion), kind=kLoop, calls=%fused_computation.4 | loop fusion | bytes 2097152 | tf_op jit(solution)/shard_map/squeeze | solution.py:355
  25.1 7.4 %shard_map.82 = (f32[512,8]{1,0:T(8,128)}, f32[512,8]{1,0:T(8,128)}, f32[512,1024]{1,0:T(8,128)}) custom-call(s32[1]{0:T(128)} %bitcast.first_ref, bf16[512,1024]{1,0:T(8,128)(2,1)} %q_ref.9, bf16[512,512]{1,0:T(8,128)(2,1)} %get-tuple-element.34.k_ref, bf16[512,512]{1,0:T(8,128)(2,1)} %get-tuple-element.33.v_ref), custom_call_target="tpu_custom_call" | custom-call | flops 805306368 | bytes 4194304 | tf_op jit(solution)/shard_map/pallas_call | solution.py:176
  32.5 0.8 %slice_bitcast_fusion.2 = (bf16[256,512]{1,0:T(8,128)(2,1)}, bf16[256,512]{1,0:T(8,128)(2,1)}) fusion(bf16[2,256,512]{2,1,0:T(8,128)(2,1)S(1)} %collective-permute-done.3), kind=kLoop, calls=%fused_computation.10 | loop fusion | bytes 1048576 | tf_op jit(solution)/shard_map/squeeze | solution.py:357
  33.3 6.6 %shard_map.83 = (f32[512,8]{1,0:T(8,128)}, f32[512,8]{1,0:T(8,128)}, f32[512,1024]{1,0:T(8,128)}) custom-call(s32[1]{0:T(128)} %bitcast.first_ref, bf16[512,1024]{1,0:T(8,128)(2,1)} %q_ref.9, bf16[256,512]{1,0:T(8,128)(2,1)} %get-tuple-element.36.k_ref, bf16[256,512]{1,0:T(8,128)(2,1)} %get-tuple-element.35.v_ref, f32[512,8]{1,0:T(8,128)} %get-tuple-element.21.rest_0_, ...), custom_call_target="tpu_custom_call" | custom-call | flops 536870912 | bytes 5767168 | tf_op jit(solution)/shard_map/pallas_call | solution.py:176
  39.9 0.0 collective-permute-done.1
  39.9 1.9 %collective-permute-start.2 = (bf16[2,256,512]{2,1,0:T(8,128)(2,1)S(1)}, bf16[2,256,512]{2,1,0:T(8,128)(2,1)S(1)}, u32[]{:S(2)}, u32[]{:S(2)}) collective-permute-start(bf16[2,256,512]{2,1,0:T(8,128)(2,1)S(1)} %collective-permute-done.1), channel_id=1, source_target_pairs={{0,4},{4,8},{8,12},{1,5},{5,9},{9,13},{2,6},{6,10},{10,14},{3,7},{... | collective-permute-start | bytes 1572872 | tf_op jit(solution)/shard_map/ppermute | solution.py:24
  41.8 0.8 %slice_bitcast_fusion.4 = (bf16[256,512]{1,0:T(8,128)(2,1)}, bf16[256,512]{1,0:T(8,128)(2,1)}) fusion(bf16[2,256,512]{2,1,0:T(8,128)(2,1)S(1)} %collective-permute-done.1), kind=kLoop, calls=%fused_computation.12 | loop fusion | bytes 1048576 | tf_op jit(solution)/shard_map/squeeze | solution.py:357
  42.7 6.6 %shard_map.84 = (f32[512,8]{1,0:T(8,128)}, f32[512,8]{1,0:T(8,128)}, f32[512,1024]{1,0:T(8,128)}) custom-call(s32[1]{0:T(128)} %bitcast.first_ref, bf16[512,1024]{1,0:T(8,128)(2,1)} %q_ref.9, bf16[256,512]{1,0:T(8,128)(2,1)} %get-tuple-element.38.k_ref, bf16[256,512]{1,0:T(8,128)(2,1)} %get-tuple-element.37.v_ref, f32[512,8]{1,0:T(8,128)} %get-tuple-element.24.rest_0_, ...), custom_call_target="tpu_custom_call" | custom-call | flops 536870912 | bytes 5767168 | tf_op jit(solution)/shard_map/pallas_call | solution.py:176
  49.3 0.0 collective-permute-done.4
  49.3 0.8 %slice_bitcast_fusion.6 = (bf16[256,512]{1,0:T(8,128)(2,1)}, bf16[256,512]{1,0:T(8,128)(2,1)}) fusion(bf16[2,256,512]{2,1,0:T(8,128)(2,1)S(1)} %collective-permute-done.4), kind=kLoop, calls=%fused_computation.14 | loop fusion | bytes 1048576 | tf_op jit(solution)/shard_map/squeeze | solution.py:362
  50.1 6.8 %shard_map.85 = (f32[512,8]{1,0:T(8,128)}, f32[512,8]{1,0:T(8,128)}, f32[512,1024]{1,0:T(8,128)}) custom-call(s32[2]{0:T(128)} %pad_add_fusion.1.scalar_ref, bf16[512,1024]{1,0:T(8,128)(2,1)} %q_ref.9, bf16[256,512]{1,0:T(8,128)(2,1)} %get-tuple-element.40.k_ref, bf16[256,512]{1,0:T(8,128)(2,1)} %get-tuple-element.39.v_ref, ...), custom_call_target="tpu_custom_call" | custom-call | flops 536870912 | bytes 5767168 | tf_op jit(solution)/shard_map/pallas_call | solution.py:295
  56.9 0.0 collective-permute-done.2
  56.9 0.8 %slice_bitcast_fusion.8 = (bf16[256,512]{1,0:T(8,128)(2,1)}, bf16[256,512]{1,0:T(8,128)(2,1)}) fusion(bf16[2,256,512]{2,1,0:T(8,128)(2,1)S(1)} %collective-permute-done.2), kind=kLoop, calls=%fused_computation.16 | loop fusion | bytes 1048576 | tf_op jit(solution)/shard_map/squeeze | solution.py:362
  57.8 8.5 %shard_map.86 = bf16[512,1024]{1,0:T(8,128)(2,1)} custom-call(s32[2]{0:T(128)} %pad_add_fusion.scalar_ref, bf16[512,1024]{1,0:T(8,128)(2,1)} %q_ref.9, bf16[256,512]{1,0:T(8,128)(2,1)} %get-tuple-element.42.k_ref, bf16[256,512]{1,0:T(8,128)(2,1)} %get-tuple-element.41.v_ref, f32[512,8]{1,0:T(8,128)} %get-tuple-element.30.m_in, ...), custom_call_target="tpu_custom_call" | custom-call | flops 536870912 | bytes 5767168 | tf_op jit(solution)/shard_map/pallas_call | solution.py:295
  (1 shorter events, 0.0 us)
Async XLA Ops:
  0.0 17.5 %copy-start = (bf16[512,512]{1,0:T(8,128)(2,1)S(1)}, bf16[512,512]{1,0:T(8,128)(2,1)}, u32[]{:S(2)}) copy-start(bf16[512,512]{1,0:T(8,128)(2,1)} %param.10) | copy-start | bytes 1572868
  0.0 17.5 %copy-start.1 = (bf16[512,512]{1,0:T(8,128)(2,1)S(1)}, bf16[512,512]{1,0:T(8,128)(2,1)}, u32[]{:S(2)}) copy-start(bf16[512,512]{1,0:T(8,128)(2,1)} %param.9) | copy-start | bytes 1572868
  3.8 13.7 %collective-permute-start = (bf16[2,256,512]{2,1,0:T(8,128)(2,1)S(1)}, bf16[2,256,512]{2,1,0:T(8,128)(2,1)S(1)}, u32[]{:S(2)}, u32[]{:S(2)}) collective-permute-start(bf16[2,256,512]{2,1,0:T(8,128)(2,1)S(1)} %get-tuple-element.19), channel_id=1, source_target_pairs={{0,2},{2,0},{1,3},{3,1},{4,6},{6,4},{5,7},{7,5},{8,10},{10,8},{9,1... | collective-permute-start | bytes 1572872 | tf_op jit(solution)/shard_map/ppermute | solution.py:306
  5.3 16.3 %collective-permute-start.3 = (bf16[2,256,512]{2,1,0:T(8,128)(2,1)S(1)}, bf16[2,256,512]{2,1,0:T(8,128)(2,1)S(1)}, u32[]{:S(2)}, u32[]{:S(2)}) collective-permute-start(bf16[2,256,512]{2,1,0:T(8,128)(2,1)S(1)} %get-tuple-element.20), channel_id=1, source_target_pairs={{0,4},{4,8},{8,12},{1,5},{5,9},{9,13},{2,6},{6,10},{10,14},{3,7},{... | collective-permute-start | bytes 1572872 | tf_op jit(solution)/shard_map/ppermute | solution.py:24
  17.7 22.2 %collective-permute-start.1 = (bf16[2,256,512]{2,1,0:T(8,128)(2,1)S(1)}, bf16[2,256,512]{2,1,0:T(8,128)(2,1)S(1)}, u32[]{:S(2)}, u32[]{:S(2)}) collective-permute-start(bf16[2,256,512]{2,1,0:T(8,128)(2,1)S(1)} %select_select_fusion), channel_id=1, source_target_pairs={{0,4},{4,8},{8,12},{1,5},{5,9},{9,13},{2,6},{6,10},{10,14},{3,7},{... | collective-permute-start | bytes 1572872 | tf_op jit(solution)/shard_map/ppermute | solution.py:24
  21.6 27.6 %collective-permute-start.4 = (bf16[2,256,512]{2,1,0:T(8,128)(2,1)S(1)}, bf16[2,256,512]{2,1,0:T(8,128)(2,1)S(1)}, u32[]{:S(2)}, u32[]{:S(2)}) collective-permute-start(bf16[2,256,512]{2,1,0:T(8,128)(2,1)S(1)} %collective-permute-done.3), channel_id=1, source_target_pairs={{0,4},{4,8},{8,12},{1,5},{5,9},{9,13},{2,6},{6,10},{10,14},{3,7},{... | collective-permute-start | bytes 1572872 | tf_op jit(solution)/shard_map/ppermute | solution.py:24
  39.9 17.0 %collective-permute-start.2 = (bf16[2,256,512]{2,1,0:T(8,128)(2,1)S(1)}, bf16[2,256,512]{2,1,0:T(8,128)(2,1)S(1)}, u32[]{:S(2)}, u32[]{:S(2)}) collective-permute-start(bf16[2,256,512]{2,1,0:T(8,128)(2,1)S(1)} %collective-permute-done.1), channel_id=1, source_target_pairs={{0,4},{4,8},{8,12},{1,5},{5,9},{9,13},{2,6},{6,10},{10,14},{3,7},{... | collective-permute-start | bytes 1572872 | tf_op jit(solution)/shard_map/ppermute | solution.py:24

commit v7 on v5

--- a/solution.py
+++ b/solution.py
@@ -8,7 +8,8 @@
 
 HEAD_DIM = 128
 WINDOW = 1024
-QUERY_BLOCK = 128
+QUERY_BLOCK = 512
+MASKED_QUERY_BLOCK = 512
 
 query_scale = 168.0 ** (-0.5)
 log2_scale = query_scale * 1.4426950408889634
@@ -144,7 +145,8 @@
     heads = kv_heads * group
     first = state is None
     last = chunk == 0
-    kernel = chunk_kernel(chunk, first, last, rows, key_count, QUERY_BLOCK, group)
+    query_block = QUERY_BLOCK if chunk == 1 else MASKED_QUERY_BLOCK
+    kernel = chunk_kernel(chunk, first, last, rows, key_count, query_block, group)
     q_spec = pl.BlockSpec((rows, group * HEAD_DIM), lambda h, f: (0, h))
     kv_spec = pl.BlockSpec((key_count, HEAD_DIM), lambda h, f: (0, h))
     stat_spec = pl.BlockSpec((rows, heads), lambda h, f: (0, 0))
@@ -157,7 +159,7 @@
     else:
         out_specs = state_specs
         out_shape = [stat_shape, stat_shape, jax.ShapeDtypeStruct((rows, query_cols), jnp.float32)]
-    keys_per_row = rows // 2 + QUERY_BLOCK // 2 if chunk != 1 else key_count
+    keys_per_row = rows // 2 + query_block // 2 if chunk != 1 else key_count
     cost = pl.CostEstimate(
         flops=4 * heads * rows * keys_per_row * HEAD_DIM,
         transcendentals=heads * rows * keys_per_row,

time: 66.8 us -> 63.5 us (0.951)
  the two profiles are of different devices: /device:TPU:24 before, /device:TPU:22 now
where the time goes in v7:
time: 63.5 us; the launch traced here: 62.9 us
  Pallas kernels  24.9 us (39%)
  waiting for transfers between devices  16.4 us (26%)
  starting transfers between devices  13 us (20%)
  other arithmetic  4.08 us (6%)
  local copies, waits for them, and re-layouts  3.75 us (6%)
  between operations  0.82 us (1%)
    pallas_call x4, Pallas kernels, attend_chunk(): pl.pallas_call(kernel, grid_spec=grid_spec, out_shape=out_shape, cost_est...  24.9 us
    ppermute x4, starting transfers between devices, shifted(): return lax.ppermute(shard, axis, pairs)  12.4 us
    ppermute x1, waiting for transfers between devices, swap_variant(): lax.ppermute(half, 'variant', [(i, (i + 1) % variants) for i in range(var...  9.65 us
    ppermute x4, waiting for transfers between devices, shifted(): return lax.ppermute(shard, axis, pairs)  6.79 us
    squeeze x2, local copies, waits for them, and re-layouts, shard_body(): state = attend_chunk(1, queries, part[0], part[1], first_row, state)  1.67 us
    another operation x1, other arithmetic, shard_body(): clean_own = jnp.stack([clean_keys, clean_values])  1.56 us
  transfers between devices with their start and end apart: 5, of which 3 were waited for; matrix products, arithmetic and copies ran while one was open for 5% of the time, Pallas kernels for 29%

profile of v7, /device:TPU:22, one launch (start us, length us, event | category | flops | bytes accessed | tf_op | source)
XLA Modules:
  0.0 62.9 jit_solution(14579013632838158257)
XLA Ops:
  0.0 0.0 copy-start.1
  0.0 0.0 copy-start
  0.7 0.7 %add_bitcast_fusion = s32[2]{0:T(128)S(1)} fusion(s32[1,2]{1,0:T(1,128)} %param.14, s32[1,2]{1,0:T(1,128)} %param.15), kind=kLoop, calls=%fused_computation.20 | loop fusion | flops 2 | bytes 24 | tf_op jit(solution)/shard_map/lt | solution.py:202
  1.4 0.7 %and_reduce_fusion = pred[512]{0:T(512)(128)(4,1)S(1)} fusion(pred[]{:T(512)} %bitcast.5, s32[2]{0:T(128)S(1)} %add_bitcast_fusion, s32[2]{0:T(128)} %bitcast.35), kind=kLoop, calls=%fused_computation.17 | loop fusion | flops 4608 | bytes 529 | tf_op jit(solution)/shard_map/reduce_or | solution.py:204
  2.2 1.6 %pad_maximum_fusion.1 = (bf16[2,256,512]{2,1,0:T(8,128)(2,1)S(1)}, bf16[2,256,512]{2,1,0:T(8,128)(2,1)S(1)}) fusion(bf16[1,256,512]{2,1,0:T(8,128)(2,1)} %bitcast.33, bf16[1,256,512]{2,1,0:T(8,128)(2,1)} %bitcast.34, bf16[1,512,512]{2,1,0:T(8,128)(2,1)} %bitcast.29, bf16[1,512,512]{2,1,0:T(8,128)(2,1)} %bitcast.31, pred[]{:T(512)S(6)} %eq.6, ...), kind=kLoop, calls=%fused_computation.10 | loop fusion | flops 3670016 | bytes 2621697 | tf_op jit(solution)/shard_map/stack | solution.py:206
  3.8 0.6 collective-permute-start.2
  4.4 3.5 %collective-permute-start = (bf16[2,256,512]{2,1,0:T(8,128)(2,1)S(1)}, bf16[2,256,512]{2,1,0:T(8,128)(2,1)S(1)}, u32[]{:S(2)}, u32[]{:S(2)}) collective-permute-start(bf16[2,256,512]{2,1,0:T(8,128)(2,1)S(1)} %get-tuple-element.16), channel_id=1, source_target_pairs={{0,4},{4,8},{8,12},{1,5},{5,9},{9,13},{2,6},{6,10},{10,14},{3,7},{... | collective-permute-start | bytes 1572872 | tf_op jit(solution)/shard_map/ppermute | solution.py:22
  7.8 9.6 %collective-permute-done.2 = bf16[2,256,512]{2,1,0:T(8,128)(2,1)S(1)} collective-permute-done((bf16[2,256,512]{2,1,0:T(8,128)(2,1)S(1)}, bf16[2,256,512]{2,1,0:T(8,128)(2,1)S(1)}, u32[]{:S(2)}, u32[]{:S(2)}) %collective-permute-start.2) | collective-permute-done | bytes 524320 | tf_op jit(solution)/shard_map/ppermute | solution.py:185
  17.5 0.0 copy-done.1
  17.5 0.0 copy-done
  17.5 0.2 select_select_fusion
  17.7 3.5 %collective-permute-start.3 = (bf16[2,256,512]{2,1,0:T(8,128)(2,1)S(1)}, bf16[2,256,512]{2,1,0:T(8,128)(2,1)S(1)}, u32[]{:S(2)}, u32[]{:S(2)}) collective-permute-start(bf16[2,256,512]{2,1,0:T(8,128)(2,1)S(1)} %select_select_fusion), channel_id=1, source_target_pairs={{0,4},{4,8},{8,12},{1,5},{5,9},{9,13},{2,6},{6,10},{10,14},{3,7},{... | collective-permute-start | bytes 1572872 | tf_op jit(solution)/shard_map/ppermute | solution.py:22
  21.2 0.0 collective-permute-done
  21.2 1.9 %collective-permute-start.1 = (bf16[2,256,512]{2,1,0:T(8,128)(2,1)S(1)}, bf16[2,256,512]{2,1,0:T(8,128)(2,1)S(1)}, u32[]{:S(2)}, u32[]{:S(2)}) collective-permute-start(bf16[2,256,512]{2,1,0:T(8,128)(2,1)S(1)} %collective-permute-done), channel_id=1, source_target_pairs={{0,4},{4,8},{8,12},{1,5},{5,9},{9,13},{2,6},{6,10},{10,14},{3,7},{... | collective-permute-start | bytes 1572872 | tf_op jit(solution)/shard_map/ppermute | solution.py:22
  23.1 0.4 maximum_select_fusion.1
  23.6 1.0 %slice_bitcast_fusion = (bf16[512,512]{1,0:T(8,128)(2,1)}, bf16[512,512]{1,0:T(8,128)(2,1)}) fusion(bf16[2,512,512]{2,1,0:T(8,128)(2,1)S(1)} %maximum_select_fusion.1), kind=kLoop, calls=%fused_computation.5 | loop fusion | bytes 2097152 | tf_op jit(solution)/shard_map/squeeze | solution.py:233
  24.6 6.4 %shard_map.82 = (f32[512,8]{1,0:T(8,128)}, f32[512,8]{1,0:T(8,128)}, f32[512,1024]{1,0:T(8,128)}) custom-call(s32[1]{0:T(128)} %bitcast.first_ref, bf16[512,1024]{1,0:T(8,128)(2,1)} %q_ref.7, bf16[512,512]{1,0:T(8,128)(2,1)} %get-tuple-element.28.k_ref, bf16[512,512]{1,0:T(8,128)(2,1)} %get-tuple-element.27.v_ref), custom_call_target="tpu_custom_call" | custom-call | flops 1073741824 | bytes 4194304 | tf_op jit(solution)/shard_map/pallas_call | solution.py:174
  31.0 3.4 %collective-permute-done.3 = bf16[2,256,512]{2,1,0:T(8,128)(2,1)S(1)} collective-permute-done((bf16[2,256,512]{2,1,0:T(8,128)(2,1)S(1)}, bf16[2,256,512]{2,1,0:T(8,128)(2,1)S(1)}, u32[]{:S(2)}, u32[]{:S(2)}) %collective-permute-start.3) | collective-permute-done | bytes 524320 | tf_op jit(solution)/shard_map/ppermute | solution.py:22
  34.4 3.5 %collective-permute-start.4 = (bf16[2,256,512]{2,1,0:T(8,128)(2,1)S(1)}, bf16[2,256,512]{2,1,0:T(8,128)(2,1)S(1)}, u32[]{:S(2)}, u32[]{:S(2)}) collective-permute-start(bf16[2,256,512]{2,1,0:T(8,128)(2,1)S(1)} %collective-permute-done.3), channel_id=1, source_target_pairs={{0,4},{4,8},{8,12},{1,5},{5,9},{9,13},{2,6},{6,10},{10,14},{3,7},{... | collective-permute-start | bytes 1572872 | tf_op jit(solution)/shard_map/ppermute | solution.py:22
  37.9 0.8 %slice_bitcast_fusion.4 = (bf16[256,512]{1,0:T(8,128)(2,1)}, bf16[256,512]{1,0:T(8,128)(2,1)}) fusion(bf16[2,256,512]{2,1,0:T(8,128)(2,1)S(1)} %collective-permute-done), kind=kLoop, calls=%fused_computation.13 | loop fusion | bytes 1048576 | tf_op jit(solution)/shard_map/squeeze | solution.py:235
  38.7 6.0 %shard_map.83 = (f32[512,8]{1,0:T(8,128)}, f32[512,8]{1,0:T(8,128)}, f32[512,1024]{1,0:T(8,128)}) custom-call(s32[1]{0:T(128)} %bitcast.first_ref, bf16[512,1024]{1,0:T(8,128)(2,1)} %q_ref.7, bf16[256,512]{1,0:T(8,128)(2,1)} %get-tuple-element.32.k_ref, bf16[256,512]{1,0:T(8,128)(2,1)} %get-tuple-element.31.v_ref, f32[512,8]{1,0:T(8,128)} %get-tuple-element.18.rest_0_, ...), custom_call_target="tpu_custom_call" | custom-call | flops 536870912 | bytes 5767168 | tf_op jit(solution)/shard_map/pallas_call | solution.py:174
  44.7 0.8 %slice_bitcast_fusion.6 = (bf16[256,512]{1,0:T(8,128)(2,1)}, bf16[256,512]{1,0:T(8,128)(2,1)}) fusion(bf16[2,256,512]{2,1,0:T(8,128)(2,1)S(1)} %collective-permute-done.3), kind=kLoop, calls=%fused_computation.15 | loop fusion | bytes 1048576 | tf_op jit(solution)/shard_map/squeeze | solution.py:235
  45.5 6.0 %shard_map.84 = (f32[512,8]{1,0:T(8,128)}, f32[512,8]{1,0:T(8,128)}, f32[512,1024]{1,0:T(8,128)}) custom-call(s32[1]{0:T(128)} %bitcast.first_ref, bf16[512,1024]{1,0:T(8,128)(2,1)} %q_ref.7, bf16[256,512]{1,0:T(8,128)(2,1)} %get-tuple-element.34.k_ref, bf16[256,512]{1,0:T(8,128)(2,1)} %get-tuple-element.33.v_ref, f32[512,8]{1,0:T(8,128)} %get-tuple-element.21.rest_0_, ...), custom_call_target="tpu_custom_call" | custom-call | flops 536870912 | bytes 5767168 | tf_op jit(solution)/shard_map/pallas_call | solution.py:174
  51.5 0.0 collective-permute-done.1
  51.5 3.4 %collective-permute-done.4 = bf16[2,256,512]{2,1,0:T(8,128)(2,1)S(1)} collective-permute-done((bf16[2,256,512]{2,1,0:T(8,128)(2,1)S(1)}, bf16[2,256,512]{2,1,0:T(8,128)(2,1)S(1)}, u32[]{:S(2)}, u32[]{:S(2)}) %collective-permute-start.4) | collective-permute-done | bytes 524320 | tf_op jit(solution)/shard_map/ppermute | solution.py:22
  54.9 0.4 maximum_select_fusion
  55.3 1.0 %slice_bitcast_fusion.2 = (bf16[512,512]{1,0:T(8,128)(2,1)}, bf16[512,512]{1,0:T(8,128)(2,1)}) fusion(bf16[2,512,512]{2,1,0:T(8,128)(2,1)S(1)} %maximum_select_fusion), kind=kLoop, calls=%fused_computation.7 | loop fusion | bytes 2097152 | tf_op jit(solution)/shard_map/squeeze | solution.py:236
  56.4 6.6 %shard_map.85 = bf16[512,1024]{1,0:T(8,128)(2,1)} custom-call(s32[1]{0:T(128)} %bitcast.first_ref, bf16[512,1024]{1,0:T(8,128)(2,1)} %q_ref.7, bf16[512,512]{1,0:T(8,128)(2,1)} %get-tuple-element.30.k_ref, bf16[512,512]{1,0:T(8,128)(2,1)} %get-tuple-element.29.v_ref, f32[512,8]{1,0:T(8,128)} %get-tuple-element.24.rest_0_, ...), custom_call_target="tpu_custom_call" | custom-call | flops 1073741824 | bytes 6291456 | tf_op jit(solution)/shard_map/pallas_call | solution.py:174
  (1 shorter events, 0.0 us)
Async XLA Ops:
  0.0 17.5 %copy-start.1 = (bf16[512,512]{1,0:T(8,128)(2,1)S(1)}, bf16[512,512]{1,0:T(8,128)(2,1)}, u32[]{:S(2)}) copy-start(bf16[512,512]{1,0:T(8,128)(2,1)} %param.9) | copy-start | bytes 1572868
  0.0 17.5 %copy-start = (bf16[512,512]{1,0:T(8,128)(2,1)S(1)}, bf16[512,512]{1,0:T(8,128)(2,1)}, u32[]{:S(2)}) copy-start(bf16[512,512]{1,0:T(8,128)(2,1)} %param.10) | copy-start | bytes 1572868
  3.8 13.7 %collective-permute-start.2 = (bf16[2,256,512]{2,1,0:T(8,128)(2,1)S(1)}, bf16[2,256,512]{2,1,0:T(8,128)(2,1)S(1)}, u32[]{:S(2)}, u32[]{:S(2)}) collective-permute-start(bf16[2,256,512]{2,1,0:T(8,128)(2,1)S(1)} %get-tuple-element.17), channel_id=1, source_target_pairs={{0,2},{2,0},{1,3},{3,1},{4,6},{6,4},{5,7},{7,5},{8,10},{10,8},{9,1... | collective-permute-start | bytes 1572872 | tf_op jit(solution)/shard_map/ppermute | solution.py:185
  4.4 16.8 %collective-permute-start = (bf16[2,256,512]{2,1,0:T(8,128)(2,1)S(1)}, bf16[2,256,512]{2,1,0:T(8,128)(2,1)S(1)}, u32[]{:S(2)}, u32[]{:S(2)}) collective-permute-start(bf16[2,256,512]{2,1,0:T(8,128)(2,1)S(1)} %get-tuple-element.16), channel_id=1, source_target_pairs={{0,4},{4,8},{8,12},{1,5},{5,9},{9,13},{2,6},{6,10},{10,14},{3,7},{... | collective-permute-start | bytes 1572872 | tf_op jit(solution)/shard_map/ppermute | solution.py:22
  17.7 16.7 %collective-permute-start.3 = (bf16[2,256,512]{2,1,0:T(8,128)(2,1)S(1)}, bf16[2,256,512]{2,1,0:T(8,128)(2,1)S(1)}, u32[]{:S(2)}, u32[]{:S(2)}) collective-permute-start(bf16[2,256,512]{2,1,0:T(8,128)(2,1)S(1)} %select_select_fusion), channel_id=1, source_target_pairs={{0,4},{4,8},{8,12},{1,5},{5,9},{9,13},{2,6},{6,10},{10,14},{3,7},{... | collective-permute-start | bytes 1572872 | tf_op jit(solution)/shard_map/ppermute | solution.py:22
  21.2 30.3 %collective-permute-start.1 = (bf16[2,256,512]{2,1,0:T(8,128)(2,1)S(1)}, bf16[2,256,512]{2,1,0:T(8,128)(2,1)S(1)}, u32[]{:S(2)}, u32[]{:S(2)}) collective-permute-start(bf16[2,256,512]{2,1,0:T(8,128)(2,1)S(1)} %collective-permute-done), channel_id=1, source_target_pairs={{0,4},{4,8},{8,12},{1,5},{5,9},{9,13},{2,6},{6,10},{10,14},{3,7},{... | collective-permute-start | bytes 1572872 | tf_op jit(solution)/shard_map/ppermute | solution.py:22
  34.4 20.5 %collective-permute-start.4 = (bf16[2,256,512]{2,1,0:T(8,128)(2,1)S(1)}, bf16[2,256,512]{2,1,0:T(8,128)(2,1)S(1)}, u32[]{:S(2)}, u32[]{:S(2)}) collective-permute-start(bf16[2,256,512]{2,1,0:T(8,128)(2,1)S(1)} %collective-permute-done.3), channel_id=1, source_target_pairs={{0,4},{4,8},{8,12},{1,5},{5,9},{9,13},{2,6},{6,10},{10,14},{3,7},{... | collective-permute-start | bytes 1572872 | tf_op jit(solution)/shard_map/ppermute | solution.py:22

commit v8 on v7

--- a/solution.py
+++ b/solution.py
@@ -30,10 +30,24 @@
     return reduce(partial, axis=1, keepdims=True)
 
 
-def chunk_kernel(chunk, first, last, rows, key_rows, query_block, group):
+def chunk_kernel(chunk, first, last, rows, key_rows, query_block, group, split):
     blocks = rows // query_block
 
-    def kernel(first_ref, q_ref, k_ref, v_ref, *rest):
+    def kernel(first_ref, q_ref, *rest):
+        if split:
+            ka_ref, va_ref, kb_ref, vb_ref = rest[:4]
+            rest = rest[4:]
+            swap = first_ref[1] != 0
+            ka, kb, va, vb = ka_ref[...], kb_ref[...], va_ref[...], vb_ref[...]
+            keys_all = jnp.concatenate([jnp.where(swap, kb, ka), jnp.where(swap, ka, kb)], axis=0)
+            values_all = jnp.concatenate([jnp.where(swap, vb, va), jnp.where(swap, va, vb)], axis=0)
+            get_keys = lambda k0, k1: keys_all[k0:k1]
+            get_values = lambda k0, k1: values_all[k0:k1]
+        else:
+            k_ref, v_ref = rest[:2]
+            rest = rest[2:]
+            get_keys = lambda k0, k1: k_ref[k0:k1, :]
+            get_values = lambda k0, k1: v_ref[k0:k1, :]
         if first:
             m_out, l_out, acc_out = rest
         elif last:
@@ -73,7 +87,7 @@
                     scores = []
                     for k0, k1, masked in pieces:
                         s = lax.dot_general(
-                            query, k_ref[k0:k1, :], (((1,), (1,)), ((), ())),
+                            query, get_keys(k0, k1), (((1,), (1,)), ((), ())),
                             preferred_element_type=jnp.float32,
                         ) * log2_scale
                         if masked:
@@ -94,7 +108,7 @@
                         p = jnp.exp2(s - m_new)
                         part = row_reduce(p, jnp.add, jnp.sum)
                         l_part = part if l_part is None else l_part + part
-                        term = jnp.dot(p.astype(jnp.bfloat16), v_ref[k0:k1, :],
+                        term = jnp.dot(p.astype(jnp.bfloat16), get_values(k0, k1),
                                        preferred_element_type=jnp.float32)
                         pv = term if pv is None else pv + term
                     if first:
@@ -137,8 +151,9 @@
     return kernel
 
 
-def attend_chunk(chunk, queries, key_rows, value_rows, first_row, state):
-    key_count, key_cols = key_rows.shape
+def attend_chunk(chunk, queries, pair, first_row, state, other=None, swap=None):
+    split = other is not None
+    key_count, key_cols = pair.shape[1:]
     rows, query_cols = queries.shape
     kv_heads = key_cols // HEAD_DIM
     group = query_cols // key_cols
@@ -146,12 +161,13 @@
     first = state is None
     last = chunk == 0
     query_block = QUERY_BLOCK if chunk == 1 else MASKED_QUERY_BLOCK
-    kernel = chunk_kernel(chunk, first, last, rows, key_count, query_block, group)
+    kernel = chunk_kernel(chunk, first, last, rows, key_count * (2 if split else 1), query_block, group, split)
     q_spec = pl.BlockSpec((rows, group * HEAD_DIM), lambda h, f: (0, h))
-    kv_spec = pl.BlockSpec((key_count, HEAD_DIM), lambda h, f: (0, h))
+    k_spec = pl.BlockSpec((None, key_count, HEAD_DIM), lambda h, f: (0, 0, h))
+    v_spec = pl.BlockSpec((None, key_count, HEAD_DIM), lambda h, f: (1, 0, h))
     stat_spec = pl.BlockSpec((rows, heads), lambda h, f: (0, 0))
     state_specs = [stat_spec, stat_spec, q_spec]
-    in_specs = [q_spec, kv_spec, kv_spec] + ([] if first else state_specs)
+    in_specs = [q_spec, k_spec, v_spec] + ([k_spec, v_spec] if split else []) + ([] if first else state_specs)
     stat_shape = jax.ShapeDtypeStruct((rows, heads), jnp.float32)
     if last:
         out_specs = q_spec
@@ -171,13 +187,15 @@
         in_specs=in_specs,
         out_specs=out_specs,
     )
+    scalars = jnp.stack([first_row, swap]).astype(jnp.int32) if split else first_row.reshape(1)
+    pairs = (pair, pair, other, other) if split else (pair, pair)
     return pl.pallas_call(
         kernel,
         grid_spec=grid_spec,
         out_shape=out_shape,
         cost_estimate=cost,
         compiler_params=pltpu.CompilerParams(dimension_semantics=("arbitrary",)),
-    )(first_row.reshape(1), queries, key_rows, value_rows, *([] if first else state))
+    )(scalars, queries, *pairs, *([] if first else state))
 
 
 def swap_variant(half):
@@ -228,12 +246,15 @@
         far_own = shifted(near_own, "seq", 1)
         far_other = shifted(near_other, "seq", 1)
         patched = halves_in_order(own_half, other_half, variant_index)
-        far = halves_in_order(far_own, far_other, variant_index)
         near_parts = (near_own, near_other)
-    state = attend_chunk(2, queries, patched[0], patched[1], first_row, None)
+        far = None
+    state = attend_chunk(2, queries, patched, first_row, None)
     for part in near_parts:
-        state = attend_chunk(1, queries, part[0], part[1], first_row, state)
-    result = attend_chunk(0, queries, far[0], far[1], first_row, state)
+        state = attend_chunk(1, queries, part, first_row, state)
+    if far is None:
+        result = attend_chunk(0, queries, far_own, first_row, state, far_other, variant_index)
+    else:
+        result = attend_chunk(0, queries, far, first_row, state)
     return result[None]
 
 

time: 63.5 us -> 67.2 us (1.058)
  the two profiles are of different devices: /device:TPU:22 before, /device:TPU:18 now
where the time goes in v8:
time: 67.2 us; the launch traced here: 66.6 us
  Pallas kernels  25.7 us (38%)
  waiting for transfers between devices  20.9 us (31%)
  starting transfers between devices  13 us (19%)
  other arithmetic  5.22 us (8%)
  local copies, waits for them, and re-layouts  0.96 us (1%)
  between operations  0.85 us (1%)
    pallas_call x4, Pallas kernels, attend_chunk(): pl.pallas_call(kernel, grid_spec=grid_spec, out_shape=out_shape, cost_est...  25.7 us
    ppermute x4, starting transfers between devices, shifted(): return lax.ppermute(shard, axis, pairs)  12.4 us
    ppermute x4, waiting for transfers between devices, shifted(): return lax.ppermute(shard, axis, pairs)  11.3 us
    ppermute x1, waiting for transfers between devices, swap_variant(): lax.ppermute(half, 'variant', [(i, (i + 1) % variants) for i in range(var...  9.65 us
    another operation x1, other arithmetic, shard_body(): clean_own = jnp.stack([clean_keys, clean_values])  1.56 us
    select_n x1, other arithmetic, halves_in_order(): jnp.where(variant_index == 0, jnp.concatenate([own, other], axis=1), jnp....  1.4 us
  transfers between devices with their start and end apart: 5, of which 2 were waited for; matrix products, arithmetic and copies ran while one was open for 3% of the time, Pallas kernels for 28%

profile of v8, /device:TPU:18, one launch (start us, length us, event | category | flops | bytes accessed | tf_op | source)
XLA Modules:
  0.0 66.6 jit_solution(1403080709371574759)
XLA Ops:
  0.0 0.0 copy-start.2
  0.0 0.0 copy-start.3
  0.7 0.7 %add_bitcast_fusion = s32[2]{0:T(128)S(1)} fusion(s32[1,2]{1,0:T(1,128)} %param.14, s32[1,2]{1,0:T(1,128)} %param.15), kind=kLoop, calls=%fused_computation.12 | loop fusion | flops 2 | bytes 24 | tf_op jit(solution)/shard_map/lt | solution.py:220
  1.4 0.7 %and_reduce_fusion = pred[512]{0:T(512)(128)(4,1)S(1)} fusion(pred[]{:T(512)} %bitcast.6, s32[2]{0:T(128)S(1)} %add_bitcast_fusion, s32[2]{0:T(128)} %bitcast.20), kind=kLoop, calls=%fused_computation.8 | loop fusion | flops 4608 | bytes 529 | tf_op jit(solution)/shard_map/reduce_or | solution.py:222
  2.2 1.6 %pad_maximum_fusion.1 = (bf16[2,256,512]{2,1,0:T(8,128)(2,1)S(1)}, bf16[2,256,512]{2,1,0:T(8,128)(2,1)S(1)}) fusion(bf16[1,256,512]{2,1,0:T(8,128)(2,1)} %bitcast.18, bf16[1,256,512]{2,1,0:T(8,128)(2,1)} %bitcast.19, bf16[1,512,512]{2,1,0:T(8,128)(2,1)} %bitcast.14, bf16[1,512,512]{2,1,0:T(8,128)(2,1)} %bitcast.16, pred[]{:T(512)S(6)} %eq.6, ...), kind=kLoop, calls=%fused_computation.5 | loop fusion | flops 3670016 | bytes 2621697 | tf_op jit(solution)/shard_map/stack | solution.py:224
  3.8 0.6 collective-permute-start.2
  4.4 3.5 %collective-permute-start = (bf16[2,256,512]{2,1,0:T(8,128)(2,1)S(1)}, bf16[2,256,512]{2,1,0:T(8,128)(2,1)S(1)}, u32[]{:S(2)}, u32[]{:S(2)}) collective-permute-start(bf16[2,256,512]{2,1,0:T(8,128)(2,1)S(1)} %get-tuple-element.16), channel_id=1, source_target_pairs={{0,4},{4,8},{8,12},{1,5},{5,9},{9,13},{2,6},{6,10},{10,14},{3,7},{... | collective-permute-start | bytes 1572872 | tf_op jit(solution)/shard_map/ppermute | solution.py:22
  7.8 9.6 %collective-permute-done.2 = bf16[2,256,512]{2,1,0:T(8,128)(2,1)S(1)} collective-permute-done((bf16[2,256,512]{2,1,0:T(8,128)(2,1)S(1)}, bf16[2,256,512]{2,1,0:T(8,128)(2,1)S(1)}, u32[]{:S(2)}, u32[]{:S(2)}) %collective-permute-start.2) | collective-permute-done | bytes 524320 | tf_op jit(solution)/shard_map/ppermute | solution.py:203
  17.5 0.0 copy-done.2
  17.5 0.0 copy-done.3
  17.5 0.2 select_select_fusion
  17.7 3.5 %collective-permute-start.3 = (bf16[2,256,512]{2,1,0:T(8,128)(2,1)S(1)}, bf16[2,256,512]{2,1,0:T(8,128)(2,1)S(1)}, u32[]{:S(2)}, u32[]{:S(2)}) collective-permute-start(bf16[2,256,512]{2,1,0:T(8,128)(2,1)S(1)} %select_select_fusion), channel_id=1, source_target_pairs={{0,4},{4,8},{8,12},{1,5},{5,9},{9,13},{2,6},{6,10},{10,14},{3,7},{... | collective-permute-start | bytes 1572872 | tf_op jit(solution)/shard_map/ppermute | solution.py:22
  21.2 0.0 collective-permute-done.rest_0_.rest_1_
  21.2 0.0 copy-start
  21.2 1.9 %collective-permute-start.1 = (bf16[2,256,512]{2,1,0:T(8,128)(2,1)S(1)}, bf16[2,256,512]{2,1,0:T(8,128)(2,1)S(1)}, u32[]{:S(2)}, u32[]{:S(2)}) collective-permute-start(bf16[2,256,512]{2,1,0:T(8,128)(2,1)S(1)} %collective-permute-done.rest_0_.rest_1_), channel_id=1, source_target_pairs={{0,4},{4,8},{8,12},{1,5},{5,9},{9,13},{2,6},{6,10},{10,14},{3,7},{... | collective-permute-start | bytes 1572872 | tf_op jit(solution)/shard_map/ppermute | solution.py:22
  23.1 11.2 %collective-permute-done.3.rest_0_.rest_1_ = bf16[2,256,512]{2,1,0:T(8,128)(2,1)S(1)} collective-permute-done((bf16[2,256,512]{2,1,0:T(8,128)(2,1)S(1)}, bf16[2,256,512]{2,1,0:T(8,128)(2,1)S(1)}, u32[]{:S(2)}, u32[]{:S(2)}) %collective-permute-start.3) | collective-permute-done | bytes 524320 | tf_op jit(solution)/shard_map/ppermute | solution.py:22
  34.4 0.0 copy-start.1
  34.4 3.5 %collective-permute-start.4 = (bf16[2,256,512]{2,1,0:T(8,128)(2,1)S(1)}, bf16[2,256,512]{2,1,0:T(8,128)(2,1)S(1)}, u32[]{:S(2)}, u32[]{:S(2)}) collective-permute-start(bf16[2,256,512]{2,1,0:T(8,128)(2,1)S(1)} %collective-permute-done.3.rest_0_.rest_1_), channel_id=1, source_target_pairs={{0,4},{4,8},{8,12},{1,5},{5,9},{9,13},{2,6},{6,10},{10,14},{3,7},{... | collective-permute-start | bytes 1572872 | tf_op jit(solution)/shard_map/ppermute | solution.py:22
  37.9 0.6 pad_add_fusion.first_ref
  38.5 1.4 %maximum_select_fusion.rest_0_.rest_1_ = bf16[2,512,512]{2,1,0:T(8,128)(2,1)} fusion(bf16[2,256,512]{2,1,0:T(8,128)(2,1)S(1)} %select_select_fusion, bf16[2,256,512]{2,1,0:T(8,128)(2,1)S(1)} %get-tuple-element.16, pred[]{:T(512)S(6)} %eq.6), kind=kLoop, calls=%fused_computation.2 | loop fusion | flops 4718592 | bytes 2097153 | tf_op jit(solution)/shard_map/jit(_where)/select_n | solution.py:207
  39.9 6.4 %shard_map.82 = (f32[512,8]{1,0:T(8,128)}, f32[512,8]{1,0:T(8,128)}, f32[512,1024]{1,0:T(8,128)}) custom-call(s32[1]{0:T(128)} %bitcast.first_ref, bf16[512,1024]{1,0:T(8,128)(2,1)} %q_ref.7, bf16[2,512,512]{2,1,0:T(8,128)(2,1)} %maximum_select_fusion.rest_0_.rest_1_, bf16[2,512,512]{2,1,0:T(8,128)(2,1)} %maximum_select_fusion.rest_0_.rest_1_), custom_call_target="tpu_custom_call" | custom-call | flops 1073741824 | bytes 4194304 | tf_op jit(solution)/shard_map/pallas_call | solution.py:192
  46.3 0.0 copy-done
  46.3 0.0 copy-done.1
  46.3 6.0 %shard_map.83 = (f32[512,8]{1,0:T(8,128)}, f32[512,8]{1,0:T(8,128)}, f32[512,1024]{1,0:T(8,128)}) custom-call(s32[1]{0:T(128)} %bitcast.first_ref, bf16[512,1024]{1,0:T(8,128)(2,1)} %q_ref.7, bf16[2,256,512]{2,1,0:T(8,128)(2,1)} %copy-done, bf16[2,256,512]{2,1,0:T(8,128)(2,1)} %copy-done, f32[512,8]{1,0:T(8,128)} %get-tuple-element.18.rest_2_, ...), custom_call_target="tpu_custom_call" | custom-call | flops 536870912 | bytes 5767168 | tf_op jit(solution)/shard_map/pallas_call | solution.py:192
  52.3 6.0 %shard_map.84 = (f32[512,8]{1,0:T(8,128)}, f32[512,8]{1,0:T(8,128)}, f32[512,1024]{1,0:T(8,128)}) custom-call(s32[1]{0:T(128)} %bitcast.first_ref, bf16[512,1024]{1,0:T(8,128)(2,1)} %q_ref.7, bf16[2,256,512]{2,1,0:T(8,128)(2,1)} %copy-done.1, bf16[2,256,512]{2,1,0:T(8,128)(2,1)} %copy-done.1, f32[512,8]{1,0:T(8,128)} %get-tuple-element.21.rest_2_, ...), custom_call_target="tpu_custom_call" | custom-call | flops 536870912 | bytes 5767168 | tf_op jit(solution)/shard_map/pallas_call | solution.py:192
  58.2 0.0 collective-permute-done.1.rest_0_.rest_1_
  58.2 0.0 copy-start.4
  58.3 0.0 collective-permute-done.4.rest_2_.rest_3_
  58.3 0.0 copy-start.5
  58.3 0.8 %copy-done.4 = bf16[2,256,512]{2,1,0:T(8,128)(2,1)} copy-done((bf16[2,256,512]{2,1,0:T(8,128)(2,1)}, bf16[2,256,512]{2,1,0:T(8,128)(2,1)S(1)}, u32[]{:S(2)}) %copy-start.4) | copy-done | bytes 524312
  59.0 0.2 copy-done.5
  59.2 7.4 %shard_map.85 = bf16[512,1024]{1,0:T(8,128)(2,1)} custom-call(s32[2]{0:T(128)} %pad_add_fusion.first_ref, bf16[512,1024]{1,0:T(8,128)(2,1)} %q_ref.7, bf16[2,256,512]{2,1,0:T(8,128)(2,1)} %copy-done.4, bf16[2,256,512]{2,1,0:T(8,128)(2,1)} %copy-done.4, bf16[2,256,512]{2,1,0:T(8,128)(2,1)} %copy-done.5, bf16[2,256,512]{2,1,0:T(8,128)(2,1)} %copy-done.5, ...), custom_call_target="tpu_custom_call" | custom-call | flops 1073741824 | bytes 5767168 | tf_op jit(solution)/shard_map/pallas_call | solution.py:192
  (1 shorter events, 0.0 us)
Async XLA Ops:
  0.0 17.5 %copy-start.2 = (bf16[512,512]{1,0:T(8,128)(2,1)S(1)}, bf16[512,512]{1,0:T(8,128)(2,1)}, u32[]{:S(2)}) copy-start(bf16[512,512]{1,0:T(8,128)(2,1)} %param.10) | copy-start | bytes 1572868
  0.0 17.5 %copy-start.3 = (bf16[512,512]{1,0:T(8,128)(2,1)S(1)}, bf16[512,512]{1,0:T(8,128)(2,1)}, u32[]{:S(2)}) copy-start(bf16[512,512]{1,0:T(8,128)(2,1)} %param.9) | copy-start | bytes 1572868
  3.8 13.7 %collective-permute-start.2 = (bf16[2,256,512]{2,1,0:T(8,128)(2,1)S(1)}, bf16[2,256,512]{2,1,0:T(8,128)(2,1)S(1)}, u32[]{:S(2)}, u32[]{:S(2)}) collective-permute-start(bf16[2,256,512]{2,1,0:T(8,128)(2,1)S(1)} %get-tuple-element.17), channel_id=1, source_target_pairs={{0,2},{2,0},{1,3},{3,1},{4,6},{6,4},{5,7},{7,5},{8,10},{10,8},{9,1... | collective-permute-start | bytes 1572872 | tf_op jit(solution)/shard_map/ppermute | solution.py:203
  4.4 16.8 %collective-permute-start = (bf16[2,256,512]{2,1,0:T(8,128)(2,1)S(1)}, bf16[2,256,512]{2,1,0:T(8,128)(2,1)S(1)}, u32[]{:S(2)}, u32[]{:S(2)}) collective-permute-start(bf16[2,256,512]{2,1,0:T(8,128)(2,1)S(1)} %get-tuple-element.16), channel_id=1, source_target_pairs={{0,4},{4,8},{8,12},{1,5},{5,9},{9,13},{2,6},{6,10},{10,14},{3,7},{... | collective-permute-start | bytes 1572872 | tf_op jit(solution)/shard_map/ppermute | solution.py:22
  17.7 16.7 %collective-permute-start.3 = (bf16[2,256,512]{2,1,0:T(8,128)(2,1)S(1)}, bf16[2,256,512]{2,1,0:T(8,128)(2,1)S(1)}, u32[]{:S(2)}, u32[]{:S(2)}) collective-permute-start(bf16[2,256,512]{2,1,0:T(8,128)(2,1)S(1)} %select_select_fusion), channel_id=1, source_target_pairs={{0,4},{4,8},{8,12},{1,5},{5,9},{9,13},{2,6},{6,10},{10,14},{3,7},{... | collective-permute-start | bytes 1572872 | tf_op jit(solution)/shard_map/ppermute | solution.py:22
  21.2 25.1 %copy-start = (bf16[2,256,512]{2,1,0:T(8,128)(2,1)}, bf16[2,256,512]{2,1,0:T(8,128)(2,1)S(1)}, u32[]{:S(2)}) copy-start(bf16[2,256,512]{2,1,0:T(8,128)(2,1)S(1)} %collective-permute-done.rest_0_.rest_1_) | copy-start | bytes 1572868
  21.2 37.0 %collective-permute-start.1 = (bf16[2,256,512]{2,1,0:T(8,128)(2,1)S(1)}, bf16[2,256,512]{2,1,0:T(8,128)(2,1)S(1)}, u32[]{:S(2)}, u32[]{:S(2)}) collective-permute-start(bf16[2,256,512]{2,1,0:T(8,128)(2,1)S(1)} %collective-permute-done.rest_0_.rest_1_), channel_id=1, source_target_pairs={{0,4},{4,8},{8,12},{1,5},{5,9},{9,13},{2,6},{6,10},{10,14},{3,7},{... | collective-permute-start | bytes 1572872 | tf_op jit(solution)/shard_map/ppermute | solution.py:22
  34.4 11.9 %copy-start.1 = (bf16[2,256,512]{2,1,0:T(8,128)(2,1)}, bf16[2,256,512]{2,1,0:T(8,128)(2,1)S(1)}, u32[]{:S(2)}) copy-start(bf16[2,256,512]{2,1,0:T(8,128)(2,1)S(1)} %collective-permute-done.3.rest_0_.rest_1_) | copy-start | bytes 1572868
  34.4 23.9 %collective-permute-start.4 = (bf16[2,256,512]{2,1,0:T(8,128)(2,1)S(1)}, bf16[2,256,512]{2,1,0:T(8,128)(2,1)S(1)}, u32[]{:S(2)}, u32[]{:S(2)}) collective-permute-start(bf16[2,256,512]{2,1,0:T(8,128)(2,1)S(1)} %collective-permute-done.3.rest_0_.rest_1_), channel_id=1, source_target_pairs={{0,4},{4,8},{8,12},{1,5},{5,9},{9,13},{2,6},{6,10},{10,14},{3,7},{... | collective-permute-start | bytes 1572872 | tf_op jit(solution)/shard_map/ppermute | solution.py:22
  58.2 0.8 %copy-start.4 = (bf16[2,256,512]{2,1,0:T(8,128)(2,1)}, bf16[2,256,512]{2,1,0:T(8,128)(2,1)S(1)}, u32[]{:S(2)}) copy-start(bf16[2,256,512]{2,1,0:T(8,128)(2,1)S(1)} %collective-permute-done.1.rest_0_.rest_1_) | copy-start | bytes 1572868
  58.3 1.0 %copy-start.5 = (bf16[2,256,512]{2,1,0:T(8,128)(2,1)}, bf16[2,256,512]{2,1,0:T(8,128)(2,1)S(1)}, u32[]{:S(2)}) copy-start(bf16[2,256,512]{2,1,0:T(8,128)(2,1)S(1)} %collective-permute-done.4.rest_2_.rest_3_) | copy-start | bytes 1572868

commit v9 on v7

--- a/solution.py
+++ b/solution.py
@@ -30,17 +30,19 @@
     return reduce(partial, axis=1, keepdims=True)
 
 
-def chunk_kernel(chunk, first, last, rows, key_rows, query_block, group):
+def chunk_kernel(chunk, first, last, rows, key_rows, query_block, group, head_base=0, aliased=False):
     blocks = rows // query_block
 
     def kernel(first_ref, q_ref, k_ref, v_ref, *rest):
+        if aliased:
+            rest = rest[:-2] + rest[-1:]
         if first:
             m_out, l_out, acc_out = rest
         elif last:
             m_in, l_in, acc_in, o_ref = rest
         else:
             m_in, l_in, acc_in, m_out, l_out, acc_out = rest
-        head = pl.program_id(0)
+        head = pl.program_id(0) + head_base
         first_row = first_ref[0]
         stat_cols = (m_out if first else m_in).shape[1]
         diag_shape = (query_block, query_block)
@@ -137,21 +139,30 @@
     return kernel
 
 
-def attend_chunk(chunk, queries, key_rows, value_rows, first_row, state):
-    key_count, key_cols = key_rows.shape
+def attend_chunk(chunk, queries, pair, first_row, state, kv_total=None, head_base=0, alias=None):
+    key_count, key_cols = pair.shape[1:]
     rows, query_cols = queries.shape
     kv_heads = key_cols // HEAD_DIM
-    group = query_cols // key_cols
-    heads = kv_heads * group
+    kv_total = kv_heads if kv_total is None else kv_total
+    group = query_cols // (kv_total * HEAD_DIM)
+    heads = kv_total * group
     first = state is None
     last = chunk == 0
     query_block = QUERY_BLOCK if chunk == 1 else MASKED_QUERY_BLOCK
-    kernel = chunk_kernel(chunk, first, last, rows, key_count, query_block, group)
-    q_spec = pl.BlockSpec((rows, group * HEAD_DIM), lambda h, f: (0, h))
-    kv_spec = pl.BlockSpec((key_count, HEAD_DIM), lambda h, f: (0, h))
+    kernel = chunk_kernel(chunk, first, last, rows, key_count, query_block, group,
+                          head_base, alias is not None)
+    q_spec = pl.BlockSpec((rows, group * HEAD_DIM), lambda h, f: (0, h + head_base))
+    k_spec = pl.BlockSpec((None, key_count, HEAD_DIM), lambda h, f: (0, 0, h))
+    v_spec = pl.BlockSpec((None, key_count, HEAD_DIM), lambda h, f: (1, 0, h))
     stat_spec = pl.BlockSpec((rows, heads), lambda h, f: (0, 0))
     state_specs = [stat_spec, stat_spec, q_spec]
-    in_specs = [q_spec, kv_spec, kv_spec] + ([] if first else state_specs)
+    in_specs = [q_spec, k_spec, v_spec] + ([] if first else state_specs)
+    operands = [first_row.reshape(1), queries, pair, pair] + ([] if first else list(state))
+    aliases = {}
+    if alias is not None:
+        in_specs.append(pl.BlockSpec(memory_space=pl.ANY))
+        aliases = {len(operands): 0}
+        operands.append(alias)
     stat_shape = jax.ShapeDtypeStruct((rows, heads), jnp.float32)
     if last:
         out_specs = q_spec
@@ -161,9 +172,9 @@
         out_shape = [stat_shape, stat_shape, jax.ShapeDtypeStruct((rows, query_cols), jnp.float32)]
     keys_per_row = rows // 2 + query_block // 2 if chunk != 1 else key_count
     cost = pl.CostEstimate(
-        flops=4 * heads * rows * keys_per_row * HEAD_DIM,
-        transcendentals=heads * rows * keys_per_row,
-        bytes_accessed=rows * query_cols * (2 + 4 + (0 if first else 4)) + 4 * key_count * key_cols,
+        flops=4 * kv_heads * group * rows * keys_per_row * HEAD_DIM,
+        transcendentals=kv_heads * group * rows * keys_per_row,
+        bytes_accessed=rows * kv_heads * group * HEAD_DIM * (2 + 4 + (0 if first else 4)) + 4 * key_count * key_cols,
     )
     grid_spec = pltpu.PrefetchScalarGridSpec(
         num_scalar_prefetch=1,
@@ -176,8 +187,9 @@
         grid_spec=grid_spec,
         out_shape=out_shape,
         cost_estimate=cost,
+        input_output_aliases=aliases,
         compiler_params=pltpu.CompilerParams(dimension_semantics=("arbitrary",)),
-    )(first_row.reshape(1), queries, key_rows, value_rows, *([] if first else state))
+    )(*operands)
 
 
 def swap_variant(half):
@@ -226,14 +238,24 @@
         other_half = jnp.where(inside_other[None, :, None], clean_other, corrupt_other)
         near_other = shifted(other_half, "seq", 1)
         far_own = shifted(near_own, "seq", 1)
-        far_other = shifted(near_other, "seq", 1)
+        split_cols = keys.shape[1] // 2
+        far_other_a = shifted(near_other[:, :, :split_cols], "seq", 1)
+        far_other_b = shifted(near_other[:, :, split_cols:], "seq", 1)
         patched = halves_in_order(own_half, other_half, variant_index)
-        far = halves_in_order(far_own, far_other, variant_index)
+        far_a = halves_in_order(far_own[:, :, :split_cols], far_other_a, variant_index)
+        far_b = halves_in_order(far_own[:, :, split_cols:], far_other_b, variant_index)
+        far = None
         near_parts = (near_own, near_other)
-    state = attend_chunk(2, queries, patched[0], patched[1], first_row, None)
+    state = attend_chunk(2, queries, patched, first_row, None)
     for part in near_parts:
-        state = attend_chunk(1, queries, part[0], part[1], first_row, state)
-    result = attend_chunk(0, queries, far[0], far[1], first_row, state)
+        state = attend_chunk(1, queries, part, first_row, state)
+    if far is not None:
+        result = attend_chunk(0, queries, far, first_row, state)
+    else:
+        kv_total = keys.shape[1] // HEAD_DIM
+        partial = attend_chunk(0, queries, far_a, first_row, state, kv_total, 0)
+        result = attend_chunk(0, queries, far_b, first_row, state, kv_total,
+                              kv_total // 2, partial)
     return result[None]
 
 

time: 63.5 us -> 62.6 us (0.986)
  the two profiles are of different devices: /device:TPU:22 before, /device:TPU:24 now
where the time goes in v9:
time: 62.6 us; the launch traced here: 62 us
  Pallas kernels  26.7 us (43%)
  waiting for transfers between devices  19.8 us (32%)
  starting transfers between devices  7.99 us (13%)
  other arithmetic  6.62 us (11%)
  between operations  0.84 us (1%)
    pallas_call x5, Pallas kernels, attend_chunk(): pl.pallas_call(kernel, grid_spec=grid_spec, out_shape=out_shape, cost_est...  26.7 us
    ppermute x1, waiting for transfers between devices, swap_variant(): lax.ppermute(half, 'variant', [(i, (i + 1) % variants) for i in range(var...  10.9 us
    ppermute x5, waiting for transfers between devices, shifted(): return lax.ppermute(shard, axis, pairs)  8.94 us
    ppermute x5, starting transfers between devices, shifted(): return lax.ppermute(shard, axis, pairs)  6.44 us
    select_n x3, other arithmetic, halves_in_order(): jnp.where(variant_index == 0, jnp.concatenate([own, other], axis=1), jnp....  3.42 us
    another operation x1, other arithmetic, shard_body(): clean_own = jnp.stack([clean_keys, clean_values])  1.56 us
    ppermute x1, starting transfers between devices, swap_variant(): lax.ppermute(half, 'variant', [(i, (i + 1) % variants) for i in range(var...  1.56 us
  transfers between devices with their start and end apart: 6, of which 3 were waited for; matrix products, arithmetic and copies ran while one was open for 4% of the time, Pallas kernels for 36%

profile of v9, /device:TPU:24, one launch (start us, length us, event | category | flops | bytes accessed | tf_op | source)
XLA Modules:
  0.0 62.0 jit_solution(11550051338993185583)
XLA Ops:
  0.0 0.0 copy-start.3
  0.0 0.0 copy-start.2
  0.7 0.7 %add_bitcast_fusion = s32[2]{0:T(128)S(1)} fusion(s32[1,2]{1,0:T(1,128)} %param.14, s32[1,2]{1,0:T(1,128)} %param.15), kind=kLoop, calls=%fused_computation.13 | loop fusion | flops 2 | bytes 24 | tf_op jit(solution)/shard_map/lt | solution.py:214
  1.4 0.7 %and_reduce_fusion = pred[512]{0:T(512)(128)(4,1)S(1)} fusion(pred[]{:T(512)} %bitcast.5, s32[2]{0:T(128)S(1)} %add_bitcast_fusion, s32[2]{0:T(128)} %bitcast.19), kind=kLoop, calls=%fused_computation.10 | loop fusion | flops 4608 | bytes 529 | tf_op jit(solution)/shard_map/reduce_or | solution.py:216
  2.2 1.6 %pad_maximum_fusion.1 = (bf16[2,256,512]{2,1,0:T(8,128)(2,1)S(1)}, bf16[2,256,512]{2,1,0:T(8,128)(2,1)S(1)}) fusion(bf16[1,256,512]{2,1,0:T(8,128)(2,1)} %bitcast.17, bf16[1,256,512]{2,1,0:T(8,128)(2,1)} %bitcast.18, bf16[1,512,512]{2,1,0:T(8,128)(2,1)} %bitcast.13, bf16[1,512,512]{2,1,0:T(8,128)(2,1)} %bitcast.15, pred[]{:T(512)S(6)} %eq.6, ...), kind=kLoop, calls=%fused_computation.5 | loop fusion | flops 3670016 | bytes 2621697 | tf_op jit(solution)/shard_map/stack | solution.py:218
  3.8 1.6 %collective-permute-start.2 = (bf16[2,256,512]{2,1,0:T(8,128)(2,1)S(1)}, bf16[2,256,512]{2,1,0:T(8,128)(2,1)S(1)}, u32[]{:S(2)}, u32[]{:S(2)}) collective-permute-start(bf16[2,256,512]{2,1,0:T(8,128)(2,1)S(1)} %get-tuple-element.17), channel_id=1, source_target_pairs={{0,2},{2,0},{1,3},{3,1},{4,6},{6,4},{5,7},{7,5},{8,10},{10,8},{9,1... | collective-permute-start | bytes 1572872 | tf_op jit(solution)/shard_map/ppermute | solution.py:197
  5.3 1.3 %collective-permute-start = (bf16[2,256,512]{2,1,0:T(8,128)(2,1)S(1)}, bf16[2,256,512]{2,1,0:T(8,128)(2,1)S(1)}, u32[]{:S(2)}, u32[]{:S(2)}) collective-permute-start(bf16[2,256,512]{2,1,0:T(8,128)(2,1)S(1)} %get-tuple-element.16), channel_id=1, source_target_pairs={{0,4},{4,8},{8,12},{1,5},{5,9},{9,13},{2,6},{6,10},{10,14},{3,7},{... | collective-permute-start | bytes 1572872 | tf_op jit(solution)/shard_map/ppermute | solution.py:22
  6.6 10.9 %collective-permute-done.2 = bf16[2,256,512]{2,1,0:T(8,128)(2,1)S(1)} collective-permute-done((bf16[2,256,512]{2,1,0:T(8,128)(2,1)S(1)}, bf16[2,256,512]{2,1,0:T(8,128)(2,1)S(1)}, u32[]{:S(2)}, u32[]{:S(2)}) %collective-permute-start.2) | collective-permute-done | bytes 524320 | tf_op jit(solution)/shard_map/ppermute | solution.py:197
  17.5 0.0 copy-done.3
  17.5 0.0 copy-done.2
  17.5 0.2 select_select_fusion
  17.7 1.3 %collective-permute-start.3 = (bf16[2,256,512]{2,1,0:T(8,128)(2,1)S(1)}, bf16[2,256,512]{2,1,0:T(8,128)(2,1)S(1)}, u32[]{:S(2)}, u32[]{:S(2)}) collective-permute-start(bf16[2,256,512]{2,1,0:T(8,128)(2,1)S(1)} %select_select_fusion), channel_id=1, source_target_pairs={{0,4},{4,8},{8,12},{1,5},{5,9},{9,13},{2,6},{6,10},{10,14},{3,7},{... | collective-permute-start | bytes 1572872 | tf_op jit(solution)/shard_map/ppermute | solution.py:22
  19.0 1.6 %collective-permute-done.k_ref.v_ref = bf16[2,256,512]{2,1,0:T(8,128)(2,1)S(1)} collective-permute-done((bf16[2,256,512]{2,1,0:T(8,128)(2,1)S(1)}, bf16[2,256,512]{2,1,0:T(8,128)(2,1)S(1)}, u32[]{:S(2)}, u32[]{:S(2)}) %collective-permute-start) | collective-permute-done | bytes 524320 | tf_op jit(solution)/shard_map/ppermute | solution.py:22
  20.6 0.0 copy-start.1
  20.6 1.3 %collective-permute-start.1 = (bf16[2,256,512]{2,1,0:T(8,128)(2,1)S(1)}, bf16[2,256,512]{2,1,0:T(8,128)(2,1)S(1)}, u32[]{:S(2)}, u32[]{:S(2)}) collective-permute-start(bf16[2,256,512]{2,1,0:T(8,128)(2,1)S(1)} %collective-permute-done.k_ref.v_ref), channel_id=1, source_target_pairs={{0,4},{4,8},{8,12},{1,5},{5,9},{9,13},{2,6},{6,10},{10,14},{3,7},{... | collective-permute-start | bytes 1572872 | tf_op jit(solution)/shard_map/ppermute | solution.py:22
  21.9 1.4 %maximum_select_fusion.k_ref.v_ref = bf16[2,512,512]{2,1,0:T(8,128)(2,1)} fusion(bf16[2,256,512]{2,1,0:T(8,128)(2,1)S(1)} %select_select_fusion, bf16[2,256,512]{2,1,0:T(8,128)(2,1)S(1)} %get-tuple-element.16, pred[]{:T(512)S(6)} %eq.6), kind=kLoop, calls=%fused_computation.2 | loop fusion | flops 4718592 | bytes 2097153 | tf_op jit(solution)/shard_map/jit(_where)/select_n | solution.py:201
  23.3 6.4 %shard_map.82 = (f32[512,8]{1,0:T(8,128)}, f32[512,8]{1,0:T(8,128)}, f32[512,1024]{1,0:T(8,128)}) custom-call(s32[1]{0:T(128)} %bitcast.first_ref, bf16[512,1024]{1,0:T(8,128)(2,1)} %q_ref.9, bf16[2,512,512]{2,1,0:T(8,128)(2,1)} %maximum_select_fusion.k_ref.v_ref, bf16[2,512,512]{2,1,0:T(8,128)(2,1)} %maximum_select_fusion.k_ref.v_ref), custom_call_target="tpu_custom_call" | custom-call | flops 1073741824 | bytes 4194304 | tf_op jit(solution)/shard_map/pallas_call | solution.py:185
  29.7 0.0 copy-done.1
  29.7 5.9 %shard_map.83 = (f32[512,8]{1,0:T(8,128)}, f32[512,8]{1,0:T(8,128)}, f32[512,1024]{1,0:T(8,128)}) custom-call(s32[1]{0:T(128)} %bitcast.first_ref, bf16[512,1024]{1,0:T(8,128)(2,1)} %q_ref.9, bf16[2,256,512]{2,1,0:T(8,128)(2,1)} %copy-done.1, bf16[2,256,512]{2,1,0:T(8,128)(2,1)} %copy-done.1, f32[512,8]{1,0:T(8,128)} %get-tuple-element.18.rest_0_, ...), custom_call_target="tpu_custom_call" | custom-call | flops 536870912 | bytes 5767168 | tf_op jit(solution)/shard_map/pallas_call | solution.py:185
  35.6 0.0 collective-permute-done.3.k_ref.v_ref
  35.6 0.0 copy-start
  35.7 1.3 %collective-permute-start.5 = (bf16[2,256,256]{2,1,0:T(8,128)(2,1)S(1)}, bf16[2,256,256]{2,1,0:T(8,128)(2,1)S(1)}, u32[]{:S(2)}, u32[]{:S(2)}) collective-permute-start(bf16[2,256,256]{2,1,0:T(8,128)(2,1)S(1)} %get-tuple-element.29), channel_id=1, source_target_pairs={{0,4},{4,8},{8,12},{1,5},{5,9},{9,13},{2,6},{6,10},{10,14},{3,7},{... | collective-permute-start | bytes 786440 | tf_op jit(solution)/shard_map/ppermute | solution.py:22
  37.0 1.3 %collective-permute-start.4 = (bf16[2,256,256]{2,1,0:T(8,128)(2,1)S(1)}, bf16[2,256,256]{2,1,0:T(8,128)(2,1)S(1)}, u32[]{:S(2)}, u32[]{:S(2)}) collective-permute-start(bf16[2,256,256]{2,1,0:T(8,128)(2,1)S(1)} %get-tuple-element.30), channel_id=1, source_target_pairs={{0,4},{4,8},{8,12},{1,5},{5,9},{9,13},{2,6},{6,10},{10,14},{3,7},{... | collective-permute-start | bytes 786440 | tf_op jit(solution)/shard_map/ppermute | solution.py:22
  38.3 7.4 %collective-permute-done.1 = bf16[2,256,512]{2,1,0:T(8,128)(2,1)S(1)} collective-permute-done((bf16[2,256,512]{2,1,0:T(8,128)(2,1)S(1)}, bf16[2,256,512]{2,1,0:T(8,128)(2,1)S(1)}, u32[]{:S(2)}, u32[]{:S(2)}) %collective-permute-start.1) | collective-permute-done | bytes 524320 | tf_op jit(solution)/shard_map/ppermute | solution.py:22
  45.7 0.0 copy-done
  45.7 6.0 %shard_map.84 = (f32[512,8]{1,0:T(8,128)}, f32[512,8]{1,0:T(8,128)}, f32[512,1024]{1,0:T(8,128)}) custom-call(s32[1]{0:T(128)} %bitcast.first_ref, bf16[512,1024]{1,0:T(8,128)(2,1)} %q_ref.9, bf16[2,256,512]{2,1,0:T(8,128)(2,1)} %copy-done, bf16[2,256,512]{2,1,0:T(8,128)(2,1)} %copy-done, f32[512,8]{1,0:T(8,128)} %get-tuple-element.21.rest_0_, ...), custom_call_target="tpu_custom_call" | custom-call | flops 536870912 | bytes 5767168 | tf_op jit(solution)/shard_map/pallas_call | solution.py:185
  51.7 0.0 collective-permute-done.5
  51.7 1.0 %maximum_select_fusion.2.k_ref.v_ref = bf16[2,512,256]{2,1,0:T(8,128)(2,1)} fusion(bf16[2,256,256]{2,1,0:T(8,128)(2,1)S(1)} %collective-permute-done.5, bf16[2,256,256]{2,1,0:T(8,128)(2,1)S(1)} %get-tuple-element.27, pred[]{:T(512)S(6)} %eq.6), kind=kLoop, calls=%fused_computation.7 | loop fusion | flops 2359296 | bytes 1048577 | tf_op jit(solution)/shard_map/jit(_where)/select_n | solution.py:201
  52.7 4.2 %shard_map.85.rest_3_ = bf16[512,1024]{1,0:T(8,128)(2,1)} custom-call(s32[1]{0:T(128)} %bitcast.first_ref, bf16[512,1024]{1,0:T(8,128)(2,1)} %q_ref.9, bf16[2,512,256]{2,1,0:T(8,128)(2,1)} %maximum_select_fusion.2.k_ref.v_ref, bf16[2,512,256]{2,1,0:T(8,128)(2,1)} %maximum_select_fusion.2.k_ref.v_ref, f32[512,8]{1,0:T(8,128)} %get-tuple-element.24.rest_0_, ...), custom_call_target="tpu_custom_call" | custom-call | flops 536870912 | bytes 3145728 | tf_op jit(solution)/shard_map/pallas_call | solution.py:185
  56.8 0.0 collective-permute-done.4
  56.8 1.0 %maximum_select_fusion.1.k_ref.v_ref = bf16[2,512,256]{2,1,0:T(8,128)(2,1)} fusion(bf16[2,256,256]{2,1,0:T(8,128)(2,1)S(1)} %collective-permute-done.4, bf16[2,256,256]{2,1,0:T(8,128)(2,1)S(1)} %get-tuple-element.28, pred[]{:T(512)S(6)} %eq.6), kind=kLoop, calls=%fused_computation.6 | loop fusion | flops 2359296 | bytes 1048577 | tf_op jit(solution)/shard_map/jit(_where)/select_n | solution.py:201
  57.8 4.2 %shard_map.86 = bf16[512,1024]{1,0:T(8,128)(2,1)} custom-call(s32[1]{0:T(128)} %bitcast.first_ref, bf16[512,1024]{1,0:T(8,128)(2,1)} %q_ref.9, bf16[2,512,256]{2,1,0:T(8,128)(2,1)} %maximum_select_fusion.1.k_ref.v_ref, bf16[2,512,256]{2,1,0:T(8,128)(2,1)} %maximum_select_fusion.1.k_ref.v_ref, ...), custom_call_target="tpu_custom_call", output_to_operand_aliasing={{}: (7, {})} | custom-call | flops 536870912 | bytes 3145728 | tf_op jit(solution)/shard_map/pallas_call | solution.py:185
  (3 shorter events, 0.1 us)
Async XLA Ops:
  0.0 17.5 %copy-start.3 = (bf16[512,512]{1,0:T(8,128)(2,1)S(1)}, bf16[512,512]{1,0:T(8,128)(2,1)}, u32[]{:S(2)}) copy-start(bf16[512,512]{1,0:T(8,128)(2,1)} %param.9) | copy-start | bytes 1572868
  0.0 17.5 %copy-start.2 = (bf16[512,512]{1,0:T(8,128)(2,1)S(1)}, bf16[512,512]{1,0:T(8,128)(2,1)}, u32[]{:S(2)}) copy-start(bf16[512,512]{1,0:T(8,128)(2,1)} %param.10) | copy-start | bytes 1572868
  3.8 13.7 %collective-permute-start.2 = (bf16[2,256,512]{2,1,0:T(8,128)(2,1)S(1)}, bf16[2,256,512]{2,1,0:T(8,128)(2,1)S(1)}, u32[]{:S(2)}, u32[]{:S(2)}) collective-permute-start(bf16[2,256,512]{2,1,0:T(8,128)(2,1)S(1)} %get-tuple-element.17), channel_id=1, source_target_pairs={{0,2},{2,0},{1,3},{3,1},{4,6},{6,4},{5,7},{7,5},{8,10},{10,8},{9,1... | collective-permute-start | bytes 1572872 | tf_op jit(solution)/shard_map/ppermute | solution.py:197
  5.3 15.3 %collective-permute-start = (bf16[2,256,512]{2,1,0:T(8,128)(2,1)S(1)}, bf16[2,256,512]{2,1,0:T(8,128)(2,1)S(1)}, u32[]{:S(2)}, u32[]{:S(2)}) collective-permute-start(bf16[2,256,512]{2,1,0:T(8,128)(2,1)S(1)} %get-tuple-element.16), channel_id=1, source_target_pairs={{0,4},{4,8},{8,12},{1,5},{5,9},{9,13},{2,6},{6,10},{10,14},{3,7},{... | collective-permute-start | bytes 1572872 | tf_op jit(solution)/shard_map/ppermute | solution.py:22
  17.7 17.9 %collective-permute-start.3 = (bf16[2,256,512]{2,1,0:T(8,128)(2,1)S(1)}, bf16[2,256,512]{2,1,0:T(8,128)(2,1)S(1)}, u32[]{:S(2)}, u32[]{:S(2)}) collective-permute-start(bf16[2,256,512]{2,1,0:T(8,128)(2,1)S(1)} %select_select_fusion), channel_id=1, source_target_pairs={{0,4},{4,8},{8,12},{1,5},{5,9},{9,13},{2,6},{6,10},{10,14},{3,7},{... | collective-permute-start | bytes 1572872 | tf_op jit(solution)/shard_map/ppermute | solution.py:22
  20.6 9.1 %copy-start.1 = (bf16[2,256,512]{2,1,0:T(8,128)(2,1)}, bf16[2,256,512]{2,1,0:T(8,128)(2,1)S(1)}, u32[]{:S(2)}) copy-start(bf16[2,256,512]{2,1,0:T(8,128)(2,1)S(1)} %collective-permute-done.k_ref.v_ref) | copy-start | bytes 1572868
  20.6 25.0 %collective-permute-start.1 = (bf16[2,256,512]{2,1,0:T(8,128)(2,1)S(1)}, bf16[2,256,512]{2,1,0:T(8,128)(2,1)S(1)}, u32[]{:S(2)}, u32[]{:S(2)}) collective-permute-start(bf16[2,256,512]{2,1,0:T(8,128)(2,1)S(1)} %collective-permute-done.k_ref.v_ref), channel_id=1, source_target_pairs={{0,4},{4,8},{8,12},{1,5},{5,9},{9,13},{2,6},{6,10},{10,14},{3,7},{... | collective-permute-start | bytes 1572872 | tf_op jit(solution)/shard_map/ppermute | solution.py:22
  35.6 10.1 %copy-start = (bf16[2,256,512]{2,1,0:T(8,128)(2,1)}, bf16[2,256,512]{2,1,0:T(8,128)(2,1)S(1)}, u32[]{:S(2)}) copy-start(bf16[2,256,512]{2,1,0:T(8,128)(2,1)S(1)} %collective-permute-done.3.k_ref.v_ref) | copy-start | bytes 1572868
  35.7 16.0 %collective-permute-start.5 = (bf16[2,256,256]{2,1,0:T(8,128)(2,1)S(1)}, bf16[2,256,256]{2,1,0:T(8,128)(2,1)S(1)}, u32[]{:S(2)}, u32[]{:S(2)}) collective-permute-start(bf16[2,256,256]{2,1,0:T(8,128)(2,1)S(1)} %get-tuple-element.29), channel_id=1, source_target_pairs={{0,4},{4,8},{8,12},{1,5},{5,9},{9,13},{2,6},{6,10},{10,14},{3,7},{... | collective-permute-start | bytes 786440 | tf_op jit(solution)/shard_map/ppermute | solution.py:22
  37.0 19.9 %collective-permute-start.4 = (bf16[2,256,256]{2,1,0:T(8,128)(2,1)S(1)}, bf16[2,256,256]{2,1,0:T(8,128)(2,1)S(1)}, u32[]{:S(2)}, u32[]{:S(2)}) collective-permute-start(bf16[2,256,256]{2,1,0:T(8,128)(2,1)S(1)} %get-tuple-element.30), channel_id=1, source_target_pairs={{0,4},{4,8},{8,12},{1,5},{5,9},{9,13},{2,6},{6,10},{10,14},{3,7},{... | collective-permute-start | bytes 786440 | tf_op jit(solution)/shard_map/ppermute | solution.py:22

commit v10 on v7

--- a/solution.py
+++ b/solution.py
@@ -137,8 +137,8 @@
     return kernel
 
 
-def attend_chunk(chunk, queries, key_rows, value_rows, first_row, state):
-    key_count, key_cols = key_rows.shape
+def attend_chunk(chunk, queries, pair, first_row, state):
+    key_count, key_cols = pair.shape[1:]
     rows, query_cols = queries.shape
     kv_heads = key_cols // HEAD_DIM
     group = query_cols // key_cols
@@ -148,10 +148,11 @@
     query_block = QUERY_BLOCK if chunk == 1 else MASKED_QUERY_BLOCK
     kernel = chunk_kernel(chunk, first, last, rows, key_count, query_block, group)
     q_spec = pl.BlockSpec((rows, group * HEAD_DIM), lambda h, f: (0, h))
-    kv_spec = pl.BlockSpec((key_count, HEAD_DIM), lambda h, f: (0, h))
+    k_spec = pl.BlockSpec((None, key_count, HEAD_DIM), lambda h, f: (0, 0, h))
+    v_spec = pl.BlockSpec((None, key_count, HEAD_DIM), lambda h, f: (1, 0, h))
     stat_spec = pl.BlockSpec((rows, heads), lambda h, f: (0, 0))
     state_specs = [stat_spec, stat_spec, q_spec]
-    in_specs = [q_spec, kv_spec, kv_spec] + ([] if first else state_specs)
+    in_specs = [q_spec, k_spec, v_spec] + ([] if first else state_specs)
     stat_shape = jax.ShapeDtypeStruct((rows, heads), jnp.float32)
     if last:
         out_specs = q_spec
@@ -177,7 +178,7 @@
         out_shape=out_shape,
         cost_estimate=cost,
         compiler_params=pltpu.CompilerParams(dimension_semantics=("arbitrary",)),
-    )(first_row.reshape(1), queries, key_rows, value_rows, *([] if first else state))
+    )(first_row.reshape(1), queries, pair, pair, *([] if first else state))
 
 
 def swap_variant(half):
@@ -219,10 +220,11 @@
         corrupt_other = jnp.where(variant_index == 0, hi, lo)
         inside_own = jnp.where(variant_index == 0, inside_lo, inside_hi)
         inside_other = jnp.where(variant_index == 0, inside_hi, inside_lo)
+        clean_own = lax.optimization_barrier(clean_own)
+        clean_other = swap_variant(clean_own)
+        corrupt_other, inside_other = lax.optimization_barrier((corrupt_other, inside_other))
         own_half = jnp.where(inside_own[None, :, None], clean_own, corrupt_own)
-        own_half, clean_own = lax.optimization_barrier((own_half, clean_own))
         near_own = shifted(own_half, "seq", 1)
-        clean_other = swap_variant(clean_own)
         other_half = jnp.where(inside_other[None, :, None], clean_other, corrupt_other)
         near_other = shifted(other_half, "seq", 1)
         far_own = shifted(near_own, "seq", 1)
@@ -230,10 +232,10 @@
         patched = halves_in_order(own_half, other_half, variant_index)
         far = halves_in_order(far_own, far_other, variant_index)
         near_parts = (near_own, near_other)
-    state = attend_chunk(2, queries, patched[0], patched[1], first_row, None)
+    state = attend_chunk(2, queries, patched, first_row, None)
     for part in near_parts:
-        state = attend_chunk(1, queries, part[0], part[1], first_row, state)
-    result = attend_chunk(0, queries, far[0], far[1], first_row, state)
+        state = attend_chunk(1, queries, part, first_row, state)
+    result = attend_chunk(0, queries, far, first_row, state)
     return result[None]
 
 

time: 63.5 us -> 66.1 us (1.041)
  the two profiles are of different devices: /device:TPU:22 before, /device:TPU:16 now
where the time goes in v10:
time: 66.1 us; the launch traced here: 65.5 us
  Pallas kernels  24.9 us (38%)
  waiting for transfers between devices  17.3 us (26%)
  starting transfers between devices  15.5 us (23%)
  other arithmetic  7.08 us (11%)
  between operations  0.73 us (1%)
    pallas_call x4, Pallas kernels, attend_chunk(): pl.pallas_call(kernel, grid_spec=grid_spec, out_shape=out_shape, cost_est...  24.9 us
    ppermute x4, starting transfers between devices, shifted(): return lax.ppermute(shard, axis, pairs)  13.9 us
    ppermute x4, waiting for transfers between devices, shifted(): return lax.ppermute(shard, axis, pairs)  12.4 us
    ppermute x1, waiting for transfers between devices, swap_variant(): lax.ppermute(half, 'variant', [(i, (i + 1) % variants) for i in range(var...  4.94 us
    select_n x2, other arithmetic, halves_in_order(): jnp.where(variant_index == 0, jnp.concatenate([own, other], axis=1), jnp....  2.8 us
    select_n x1, other arithmetic, shard_body(): own_half = jnp.where(inside_own[None, :, None], clean_own, corrupt_own)  1.64 us
    ppermute x1, starting transfers between devices, swap_variant(): lax.ppermute(half, 'variant', [(i, (i + 1) % variants) for i in range(var...  1.56 us
  transfers between devices with their start and end apart: 5, of which 3 were waited for; matrix products, arithmetic and copies ran while one was open for 7% of the time, Pallas kernels for 28%

profile of v10, /device:TPU:16, one launch (start us, length us, event | category | flops | bytes accessed | tf_op | source)
XLA Modules:
  0.0 65.5 jit_solution(440597111903634480)
XLA Ops:
  0.0 1.1 %pad_maximum_fusion.1 = bf16[2,256,512]{2,1,0:T(8,128)(2,1)S(1)} fusion(bf16[1,256,512]{2,1,0:T(8,128)(2,1)} %bitcast.15, bf16[1,256,512]{2,1,0:T(8,128)(2,1)} %bitcast.16), kind=kLoop, calls=%fused_computation.6 | loop fusion | flops 262144 | bytes 1048576 | tf_op jit(solution)/shard_map/stack | solution.py:207
  1.1 1.6 %collective-permute-start.2 = (bf16[2,256,512]{2,1,0:T(8,128)(2,1)S(1)}, bf16[2,256,512]{2,1,0:T(8,128)(2,1)S(1)}, u32[]{:S(2)}, u32[]{:S(2)}) collective-permute-start(bf16[2,256,512]{2,1,0:T(8,128)(2,1)S(1)} %pad_maximum_fusion.1), channel_id=1, source_target_pairs={{0,2},{2,0},{1,3},{3,1},{4,6},{6,4},{5,7},{7,5},{8,10},{10,8},{9,1... | collective-permute-start | bytes 1572872 | tf_op jit(solution)/shard_map/ppermute | solution.py:186
  3.3 0.7 %add_bitcast_fusion = s32[2]{0:T(128)S(1)} fusion(s32[1,2]{1,0:T(1,128)} %param.14, s32[1,2]{1,0:T(1,128)} %param.15), kind=kLoop, calls=%fused_computation.13 | loop fusion | flops 2 | bytes 24 | tf_op jit(solution)/shard_map/lt | solution.py:203
  4.0 0.7 %and_reduce_fusion = pred[512]{0:T(512)(128)(4,1)S(1)} fusion(pred[]{:T(512)} %bitcast.5, s32[2]{0:T(128)S(1)} %add_bitcast_fusion, s32[2]{0:T(128)} %bitcast.17), kind=kLoop, calls=%fused_computation.10 | loop fusion | flops 4608 | bytes 529 | tf_op jit(solution)/shard_map/reduce_or | solution.py:205
  4.7 1.6 %select_select_fusion = (bf16[2,256,512]{2,1,0:T(8,128)(2,1)S(1)}, bf16[2,256,512]{2,1,0:T(8,128)(2,1)S(1)}) fusion(bf16[2,256,512]{2,1,0:T(8,128)(2,1)S(1)} %pad_maximum_fusion.1, pred[256]{0:T(512)(128)(4,1)S(1)} %get-tuple-element.29, pred[]{:T(512)S(6)} %eq.6, bf16[1,512,512]{2,1,0:T(8,128)(2,1)} %bitcast.13, bf16[1,512,512]{2,1,0:T(8,128)(2,1)} %bitcast.14), kind=kLoop, calls=%fused_computation.7 | loop fusion | flops 3932160 | bytes 2621697 | tf_op jit(solution)/shard_map/jit(_where)/select_n | solution.py:226
  6.4 3.5 %collective-permute-start = (bf16[2,256,512]{2,1,0:T(8,128)(2,1)S(1)}, bf16[2,256,512]{2,1,0:T(8,128)(2,1)S(1)}, u32[]{:S(2)}, u32[]{:S(2)}) collective-permute-start(bf16[2,256,512]{2,1,0:T(8,128)(2,1)S(1)} %get-tuple-element.27), channel_id=1, source_target_pairs={{0,4},{4,8},{8,12},{1,5},{5,9},{9,13},{2,6},{6,10},{10,14},{3,7},{... | collective-permute-start | bytes 1572872 | tf_op jit(solution)/shard_map/ppermute | solution.py:22
  9.9 4.9 %collective-permute-done.2 = bf16[2,256,512]{2,1,0:T(8,128)(2,1)S(1)} collective-permute-done((bf16[2,256,512]{2,1,0:T(8,128)(2,1)S(1)}, bf16[2,256,512]{2,1,0:T(8,128)(2,1)S(1)}, u32[]{:S(2)}, u32[]{:S(2)}) %collective-permute-start.2) | collective-permute-done | bytes 524320 | tf_op jit(solution)/shard_map/ppermute | solution.py:186
  14.8 0.1 broadcast_select_fusion
  14.9 3.5 %collective-permute-start.3 = (bf16[2,256,512]{2,1,0:T(8,128)(2,1)S(1)}, bf16[2,256,512]{2,1,0:T(8,128)(2,1)S(1)}, u32[]{:S(2)}, u32[]{:S(2)}) collective-permute-start(bf16[2,256,512]{2,1,0:T(8,128)(2,1)S(1)} %broadcast_select_fusion), channel_id=1, source_target_pairs={{0,4},{4,8},{8,12},{1,5},{5,9},{9,13},{2,6},{6,10},{10,14},{3,7},{... | collective-permute-start | bytes 1572872 | tf_op jit(solution)/shard_map/ppermute | solution.py:22
  18.4 4.6 %collective-permute-done.k_ref.v_ref = bf16[2,256,512]{2,1,0:T(8,128)(2,1)S(1)} collective-permute-done((bf16[2,256,512]{2,1,0:T(8,128)(2,1)S(1)}, bf16[2,256,512]{2,1,0:T(8,128)(2,1)S(1)}, u32[]{:S(2)}, u32[]{:S(2)}) %collective-permute-start) | collective-permute-done | bytes 524320 | tf_op jit(solution)/shard_map/ppermute | solution.py:22
  23.1 0.0 copy-start
  23.1 3.5 %collective-permute-start.1 = (bf16[2,256,512]{2,1,0:T(8,128)(2,1)S(1)}, bf16[2,256,512]{2,1,0:T(8,128)(2,1)S(1)}, u32[]{:S(2)}, u32[]{:S(2)}) collective-permute-start(bf16[2,256,512]{2,1,0:T(8,128)(2,1)S(1)} %collective-permute-done.k_ref.v_ref), channel_id=1, source_target_pairs={{0,4},{4,8},{8,12},{1,5},{5,9},{9,13},{2,6},{6,10},{10,14},{3,7},{... | collective-permute-start | bytes 1572872 | tf_op jit(solution)/shard_map/ppermute | solution.py:22
  26.5 7.8 %collective-permute-done.3.k_ref.v_ref = bf16[2,256,512]{2,1,0:T(8,128)(2,1)S(1)} collective-permute-done((bf16[2,256,512]{2,1,0:T(8,128)(2,1)S(1)}, bf16[2,256,512]{2,1,0:T(8,128)(2,1)S(1)}, u32[]{:S(2)}, u32[]{:S(2)}) %collective-permute-start.3) | collective-permute-done | bytes 524320 | tf_op jit(solution)/shard_map/ppermute | solution.py:22
  34.3 0.0 copy-start.1
  34.3 3.5 %collective-permute-start.4 = (bf16[2,256,512]{2,1,0:T(8,128)(2,1)S(1)}, bf16[2,256,512]{2,1,0:T(8,128)(2,1)S(1)}, u32[]{:S(2)}, u32[]{:S(2)}) collective-permute-start(bf16[2,256,512]{2,1,0:T(8,128)(2,1)S(1)} %collective-permute-done.3.k_ref.v_ref), channel_id=1, source_target_pairs={{0,4},{4,8},{8,12},{1,5},{5,9},{9,13},{2,6},{6,10},{10,14},{3,7},{... | collective-permute-start | bytes 1572872 | tf_op jit(solution)/shard_map/ppermute | solution.py:22
  37.8 1.4 %maximum_select_fusion.1.k_ref.v_ref = bf16[2,512,512]{2,1,0:T(8,128)(2,1)} fusion(bf16[2,256,512]{2,1,0:T(8,128)(2,1)S(1)} %broadcast_select_fusion, bf16[2,256,512]{2,1,0:T(8,128)(2,1)S(1)} %get-tuple-element.27, pred[]{:T(512)S(6)} %eq.6), kind=kLoop, calls=%fused_computation.3 | loop fusion | flops 4718592 | bytes 2097153 | tf_op jit(solution)/shard_map/jit(_where)/select_n | solution.py:190
  39.2 6.4 %shard_map.82 = (f32[512,8]{1,0:T(8,128)}, f32[512,8]{1,0:T(8,128)}, f32[512,1024]{1,0:T(8,128)}) custom-call(s32[1]{0:T(128)} %bitcast.first_ref, bf16[512,1024]{1,0:T(8,128)(2,1)} %q_ref.7, bf16[2,512,512]{2,1,0:T(8,128)(2,1)} %maximum_select_fusion.1.k_ref.v_ref, bf16[2,512,512]{2,1,0:T(8,128)(2,1)} %maximum_select_fusion.1.k_ref.v_ref), custom_call_target="tpu_custom_call" | custom-call | flops 1073741824 | bytes 4194304 | tf_op jit(solution)/shard_map/pallas_call | solution.py:175
  45.6 0.0 copy-done
  45.6 0.0 copy-done.1
  45.6 6.0 %shard_map.83 = (f32[512,8]{1,0:T(8,128)}, f32[512,8]{1,0:T(8,128)}, f32[512,1024]{1,0:T(8,128)}) custom-call(s32[1]{0:T(128)} %bitcast.first_ref, bf16[512,1024]{1,0:T(8,128)(2,1)} %q_ref.7, bf16[2,256,512]{2,1,0:T(8,128)(2,1)} %copy-done, bf16[2,256,512]{2,1,0:T(8,128)(2,1)} %copy-done, f32[512,8]{1,0:T(8,128)} %get-tuple-element.18.rest_0_, ...), custom_call_target="tpu_custom_call" | custom-call | flops 536870912 | bytes 5767168 | tf_op jit(solution)/shard_map/pallas_call | solution.py:175
  51.6 6.0 %shard_map.84 = (f32[512,8]{1,0:T(8,128)}, f32[512,8]{1,0:T(8,128)}, f32[512,1024]{1,0:T(8,128)}) custom-call(s32[1]{0:T(128)} %bitcast.first_ref, bf16[512,1024]{1,0:T(8,128)(2,1)} %q_ref.7, bf16[2,256,512]{2,1,0:T(8,128)(2,1)} %copy-done.1, bf16[2,256,512]{2,1,0:T(8,128)(2,1)} %copy-done.1, f32[512,8]{1,0:T(8,128)} %get-tuple-element.21.rest_0_, ...), custom_call_target="tpu_custom_call" | custom-call | flops 536870912 | bytes 5767168 | tf_op jit(solution)/shard_map/pallas_call | solution.py:175
  57.6 0.0 collective-permute-done.1
  57.6 0.0 collective-permute-done.4
  57.6 1.4 %maximum_select_fusion.k_ref.v_ref = bf16[2,512,512]{2,1,0:T(8,128)(2,1)} fusion(bf16[2,256,512]{2,1,0:T(8,128)(2,1)S(1)} %collective-permute-done.4, bf16[2,256,512]{2,1,0:T(8,128)(2,1)S(1)} %collective-permute-done.1, pred[]{:T(512)S(6)} %eq.6), kind=kLoop, calls=%fused_computation.2 | loop fusion | flops 4718592 | bytes 2097153 | tf_op jit(solution)/shard_map/jit(_where)/select_n | solution.py:190
  59.0 6.5 %shard_map.85 = bf16[512,1024]{1,0:T(8,128)(2,1)} custom-call(s32[1]{0:T(128)} %bitcast.first_ref, bf16[512,1024]{1,0:T(8,128)(2,1)} %q_ref.7, bf16[2,512,512]{2,1,0:T(8,128)(2,1)} %maximum_select_fusion.k_ref.v_ref, bf16[2,512,512]{2,1,0:T(8,128)(2,1)} %maximum_select_fusion.k_ref.v_ref, f32[512,8]{1,0:T(8,128)} %get-tuple-element.24.rest_0_, ...), custom_call_target="tpu_custom_call" | custom-call | flops 1073741824 | bytes 6291456 | tf_op jit(solution)/shard_map/pallas_call | solution.py:175
  (1 shorter events, 0.0 us)
Async XLA Ops:
  1.1 13.7 %collective-permute-start.2 = (bf16[2,256,512]{2,1,0:T(8,128)(2,1)S(1)}, bf16[2,256,512]{2,1,0:T(8,128)(2,1)S(1)}, u32[]{:S(2)}, u32[]{:S(2)}) collective-permute-start(bf16[2,256,512]{2,1,0:T(8,128)(2,1)S(1)} %pad_maximum_fusion.1), channel_id=1, source_target_pairs={{0,2},{2,0},{1,3},{3,1},{4,6},{6,4},{5,7},{7,5},{8,10},{10,8},{9,1... | collective-permute-start | bytes 1572872 | tf_op jit(solution)/shard_map/ppermute | solution.py:186
  6.4 16.7 %collective-permute-start = (bf16[2,256,512]{2,1,0:T(8,128)(2,1)S(1)}, bf16[2,256,512]{2,1,0:T(8,128)(2,1)S(1)}, u32[]{:S(2)}, u32[]{:S(2)}) collective-permute-start(bf16[2,256,512]{2,1,0:T(8,128)(2,1)S(1)} %get-tuple-element.27), channel_id=1, source_target_pairs={{0,4},{4,8},{8,12},{1,5},{5,9},{9,13},{2,6},{6,10},{10,14},{3,7},{... | collective-permute-start | bytes 1572872 | tf_op jit(solution)/shard_map/ppermute | solution.py:22
  14.9 19.4 %collective-permute-start.3 = (bf16[2,256,512]{2,1,0:T(8,128)(2,1)S(1)}, bf16[2,256,512]{2,1,0:T(8,128)(2,1)S(1)}, u32[]{:S(2)}, u32[]{:S(2)}) collective-permute-start(bf16[2,256,512]{2,1,0:T(8,128)(2,1)S(1)} %broadcast_select_fusion), channel_id=1, source_target_pairs={{0,4},{4,8},{8,12},{1,5},{5,9},{9,13},{2,6},{6,10},{10,14},{3,7},{... | collective-permute-start | bytes 1572872 | tf_op jit(solution)/shard_map/ppermute | solution.py:22
  23.1 22.5 %copy-start = (bf16[2,256,512]{2,1,0:T(8,128)(2,1)}, bf16[2,256,512]{2,1,0:T(8,128)(2,1)S(1)}, u32[]{:S(2)}) copy-start(bf16[2,256,512]{2,1,0:T(8,128)(2,1)S(1)} %collective-permute-done.k_ref.v_ref) | copy-start | bytes 1572868
  23.1 34.5 %collective-permute-start.1 = (bf16[2,256,512]{2,1,0:T(8,128)(2,1)S(1)}, bf16[2,256,512]{2,1,0:T(8,128)(2,1)S(1)}, u32[]{:S(2)}, u32[]{:S(2)}) collective-permute-start(bf16[2,256,512]{2,1,0:T(8,128)(2,1)S(1)} %collective-permute-done.k_ref.v_ref), channel_id=1, source_target_pairs={{0,4},{4,8},{8,12},{1,5},{5,9},{9,13},{2,6},{6,10},{10,14},{3,7},{... | collective-permute-start | bytes 1572872 | tf_op jit(solution)/shard_map/ppermute | solution.py:22
  34.3 11.3 %copy-start.1 = (bf16[2,256,512]{2,1,0:T(8,128)(2,1)}, bf16[2,256,512]{2,1,0:T(8,128)(2,1)S(1)}, u32[]{:S(2)}) copy-start(bf16[2,256,512]{2,1,0:T(8,128)(2,1)S(1)} %collective-permute-done.3.k_ref.v_ref) | copy-start | bytes 1572868
  34.3 23.3 %collective-permute-start.4 = (bf16[2,256,512]{2,1,0:T(8,128)(2,1)S(1)}, bf16[2,256,512]{2,1,0:T(8,128)(2,1)S(1)}, u32[]{:S(2)}, u32[]{:S(2)}) collective-permute-start(bf16[2,256,512]{2,1,0:T(8,128)(2,1)S(1)} %collective-permute-done.3.k_ref.v_ref), channel_id=1, source_target_pairs={{0,4},{4,8},{8,12},{1,5},{5,9},{9,13},{2,6},{6,10},{10,14},{3,7},{... | collective-permute-start | bytes 1572872 | tf_op jit(solution)/shard_map/ppermute | solution.py:22

commit v11 on v10

--- a/solution.py
+++ b/solution.py
@@ -230,7 +230,10 @@
         far_own = shifted(near_own, "seq", 1)
         far_other = shifted(near_other, "seq", 1)
         patched = halves_in_order(own_half, other_half, variant_index)
-        far = halves_in_order(far_own, far_other, variant_index)
+        far_placed = lax.dynamic_update_slice_in_dim(
+            jnp.zeros(far_own.shape[:1] + (row_count,) + far_own.shape[2:], far_own.dtype),
+            far_own, half * variant_index, 1)
+        far = lax.dynamic_update_slice_in_dim(far_placed, far_other, half * (1 - variant_index), 1)
         near_parts = (near_own, near_other)
     state = attend_chunk(2, queries, patched, first_row, None)
     for part in near_parts:

time: 66.1 us -> 65.9 us (level)
  other arithmetic: 7.08 us -> 5.68 us
  local copies, waits for them, and re-layouts: 0.01 us -> 1.14 us
    select_n x2 -> x1, other arithmetic: 2.8 us -> 1.4 us  [halves_in_order(): jnp.where(variant_index == 0, jnp.concatenate([own, other], axis=1), jnp....]
    unnamed x4 -> x6, local copies, waits for them, and re-layouts: 0.01 us -> 0.98 us
where the time goes in v11:
time: 65.9 us; the launch traced here: 65.3 us
  Pallas kernels  24.9 us (38%)
  waiting for transfers between devices  17.3 us (26%)
  starting transfers between devices  15.5 us (24%)
  other arithmetic  5.68 us (9%)
  local copies, waits for them, and re-layouts  1.14 us (2%)
  between operations  0.77 us (1%)
    pallas_call x4, Pallas kernels, attend_chunk(): pl.pallas_call(kernel, grid_spec=grid_spec, out_shape=out_shape, cost_est...  24.9 us
    ppermute x4, starting transfers between devices, shifted(): return lax.ppermute(shard, axis, pairs)  13.9 us
    ppermute x4, waiting for transfers between devices, shifted(): return lax.ppermute(shard, axis, pairs)  12.4 us
    ppermute x1, waiting for transfers between devices, swap_variant(): lax.ppermute(half, 'variant', [(i, (i + 1) % variants) for i in range(var...  4.95 us
    select_n x1, other arithmetic, shard_body(): corrupt_other = jnp.where(variant_index == 0, hi, lo)  1.64 us
    ppermute x1, starting transfers between devices, swap_variant(): lax.ppermute(half, 'variant', [(i, (i + 1) % variants) for i in range(var...  1.56 us
    select_n x1, other arithmetic, halves_in_order(): jnp.where(variant_index == 0, jnp.concatenate([own, other], axis=1), jnp....  1.4 us
  transfers between devices with their start and end apart: 5, of which 3 were waited for; matrix products, arithmetic and copies ran while one was open for 7% of the time, Pallas kernels for 28%

profile of v11, /device:TPU:16, one launch (start us, length us, event | category | flops | bytes accessed | tf_op | source)
XLA Modules:
  0.0 65.3 jit_solution(11323144736950805295)
XLA Ops:
  0.0 1.1 %pad_maximum_fusion.1 = bf16[2,256,512]{2,1,0:T(8,128)(2,1)S(1)} fusion(bf16[1,256,512]{2,1,0:T(8,128)(2,1)} %bitcast.15, bf16[1,256,512]{2,1,0:T(8,128)(2,1)} %bitcast.16), kind=kLoop, calls=%fused_computation.5 | loop fusion | flops 262144 | bytes 1048576 | tf_op jit(solution)/shard_map/stack | solution.py:207
  1.1 1.6 %collective-permute-start.2 = (bf16[2,256,512]{2,1,0:T(8,128)(2,1)S(1)}, bf16[2,256,512]{2,1,0:T(8,128)(2,1)S(1)}, u32[]{:S(2)}, u32[]{:S(2)}) collective-permute-start(bf16[2,256,512]{2,1,0:T(8,128)(2,1)S(1)} %pad_maximum_fusion.1), channel_id=1, source_target_pairs={{0,2},{2,0},{1,3},{3,1},{4,6},{6,4},{5,7},{7,5},{8,10},{10,8},{9,1... | collective-permute-start | bytes 1572872 | tf_op jit(solution)/shard_map/ppermute | solution.py:186
  3.3 0.7 %add_bitcast_fusion = s32[2]{0:T(128)S(1)} fusion(s32[1,2]{1,0:T(1,128)} %param.14, s32[1,2]{1,0:T(1,128)} %param.15), kind=kLoop, calls=%fused_computation.12 | loop fusion | flops 2 | bytes 24 | tf_op jit(solution)/shard_map/lt | solution.py:203
  4.0 0.7 %and_reduce_fusion = pred[512]{0:T(512)(128)(4,1)S(1)} fusion(pred[]{:T(512)} %bitcast.5, s32[2]{0:T(128)S(1)} %add_bitcast_fusion, s32[2]{0:T(128)} %bitcast.17), kind=kLoop, calls=%fused_computation.9 | loop fusion | flops 4608 | bytes 529 | tf_op jit(solution)/shard_map/reduce_or | solution.py:205
  4.7 1.6 %broadcast_select_fusion.1 = (bf16[2,256,512]{2,1,0:T(8,128)(2,1)S(1)}, bf16[2,256,512]{2,1,0:T(8,128)(2,1)S(1)}) fusion(pred[]{:T(512)S(6)} %eq.6, bf16[1,512,512]{2,1,0:T(8,128)(2,1)} %bitcast.13, bf16[1,512,512]{2,1,0:T(8,128)(2,1)} %bitcast.14, bf16[2,256,512]{2,1,0:T(8,128)(2,1)S(1)} %pad_maximum_fusion.1, pred[256]{0:T(512)(128)(4,1)S(1)} %get-tuple-element.30), kind=kLoop, calls=%fused_computation.8 | loop fusion | flops 3932160 | bytes 2621697 | tf_op jit(solution)/shard_map/jit(_where)/select_n | solution.py:220
  6.4 3.5 %collective-permute-start = (bf16[2,256,512]{2,1,0:T(8,128)(2,1)S(1)}, bf16[2,256,512]{2,1,0:T(8,128)(2,1)S(1)}, u32[]{:S(2)}, u32[]{:S(2)}) collective-permute-start(bf16[2,256,512]{2,1,0:T(8,128)(2,1)S(1)} %get-tuple-element.28), channel_id=1, source_target_pairs={{0,4},{4,8},{8,12},{1,5},{5,9},{9,13},{2,6},{6,10},{10,14},{3,7},{... | collective-permute-start | bytes 1572872 | tf_op jit(solution)/shard_map/ppermute | solution.py:22
  9.9 4.9 %collective-permute-done.2 = bf16[2,256,512]{2,1,0:T(8,128)(2,1)S(1)} collective-permute-done((bf16[2,256,512]{2,1,0:T(8,128)(2,1)S(1)}, bf16[2,256,512]{2,1,0:T(8,128)(2,1)S(1)}, u32[]{:S(2)}, u32[]{:S(2)}) %collective-permute-start.2) | collective-permute-done | bytes 524320 | tf_op jit(solution)/shard_map/ppermute | solution.py:186
  14.8 0.1 broadcast_select_fusion
  14.9 3.5 %collective-permute-start.3 = (bf16[2,256,512]{2,1,0:T(8,128)(2,1)S(1)}, bf16[2,256,512]{2,1,0:T(8,128)(2,1)S(1)}, u32[]{:S(2)}, u32[]{:S(2)}) collective-permute-start(bf16[2,256,512]{2,1,0:T(8,128)(2,1)S(1)} %broadcast_select_fusion), channel_id=1, source_target_pairs={{0,4},{4,8},{8,12},{1,5},{5,9},{9,13},{2,6},{6,10},{10,14},{3,7},{... | collective-permute-start | bytes 1572872 | tf_op jit(solution)/shard_map/ppermute | solution.py:22
  18.4 4.6 %collective-permute-done.k_ref.v_ref = bf16[2,256,512]{2,1,0:T(8,128)(2,1)S(1)} collective-permute-done((bf16[2,256,512]{2,1,0:T(8,128)(2,1)S(1)}, bf16[2,256,512]{2,1,0:T(8,128)(2,1)S(1)}, u32[]{:S(2)}, u32[]{:S(2)}) %collective-permute-start) | collective-permute-done | bytes 524320 | tf_op jit(solution)/shard_map/ppermute | solution.py:22
  23.1 0.0 copy-start.1
  23.1 3.5 %collective-permute-start.1 = (bf16[2,256,512]{2,1,0:T(8,128)(2,1)S(1)}, bf16[2,256,512]{2,1,0:T(8,128)(2,1)S(1)}, u32[]{:S(2)}, u32[]{:S(2)}) collective-permute-start(bf16[2,256,512]{2,1,0:T(8,128)(2,1)S(1)} %collective-permute-done.k_ref.v_ref), channel_id=1, source_target_pairs={{0,4},{4,8},{8,12},{1,5},{5,9},{9,13},{2,6},{6,10},{10,14},{3,7},{... | collective-permute-start | bytes 1572872 | tf_op jit(solution)/shard_map/ppermute | solution.py:22
  26.5 7.8 %collective-permute-done.3.k_ref.v_ref = bf16[2,256,512]{2,1,0:T(8,128)(2,1)S(1)} collective-permute-done((bf16[2,256,512]{2,1,0:T(8,128)(2,1)S(1)}, bf16[2,256,512]{2,1,0:T(8,128)(2,1)S(1)}, u32[]{:S(2)}, u32[]{:S(2)}) %collective-permute-start.3) | collective-permute-done | bytes 524320 | tf_op jit(solution)/shard_map/ppermute | solution.py:22
  34.3 0.0 copy-start.2
  34.3 3.5 %collective-permute-start.4 = (bf16[2,256,512]{2,1,0:T(8,128)(2,1)S(1)}, bf16[2,256,512]{2,1,0:T(8,128)(2,1)S(1)}, u32[]{:S(2)}, u32[]{:S(2)}) collective-permute-start(bf16[2,256,512]{2,1,0:T(8,128)(2,1)S(1)} %collective-permute-done.3.k_ref.v_ref), channel_id=1, source_target_pairs={{0,4},{4,8},{8,12},{1,5},{5,9},{9,13},{2,6},{6,10},{10,14},{3,7},{... | collective-permute-start | bytes 1572872 | tf_op jit(solution)/shard_map/ppermute | solution.py:22
  37.8 1.4 %maximum_select_fusion.k_ref.v_ref = bf16[2,512,512]{2,1,0:T(8,128)(2,1)} fusion(bf16[2,256,512]{2,1,0:T(8,128)(2,1)S(1)} %broadcast_select_fusion, bf16[2,256,512]{2,1,0:T(8,128)(2,1)S(1)} %get-tuple-element.28, pred[]{:T(512)S(6)} %eq.6), kind=kLoop, calls=%fused_computation.2 | loop fusion | flops 4718592 | bytes 2097153 | tf_op jit(solution)/shard_map/jit(_where)/select_n | solution.py:190
  39.2 6.4 %shard_map.82 = (f32[512,8]{1,0:T(8,128)}, f32[512,8]{1,0:T(8,128)}, f32[512,1024]{1,0:T(8,128)}) custom-call(s32[1]{0:T(128)} %bitcast.first_ref, bf16[512,1024]{1,0:T(8,128)(2,1)} %q_ref.7, bf16[2,512,512]{2,1,0:T(8,128)(2,1)} %maximum_select_fusion.k_ref.v_ref, bf16[2,512,512]{2,1,0:T(8,128)(2,1)} %maximum_select_fusion.k_ref.v_ref), custom_call_target="tpu_custom_call" | custom-call | flops 1073741824 | bytes 4194304 | tf_op jit(solution)/shard_map/pallas_call | solution.py:175
  45.6 0.0 copy-done.1
  45.6 0.0 copy-done.2
  45.6 6.0 %shard_map.83 = (f32[512,8]{1,0:T(8,128)}, f32[512,8]{1,0:T(8,128)}, f32[512,1024]{1,0:T(8,128)}) custom-call(s32[1]{0:T(128)} %bitcast.first_ref, bf16[512,1024]{1,0:T(8,128)(2,1)} %q_ref.7, bf16[2,256,512]{2,1,0:T(8,128)(2,1)} %copy-done.1, bf16[2,256,512]{2,1,0:T(8,128)(2,1)} %copy-done.1, f32[512,8]{1,0:T(8,128)} %get-tuple-element.18.rest_0_, ...), custom_call_target="tpu_custom_call" | custom-call | flops 536870912 | bytes 5767168 | tf_op jit(solution)/shard_map/pallas_call | solution.py:175
  51.5 6.0 %shard_map.84 = (f32[512,8]{1,0:T(8,128)}, f32[512,8]{1,0:T(8,128)}, f32[512,1024]{1,0:T(8,128)}) custom-call(s32[1]{0:T(128)} %bitcast.first_ref, bf16[512,1024]{1,0:T(8,128)(2,1)} %q_ref.7, bf16[2,256,512]{2,1,0:T(8,128)(2,1)} %copy-done.2, bf16[2,256,512]{2,1,0:T(8,128)(2,1)} %copy-done.2, f32[512,8]{1,0:T(8,128)} %get-tuple-element.21.rest_0_, ...), custom_call_target="tpu_custom_call" | custom-call | flops 536870912 | bytes 5767168 | tf_op jit(solution)/shard_map/pallas_call | solution.py:175
  57.5 0.0 collective-permute-done.1
  57.5 0.1 broadcast_in_dim.24
  57.7 0.0 collective-permute-done.4
  57.7 0.0 copy-start
  57.7 1.0 %copy-done = bf16[2,512,512]{2,1,0:T(8,128)(2,1)} copy-done((bf16[2,512,512]{2,1,0:T(8,128)(2,1)}, bf16[2,512,512]{2,1,0:T(8,128)(2,1)S(1)}, u32[]{:S(2)}) %copy-start) | copy-done | bytes 1048600
  58.7 6.6 %shard_map.85 = bf16[512,1024]{1,0:T(8,128)(2,1)} custom-call(s32[1]{0:T(128)} %bitcast.first_ref, bf16[512,1024]{1,0:T(8,128)(2,1)} %q_ref.7, bf16[2,512,512]{2,1,0:T(8,128)(2,1)} %copy-done, bf16[2,512,512]{2,1,0:T(8,128)(2,1)} %copy-done, f32[512,8]{1,0:T(8,128)} %get-tuple-element.24.rest_0_, f32[512,8]{1,0:T(8,128)} %get-tuple-element.25.rest_1_, ...), custom_call_target="tpu_custom_call" | custom-call | flops 1073741824 | bytes 6291456 | tf_op jit(solution)/shard_map/pallas_call | solution.py:175
  (3 shorter events, 0.1 us)
Async XLA Ops:
  1.1 13.7 %collective-permute-start.2 = (bf16[2,256,512]{2,1,0:T(8,128)(2,1)S(1)}, bf16[2,256,512]{2,1,0:T(8,128)(2,1)S(1)}, u32[]{:S(2)}, u32[]{:S(2)}) collective-permute-start(bf16[2,256,512]{2,1,0:T(8,128)(2,1)S(1)} %pad_maximum_fusion.1), channel_id=1, source_target_pairs={{0,2},{2,0},{1,3},{3,1},{4,6},{6,4},{5,7},{7,5},{8,10},{10,8},{9,1... | collective-permute-start | bytes 1572872 | tf_op jit(solution)/shard_map/ppermute | solution.py:186
  6.4 16.7 %collective-permute-start = (bf16[2,256,512]{2,1,0:T(8,128)(2,1)S(1)}, bf16[2,256,512]{2,1,0:T(8,128)(2,1)S(1)}, u32[]{:S(2)}, u32[]{:S(2)}) collective-permute-start(bf16[2,256,512]{2,1,0:T(8,128)(2,1)S(1)} %get-tuple-element.28), channel_id=1, source_target_pairs={{0,4},{4,8},{8,12},{1,5},{5,9},{9,13},{2,6},{6,10},{10,14},{3,7},{... | collective-permute-start | bytes 1572872 | tf_op jit(solution)/shard_map/ppermute | solution.py:22
  14.9 19.3 %collective-permute-start.3 = (bf16[2,256,512]{2,1,0:T(8,128)(2,1)S(1)}, bf16[2,256,512]{2,1,0:T(8,128)(2,1)S(1)}, u32[]{:S(2)}, u32[]{:S(2)}) collective-permute-start(bf16[2,256,512]{2,1,0:T(8,128)(2,1)S(1)} %broadcast_select_fusion), channel_id=1, source_target_pairs={{0,4},{4,8},{8,12},{1,5},{5,9},{9,13},{2,6},{6,10},{10,14},{3,7},{... | collective-permute-start | bytes 1572872 | tf_op jit(solution)/shard_map/ppermute | solution.py:22
  23.1 22.5 %copy-start.1 = (bf16[2,256,512]{2,1,0:T(8,128)(2,1)}, bf16[2,256,512]{2,1,0:T(8,128)(2,1)S(1)}, u32[]{:S(2)}) copy-start(bf16[2,256,512]{2,1,0:T(8,128)(2,1)S(1)} %collective-permute-done.k_ref.v_ref) | copy-start | bytes 1572868
  23.1 34.5 %collective-permute-start.1 = (bf16[2,256,512]{2,1,0:T(8,128)(2,1)S(1)}, bf16[2,256,512]{2,1,0:T(8,128)(2,1)S(1)}, u32[]{:S(2)}, u32[]{:S(2)}) collective-permute-start(bf16[2,256,512]{2,1,0:T(8,128)(2,1)S(1)} %collective-permute-done.k_ref.v_ref), channel_id=1, source_target_pairs={{0,4},{4,8},{8,12},{1,5},{5,9},{9,13},{2,6},{6,10},{10,14},{3,7},{... | collective-permute-start | bytes 1572872 | tf_op jit(solution)/shard_map/ppermute | solution.py:22
  34.3 11.3 %copy-start.2 = (bf16[2,256,512]{2,1,0:T(8,128)(2,1)}, bf16[2,256,512]{2,1,0:T(8,128)(2,1)S(1)}, u32[]{:S(2)}) copy-start(bf16[2,256,512]{2,1,0:T(8,128)(2,1)S(1)} %collective-permute-done.3.k_ref.v_ref) | copy-start | bytes 1572868
  34.3 23.4 %collective-permute-start.4 = (bf16[2,256,512]{2,1,0:T(8,128)(2,1)S(1)}, bf16[2,256,512]{2,1,0:T(8,128)(2,1)S(1)}, u32[]{:S(2)}, u32[]{:S(2)}) collective-permute-start(bf16[2,256,512]{2,1,0:T(8,128)(2,1)S(1)} %collective-permute-done.3.k_ref.v_ref), channel_id=1, source_target_pairs={{0,4},{4,8},{8,12},{1,5},{5,9},{9,13},{2,6},{6,10},{10,14},{3,7},{... | collective-permute-start | bytes 1572872 | tf_op jit(solution)/shard_map/ppermute | solution.py:22
  57.7 1.0 %copy-start = (bf16[2,512,512]{2,1,0:T(8,128)(2,1)}, bf16[2,512,512]{2,1,0:T(8,128)(2,1)S(1)}, u32[]{:S(2)}) copy-start(bf16[2,512,512]{2,1,0:T(8,128)(2,1)S(1)} %constant_dynamic-update-slice_fusion.k_ref.v_ref) | copy-start | bytes 3145732

commit v12 on v11

--- a/solution.py
+++ b/solution.py
@@ -220,8 +220,10 @@
         corrupt_other = jnp.where(variant_index == 0, hi, lo)
         inside_own = jnp.where(variant_index == 0, inside_lo, inside_hi)
         inside_other = jnp.where(variant_index == 0, inside_hi, inside_lo)
-        clean_own = lax.optimization_barrier(clean_own)
-        clean_other = swap_variant(clean_own)
+        clean_k, clean_v = lax.optimization_barrier((clean_keys, clean_values))
+        other_k, other_v = swap_variant((clean_k, clean_v))
+        clean_other = jnp.stack([other_k, other_v])
+        clean_own = jnp.stack([clean_k, clean_v])
         corrupt_other, inside_other = lax.optimization_barrier((corrupt_other, inside_other))
         own_half = jnp.where(inside_own[None, :, None], clean_own, corrupt_own)
         near_own = shifted(own_half, "seq", 1)

time: 65.9 us -> 65.4 us (level)
  other arithmetic: 5.68 us -> 4.76 us
    another operation x1 -> x0, other arithmetic: 1.08 us -> none  [shard_body(): clean_own = jnp.stack([clean_keys, clean_values])]
    ppermute x1 -> x2, waiting for transfers between devices: 4.95 us -> 4.45 us  [swap_variant(): lax.ppermute(half, 'variant', [(i, (i + 1) % variants) for i in range(var...]
    ppermute x1 -> x2, starting transfers between devices: 1.56 us -> 2.03 us  [swap_variant(): lax.ppermute(half, 'variant', [(i, (i + 1) % variants) for i in range(var...]
  transfers between devices with their start and end apart: 5 -> 6, of which waited for: 3 -> 3; matrix products, arithmetic and copies ran while one was open for 7% -> 8% of each run, Pallas kernels for 28% -> 28%
where the time goes in v12:
time: 65.4 us; the launch traced here: 64.8 us
  Pallas kernels  24.9 us (38%)
  waiting for transfers between devices  17.3 us (26%)
  starting transfers between devices  15.9 us (24%)
  other arithmetic  4.76 us (7%)
  local copies, waits for them, and re-layouts  1.13 us (2%)
  between operations  0.77 us (1%)
    pallas_call x4, Pallas kernels, attend_chunk(): pl.pallas_call(kernel, grid_spec=grid_spec, out_shape=out_shape, cost_est...  24.9 us
    ppermute x4, starting transfers between devices, shifted(): return lax.ppermute(shard, axis, pairs)  13.9 us
    ppermute x4, waiting for transfers between devices, shifted(): return lax.ppermute(shard, axis, pairs)  12.9 us
    ppermute x2, waiting for transfers between devices, swap_variant(): lax.ppermute(half, 'variant', [(i, (i + 1) % variants) for i in range(var...  4.45 us
    ppermute x2, starting transfers between devices, swap_variant(): lax.ppermute(half, 'variant', [(i, (i + 1) % variants) for i in range(var...  2.03 us
    select_n x1, other arithmetic, shard_body(): corrupt_other = jnp.where(variant_index == 0, hi, lo)  1.81 us
    select_n x1, other arithmetic, halves_in_order(): jnp.where(variant_index == 0, jnp.concatenate([own, other], axis=1), jnp....  1.4 us
  transfers between devices with their start and end apart: 6, of which 3 were waited for; matrix products, arithmetic and copies ran while one was open for 8% of the time, Pallas kernels for 28%

profile of v12, /device:TPU:16, one launch (start us, length us, event | category | flops | bytes accessed | tf_op | source)
XLA Modules:
  0.0 64.8 jit_solution(6946191169953861917)
XLA Ops:
  0.0 1.5 %collective-permute-start.2 = (bf16[256,512]{1,0:T(8,128)(2,1)}, bf16[256,512]{1,0:T(8,128)(2,1)S(1)}, u32[]{:S(2)}, u32[]{:S(2)}) collective-permute-start(bf16[256,512]{1,0:T(8,128)(2,1)} %param.11), channel_id=1, source_target_pairs={{0,2},{2,0},{1,3},{3,1},{4,6},{6,4},{5,7},{7,5},{8,10},{10,8},{9,1... | collective-permute-start | bytes 786440 | tf_op jit(solution)/shard_map/ppermute | solution.py:186
  1.5 0.5 collective-permute-start.3
  2.7 0.7 %add_bitcast_fusion = s32[2]{0:T(128)S(1)} fusion(s32[1,2]{1,0:T(1,128)} %param.14, s32[1,2]{1,0:T(1,128)} %param.15), kind=kLoop, calls=%fused_computation.11 | loop fusion | flops 2 | bytes 24 | tf_op jit(solution)/shard_map/lt | solution.py:203
  3.4 0.7 %and_reduce_fusion = pred[512]{0:T(512)(128)(4,1)S(1)} fusion(pred[]{:T(512)} %bitcast.5, s32[2]{0:T(128)S(1)} %add_bitcast_fusion, s32[2]{0:T(128)} %bitcast.21), kind=kLoop, calls=%fused_computation.8 | loop fusion | flops 4608 | bytes 529 | tf_op jit(solution)/shard_map/reduce_or | solution.py:205
  4.1 1.8 %broadcast_select_fusion = (bf16[2,256,512]{2,1,0:T(8,128)(2,1)S(1)}, bf16[2,256,512]{2,1,0:T(8,128)(2,1)S(1)}) fusion(pred[]{:T(512)S(6)} %eq.6, bf16[1,512,512]{2,1,0:T(8,128)(2,1)} %bitcast.15, bf16[1,512,512]{2,1,0:T(8,128)(2,1)} %bitcast.16, bf16[1,256,512]{2,1,0:T(8,128)(2,1)} %bitcast.18, bf16[1,256,512]{2,1,0:T(8,128)(2,1)} %bitcast.17, ...), kind=kLoop, calls=%fused_computation.7 | loop fusion | flops 4980736 | bytes 2621697 | tf_op jit(solution)/shard_map/jit(_where)/select_n | solution.py:220
  5.9 3.5 %collective-permute-start = (bf16[2,256,512]{2,1,0:T(8,128)(2,1)S(1)}, bf16[2,256,512]{2,1,0:T(8,128)(2,1)S(1)}, u32[]{:S(2)}, u32[]{:S(2)}) collective-permute-start(bf16[2,256,512]{2,1,0:T(8,128)(2,1)S(1)} %get-tuple-element.32), channel_id=1, source_target_pairs={{0,4},{4,8},{8,12},{1,5},{5,9},{9,13},{2,6},{6,10},{10,14},{3,7},{... | collective-permute-start | bytes 1572872 | tf_op jit(solution)/shard_map/ppermute | solution.py:22
  9.4 0.0 collective-permute-done.2
  9.4 4.4 %collective-permute-done.3 = bf16[256,512]{1,0:T(8,128)(2,1)S(1)} collective-permute-done((bf16[256,512]{1,0:T(8,128)(2,1)}, bf16[256,512]{1,0:T(8,128)(2,1)S(1)}, u32[]{:S(2)}, u32[]{:S(2)}) %collective-permute-start.3) | collective-permute-done | bytes 262176 | tf_op jit(solution)/shard_map/ppermute | solution.py:186
  13.9 0.1 maximum_select_fusion.2
  14.0 3.5 %collective-permute-start.4 = (bf16[2,256,512]{2,1,0:T(8,128)(2,1)S(1)}, bf16[2,256,512]{2,1,0:T(8,128)(2,1)S(1)}, u32[]{:S(2)}, u32[]{:S(2)}) collective-permute-start(bf16[2,256,512]{2,1,0:T(8,128)(2,1)S(1)} %maximum_select_fusion.2), channel_id=1, source_target_pairs={{0,4},{4,8},{8,12},{1,5},{5,9},{9,13},{2,6},{6,10},{10,14},{3,7},{... | collective-permute-start | bytes 1572872 | tf_op jit(solution)/shard_map/ppermute | solution.py:22
  17.5 5.1 %collective-permute-done.k_ref.v_ref = bf16[2,256,512]{2,1,0:T(8,128)(2,1)S(1)} collective-permute-done((bf16[2,256,512]{2,1,0:T(8,128)(2,1)S(1)}, bf16[2,256,512]{2,1,0:T(8,128)(2,1)S(1)}, u32[]{:S(2)}, u32[]{:S(2)}) %collective-permute-start) | collective-permute-done | bytes 524320 | tf_op jit(solution)/shard_map/ppermute | solution.py:22
  22.6 0.0 copy-start.1
  22.6 3.5 %collective-permute-start.1 = (bf16[2,256,512]{2,1,0:T(8,128)(2,1)S(1)}, bf16[2,256,512]{2,1,0:T(8,128)(2,1)S(1)}, u32[]{:S(2)}, u32[]{:S(2)}) collective-permute-start(bf16[2,256,512]{2,1,0:T(8,128)(2,1)S(1)} %collective-permute-done.k_ref.v_ref), channel_id=1, source_target_pairs={{0,4},{4,8},{8,12},{1,5},{5,9},{9,13},{2,6},{6,10},{10,14},{3,7},{... | collective-permute-start | bytes 1572872 | tf_op jit(solution)/shard_map/ppermute | solution.py:22
  26.1 7.8 %collective-permute-done.4.k_ref.v_ref = bf16[2,256,512]{2,1,0:T(8,128)(2,1)S(1)} collective-permute-done((bf16[2,256,512]{2,1,0:T(8,128)(2,1)S(1)}, bf16[2,256,512]{2,1,0:T(8,128)(2,1)S(1)}, u32[]{:S(2)}, u32[]{:S(2)}) %collective-permute-start.4) | collective-permute-done | bytes 524320 | tf_op jit(solution)/shard_map/ppermute | solution.py:22
  33.9 0.0 copy-start.2
  33.9 3.5 %collective-permute-start.5 = (bf16[2,256,512]{2,1,0:T(8,128)(2,1)S(1)}, bf16[2,256,512]{2,1,0:T(8,128)(2,1)S(1)}, u32[]{:S(2)}, u32[]{:S(2)}) collective-permute-start(bf16[2,256,512]{2,1,0:T(8,128)(2,1)S(1)} %collective-permute-done.4.k_ref.v_ref), channel_id=1, source_target_pairs={{0,4},{4,8},{8,12},{1,5},{5,9},{9,13},{2,6},{6,10},{10,14},{3,7},{... | collective-permute-start | bytes 1572872 | tf_op jit(solution)/shard_map/ppermute | solution.py:22
  37.3 1.4 %maximum_select_fusion.k_ref.v_ref = bf16[2,512,512]{2,1,0:T(8,128)(2,1)} fusion(bf16[2,256,512]{2,1,0:T(8,128)(2,1)S(1)} %maximum_select_fusion.2, bf16[2,256,512]{2,1,0:T(8,128)(2,1)S(1)} %get-tuple-element.32, pred[]{:T(512)S(6)} %eq.6), kind=kLoop, calls=%fused_computation.2 | loop fusion | flops 4718592 | bytes 2097153 | tf_op jit(solution)/shard_map/jit(_where)/select_n | solution.py:190
  38.8 6.4 %shard_map.82 = (f32[512,8]{1,0:T(8,128)}, f32[512,8]{1,0:T(8,128)}, f32[512,1024]{1,0:T(8,128)}) custom-call(s32[1]{0:T(128)} %bitcast.first_ref, bf16[512,1024]{1,0:T(8,128)(2,1)} %q_ref.7, bf16[2,512,512]{2,1,0:T(8,128)(2,1)} %maximum_select_fusion.k_ref.v_ref, bf16[2,512,512]{2,1,0:T(8,128)(2,1)} %maximum_select_fusion.k_ref.v_ref), custom_call_target="tpu_custom_call" | custom-call | flops 1073741824 | bytes 4194304 | tf_op jit(solution)/shard_map/pallas_call | solution.py:175
  45.1 0.0 copy-done.1
  45.1 0.0 copy-done.2
  45.1 6.0 %shard_map.83 = (f32[512,8]{1,0:T(8,128)}, f32[512,8]{1,0:T(8,128)}, f32[512,1024]{1,0:T(8,128)}) custom-call(s32[1]{0:T(128)} %bitcast.first_ref, bf16[512,1024]{1,0:T(8,128)(2,1)} %q_ref.7, bf16[2,256,512]{2,1,0:T(8,128)(2,1)} %copy-done.1, bf16[2,256,512]{2,1,0:T(8,128)(2,1)} %copy-done.1, f32[512,8]{1,0:T(8,128)} %get-tuple-element.22.rest_0_, ...), custom_call_target="tpu_custom_call" | custom-call | flops 536870912 | bytes 5767168 | tf_op jit(solution)/shard_map/pallas_call | solution.py:175
  51.1 6.0 %shard_map.84 = (f32[512,8]{1,0:T(8,128)}, f32[512,8]{1,0:T(8,128)}, f32[512,1024]{1,0:T(8,128)}) custom-call(s32[1]{0:T(128)} %bitcast.first_ref, bf16[512,1024]{1,0:T(8,128)(2,1)} %q_ref.7, bf16[2,256,512]{2,1,0:T(8,128)(2,1)} %copy-done.2, bf16[2,256,512]{2,1,0:T(8,128)(2,1)} %copy-done.2, f32[512,8]{1,0:T(8,128)} %get-tuple-element.25.rest_0_, ...), custom_call_target="tpu_custom_call" | custom-call | flops 536870912 | bytes 5767168 | tf_op jit(solution)/shard_map/pallas_call | solution.py:175
  57.1 0.0 collective-permute-done.1
  57.1 0.1 broadcast_in_dim.24
  57.2 0.0 collective-permute-done.5
  57.3 0.0 copy-start
  57.3 1.0 %copy-done = bf16[2,512,512]{2,1,0:T(8,128)(2,1)} copy-done((bf16[2,512,512]{2,1,0:T(8,128)(2,1)}, bf16[2,512,512]{2,1,0:T(8,128)(2,1)S(1)}, u32[]{:S(2)}) %copy-start) | copy-done | bytes 1048600
  58.3 6.6 %shard_map.85 = bf16[512,1024]{1,0:T(8,128)(2,1)} custom-call(s32[1]{0:T(128)} %bitcast.first_ref, bf16[512,1024]{1,0:T(8,128)(2,1)} %q_ref.7, bf16[2,512,512]{2,1,0:T(8,128)(2,1)} %copy-done, bf16[2,512,512]{2,1,0:T(8,128)(2,1)} %copy-done, f32[512,8]{1,0:T(8,128)} %get-tuple-element.28.rest_0_, f32[512,8]{1,0:T(8,128)} %get-tuple-element.29.rest_1_, ...), custom_call_target="tpu_custom_call" | custom-call | flops 1073741824 | bytes 6291456 | tf_op jit(solution)/shard_map/pallas_call | solution.py:175
  (3 shorter events, 0.1 us)
Async XLA Ops:
  0.0 9.4 %collective-permute-start.2 = (bf16[256,512]{1,0:T(8,128)(2,1)}, bf16[256,512]{1,0:T(8,128)(2,1)S(1)}, u32[]{:S(2)}, u32[]{:S(2)}) collective-permute-start(bf16[256,512]{1,0:T(8,128)(2,1)} %param.11), channel_id=1, source_target_pairs={{0,2},{2,0},{1,3},{3,1},{4,6},{6,4},{5,7},{7,5},{8,10},{10,8},{9,1... | collective-permute-start | bytes 786440 | tf_op jit(solution)/shard_map/ppermute | solution.py:186
  1.5 12.4 %collective-permute-start.3 = (bf16[256,512]{1,0:T(8,128)(2,1)}, bf16[256,512]{1,0:T(8,128)(2,1)S(1)}, u32[]{:S(2)}, u32[]{:S(2)}) collective-permute-start(bf16[256,512]{1,0:T(8,128)(2,1)} %param.12), channel_id=1, source_target_pairs={{0,2},{2,0},{1,3},{3,1},{4,6},{6,4},{5,7},{7,5},{8,10},{10,8},{9,1... | collective-permute-start | bytes 786440 | tf_op jit(solution)/shard_map/ppermute | solution.py:186
  5.9 16.7 %collective-permute-start = (bf16[2,256,512]{2,1,0:T(8,128)(2,1)S(1)}, bf16[2,256,512]{2,1,0:T(8,128)(2,1)S(1)}, u32[]{:S(2)}, u32[]{:S(2)}) collective-permute-start(bf16[2,256,512]{2,1,0:T(8,128)(2,1)S(1)} %get-tuple-element.32), channel_id=1, source_target_pairs={{0,4},{4,8},{8,12},{1,5},{5,9},{9,13},{2,6},{6,10},{10,14},{3,7},{... | collective-permute-start | bytes 1572872 | tf_op jit(solution)/shard_map/ppermute | solution.py:22
  14.0 19.9 %collective-permute-start.4 = (bf16[2,256,512]{2,1,0:T(8,128)(2,1)S(1)}, bf16[2,256,512]{2,1,0:T(8,128)(2,1)S(1)}, u32[]{:S(2)}, u32[]{:S(2)}) collective-permute-start(bf16[2,256,512]{2,1,0:T(8,128)(2,1)S(1)} %maximum_select_fusion.2), channel_id=1, source_target_pairs={{0,4},{4,8},{8,12},{1,5},{5,9},{9,13},{2,6},{6,10},{10,14},{3,7},{... | collective-permute-start | bytes 1572872 | tf_op jit(solution)/shard_map/ppermute | solution.py:22
  22.6 22.5 %copy-start.1 = (bf16[2,256,512]{2,1,0:T(8,128)(2,1)}, bf16[2,256,512]{2,1,0:T(8,128)(2,1)S(1)}, u32[]{:S(2)}) copy-start(bf16[2,256,512]{2,1,0:T(8,128)(2,1)S(1)} %collective-permute-done.k_ref.v_ref) | copy-start | bytes 1572868
  22.6 34.5 %collective-permute-start.1 = (bf16[2,256,512]{2,1,0:T(8,128)(2,1)S(1)}, bf16[2,256,512]{2,1,0:T(8,128)(2,1)S(1)}, u32[]{:S(2)}, u32[]{:S(2)}) collective-permute-start(bf16[2,256,512]{2,1,0:T(8,128)(2,1)S(1)} %collective-permute-done.k_ref.v_ref), channel_id=1, source_target_pairs={{0,4},{4,8},{8,12},{1,5},{5,9},{9,13},{2,6},{6,10},{10,14},{3,7},{... | collective-permute-start | bytes 1572872 | tf_op jit(solution)/shard_map/ppermute | solution.py:22
  33.9 11.3 %copy-start.2 = (bf16[2,256,512]{2,1,0:T(8,128)(2,1)}, bf16[2,256,512]{2,1,0:T(8,128)(2,1)S(1)}, u32[]{:S(2)}) copy-start(bf16[2,256,512]{2,1,0:T(8,128)(2,1)S(1)} %collective-permute-done.4.k_ref.v_ref) | copy-start | bytes 1572868
  33.9 23.4 %collective-permute-start.5 = (bf16[2,256,512]{2,1,0:T(8,128)(2,1)S(1)}, bf16[2,256,512]{2,1,0:T(8,128)(2,1)S(1)}, u32[]{:S(2)}, u32[]{:S(2)}) collective-permute-start(bf16[2,256,512]{2,1,0:T(8,128)(2,1)S(1)} %collective-permute-done.4.k_ref.v_ref), channel_id=1, source_target_pairs={{0,4},{4,8},{8,12},{1,5},{5,9},{9,13},{2,6},{6,10},{10,14},{3,7},{... | collective-permute-start | bytes 1572872 | tf_op jit(solution)/shard_map/ppermute | solution.py:22
  57.3 1.0 %copy-start = (bf16[2,512,512]{2,1,0:T(8,128)(2,1)}, bf16[2,512,512]{2,1,0:T(8,128)(2,1)S(1)}, u32[]{:S(2)}) copy-start(bf16[2,512,512]{2,1,0:T(8,128)(2,1)S(1)} %constant_dynamic-update-slice_fusion.k_ref.v_ref) | copy-start | bytes 3145732
